TPU v7x, 256 devices: a whole 4x4x8 slice. The times are simulated.
256 devices in a mesh: kv: 8 (over y, z_lo), blk: 32 (over x, z_hi, core).
Axes of the slice: x: 4, y: 4, z: 8 (z_hi: 4, z_lo: 2; z = z_hi * 2 + z_lo), core: 2. Of those that a mesh axis runs over, the one named last changes fastest.
Arguments:
- suffix_query: bfloat16 [6144, 4096], P('blk', 'kv'), may hold values from -6 to 6
- suffix_key_value: bfloat16 [2, 6144, 2048], P(None, 'blk', 'kv'), may hold values from -6 to 6
- suffix_resid: bfloat16 [6144, 4608], P('blk', 'kv'), may hold values from -6 to 6
- decode_query_rows: bfloat16 [64, 4096], P('blk', 'kv'), may hold values from -6 to 6
- decode_key_value: bfloat16 [2, 64, 2048], P(None, 'blk', 'kv'), may hold values from -6 to 6
- decode_resid: bfloat16 [64, 4608], P('blk', 'kv'), may hold values from -6 to 6
- out_weight: bfloat16 [4096, 4608], P('kv'), may hold values from -1.125 to 1.125
- post_gain: float32 [4608], P('kv'), may hold values from 0.1 to 1.9
- prefix_page_store: bfloat16 [2, 96, 128, 2048], P(None, 'blk', None, 'kv'), may hold values from -6 to 6
- prefix_table: int32 [96], replicated, may hold values from 0 to 95, each once
- decode_page_store: bfloat16 [2, 512, 128, 2048], P(None, 'blk', None, 'kv'), may hold values from -6 to 6
- page_table: int32 [512], replicated, may hold values from 0 to 511, each once
- suffix_lengths: int32 [16], replicated, may hold values from 1 to 768, 6144 in all
- suffix_prefix: int32 [16], replicated, may hold values from 0 to 3
- decode_ages: int32 [64], replicated, may hold values from 1 to 1023, as said below
Outputs:
- suffix_hidden: bfloat16 [6144, 4608], P('blk', 'kv')
- decode_hidden: bfloat16 [64, 4608], P('blk', 'kv')
- new_cache: bfloat16 [2, 512, 128, 2048], P(None, 'blk', None, 'kv')
Inputs may be any that keep to these rules, and one draw needn't show every extreme that they name: `page_table`: every page of the decode pool is named once. `prefix_table`: every page of the prefix pool is named once. `suffix_lengths`: the lengths sum to 6144; one is exactly 768. `decode_ages`: some slot has age 1024 - 1.
All inputs are finite; a program needn't handle non-finite values.
Results may differ from a plain program's by a relative error of at most 0.024.
Values may be sent and summed in bfloat16 or wider, within the bound.
No kernel may reach another device: no remote copies, remote signals or barrier semaphores. Data moves between devices by JAX's collectives and lax.ppermute only.
A program may use at most 128 MiB of HBM per device.

v0:
```python
import math

import jax
import jax.numpy as jnp
from jax import lax
from jax.sharding import PartitionSpec as P

D = 4608
QUERY_HEADS = 32
HEAD_SIZE = 128
PAGE_TOKENS = 128
PREFIX_LENGTH = 3072
SLOT_CAPACITY = 1024


soft_cap = 50.0
norm_eps = 1e-06


def from_behind(block, axis, distance):
    devices = range(lax.axis_size(axis))
    route = [(i - distance, i) for i in devices if i - distance in devices]
    return lax.ppermute(block, axis, route)


def attend(query_rows, key_rows, value_rows, visible, q_scale):
    logits = (
        jnp.einsum("qhgd,khd->qhgk", query_rows, key_rows, preferred_element_type=jnp.float32)
        * q_scale
    )
    capped = soft_cap * jnp.tanh(logits / soft_cap)
    weights = jnp.where(visible[:, None, None, :], jnp.exp(capped), 0.0)
    denominator = jnp.sum(weights, axis=3)
    numerator = jnp.einsum(
        "qhgk,khd->qhgd",
        weights.astype(jnp.bfloat16),
        value_rows,
        preferred_element_type=jnp.float32,
    )
    return (numerator, denominator)


def earlier(block_rows):
    return from_behind(block_rows, "blk", 1)


def token_tables(lengths, prefix_ids, token_ids):
    suffix_ends = jnp.cumsum(lengths)
    starts = suffix_ends - lengths
    inside = (
        (token_ids[:, None] >= starts[None, :]) & (token_ids[:, None] < suffix_ends[None, :])
    ).astype(jnp.int32)
    tok_start = jnp.sum(inside * starts[None, :], axis=1)
    tok_prefix = jnp.sum(inside * prefix_ids[None, :], axis=1)
    return (tok_start, tok_prefix)


def inverse_rows(table, wanted):
    hits = (table[None, :] == wanted[:, None]).astype(jnp.int32)
    places = jnp.arange(table.shape[0], dtype=jnp.int32)
    return jnp.sum(hits * places[None, :], axis=1)


def body(
    suffix_query,
    suffix_key_value,
    suffix_resid,
    decode_query_rows,
    decode_key_value,
    decode_resid,
    out_weight,
    post_gain,
    prefix_page_store,
    prefix_table,
    decode_page_store,
    page_table,
    suffix_lengths,
    suffix_prefix,
    decode_ages,
):
    head_dim = HEAD_SIZE
    page_len = PAGE_TOKENS
    q_scale = (D // QUERY_HEADS) ** (-0.5)
    tok_rows = suffix_query.shape[0]
    q_heads = suffix_query.shape[1] // head_dim
    kv_heads = suffix_key_value.shape[2] // head_dim
    query_group_width = q_heads // kv_heads
    my_index = lax.axis_index("blk")
    own_queries = suffix_query.reshape(tok_rows, kv_heads, query_group_width, head_dim)
    token_ids = my_index * tok_rows + jnp.arange(tok_rows, dtype=jnp.int32)
    tok_start, tok_prefix = token_tables(suffix_lengths, suffix_prefix, token_ids)
    look_back = 4
    pieces_back = [suffix_key_value]
    for step in range(look_back):
        pieces_back.insert(0, earlier(pieces_back[0]))
    window = jnp.concatenate(pieces_back, axis=1)
    key_ids = (my_index - look_back) * tok_rows + jnp.arange(
        (look_back + 1) * tok_rows, dtype=jnp.int32
    )
    visible = (key_ids[None, :] >= tok_start[:, None]) & (key_ids[None, :] <= token_ids[:, None])
    window_keys = window[0].reshape((look_back + 1) * tok_rows, kv_heads, head_dim)
    window_values = window[1].reshape((look_back + 1) * tok_rows, kv_heads, head_dim)
    own_numer, own_denom = attend(own_queries, window_keys, window_values, visible, q_scale)
    pool_pages = prefix_table.shape[0]
    page_owner = inverse_rows(prefix_table, jnp.arange(pool_pages, dtype=jnp.int32)) // (
        PREFIX_LENGTH // PAGE_TOKENS
    )
    all_queries = lax.all_gather(suffix_query, "blk", axis=0, tiled=True)
    all_tokens = all_queries.shape[0]
    all_ids = jnp.arange(all_tokens, dtype=jnp.int32)
    unused_start, all_prefix = token_tables(suffix_lengths, suffix_prefix, all_ids)
    local_pages = prefix_page_store.shape[1]
    held_owner = lax.dynamic_slice_in_dim(page_owner, my_index * local_pages, local_pages, 0)
    held_cols = jnp.repeat(held_owner, page_len)
    held_keys = prefix_page_store[0].reshape(local_pages * page_len, kv_heads, head_dim)
    held_values = prefix_page_store[1].reshape(local_pages * page_len, kv_heads, head_dim)
    block_rows = math.gcd(all_tokens, 1024)
    query_blocks = all_queries.reshape(
        all_tokens // block_rows, block_rows, kv_heads, query_group_width, head_dim
    )
    prefix_blocks = all_prefix.reshape(all_tokens // block_rows, block_rows)

    def one_block(element):
        block_queries, block_prefix = element
        seen = block_prefix[:, None] == held_cols[None, :]
        return attend(block_queries, held_keys, held_values, seen, q_scale)

    numer_all, denom_all = lax.map(one_block, (query_blocks, prefix_blocks))
    numer_all = numer_all.reshape(all_tokens, kv_heads, query_group_width, head_dim)
    denom_all = denom_all.reshape(all_tokens, kv_heads, query_group_width)
    pre_numer, pre_denom = (
        lax.psum_scatter(
            numer_all.astype(jnp.bfloat16), "blk", scatter_dimension=0, tiled=True
        ).astype(jnp.float32),
        lax.psum_scatter(
            denom_all.astype(jnp.bfloat16), "blk", scatter_dimension=0, tiled=True
        ).astype(jnp.float32),
    )
    suffix_attn = ((own_numer + pre_numer) / (own_denom + pre_denom)[..., None]).astype(
        jnp.bfloat16
    )
    suffix_attn = suffix_attn.reshape(tok_rows, q_heads * head_dim)
    all_dq, all_dkv = (
        lax.all_gather(decode_query_rows, "blk", axis=0, tiled=True),
        lax.all_gather(decode_key_value, "blk", axis=1, tiled=True),
    )
    slot_total = all_dq.shape[0]
    slot_pages = SLOT_CAPACITY // PAGE_TOKENS
    local_cache = decode_page_store.shape[1]
    page_ids = my_index * local_cache + jnp.arange(local_cache, dtype=jnp.int32)
    position = inverse_rows(page_table, page_ids)
    slot_of = position // slot_pages
    block_of = position % slot_pages
    slot_hot = slot_of[:, None] == jnp.arange(slot_total, dtype=jnp.int32)[None, :]
    page_age = jnp.sum(slot_hot.astype(jnp.int32) * decode_ages[None, :], axis=1)
    select = slot_hot.astype(jnp.bfloat16)
    new_rows = jnp.einsum(
        "ls,tsc->tlc", select, all_dkv, preferred_element_type=jnp.float32
    ).astype(jnp.bfloat16)
    write_here = (block_of == page_age // page_len)[:, None] & (
        jnp.arange(page_len, dtype=jnp.int32)[None, :] == (page_age % page_len)[:, None]
    )
    new_cache = jnp.where(write_here[None, :, :, None], new_rows[:, :, None, :], decode_page_store)
    page_queries = jnp.dot(select, all_dq, preferred_element_type=jnp.float32).astype(jnp.bfloat16)
    page_queries = page_queries.reshape(local_cache, kv_heads, query_group_width, head_dim)
    key_cache = new_cache[0].reshape(local_cache, page_len, kv_heads, head_dim)
    value_cache = new_cache[1].reshape(local_cache, page_len, kv_heads, head_dim)
    logits = (
        jnp.einsum("lhgd,lphd->lhgp", page_queries, key_cache, preferred_element_type=jnp.float32)
        * q_scale
    )
    capped = soft_cap * jnp.tanh(logits / soft_cap)
    places = block_of[:, None] * page_len + jnp.arange(page_len, dtype=jnp.int32)[None, :]
    seen_pos = places <= page_age[:, None]
    weights = jnp.where(seen_pos[:, None, None, :], jnp.exp(capped), 0.0)
    page_denom = jnp.sum(weights, axis=3)
    page_numer = jnp.einsum(
        "lhgp,lphd->lhgd",
        weights.astype(jnp.bfloat16),
        value_cache,
        preferred_element_type=jnp.float32,
    )
    slot_float = slot_hot.astype(jnp.float32)
    slot_numer = jnp.einsum(
        "ls,lhgd->shgd", slot_float, page_numer, precision=lax.Precision.HIGHEST
    )
    slot_denom = jnp.einsum("ls,lhg->shg", slot_float, page_denom, precision=lax.Precision.HIGHEST)
    mine_numer, mine_denom = (
        lax.psum_scatter(
            slot_numer.astype(jnp.bfloat16), "blk", scatter_dimension=0, tiled=True
        ).astype(jnp.float32),
        lax.psum_scatter(
            slot_denom.astype(jnp.bfloat16), "blk", scatter_dimension=0, tiled=True
        ).astype(jnp.float32),
    )
    decode_attn = (mine_numer / mine_denom[..., None]).astype(jnp.bfloat16)
    decode_rows = decode_attn.shape[0]
    decode_attn = decode_attn.reshape(decode_rows, q_heads * head_dim)
    attention = jnp.concatenate([suffix_attn, decode_attn], axis=0)
    projected = jnp.dot(attention, out_weight, preferred_element_type=jnp.float32)
    residual = jnp.concatenate([suffix_resid, decode_resid], axis=0).astype(jnp.float32)
    mine = lax.psum_scatter(
        projected.astype(jnp.bfloat16), "kv", scatter_dimension=1, tiled=True
    ).astype(jnp.float32)
    mean_square = lax.psum(jnp.sum(mine * mine, axis=1), "kv") / D
    normed = mine * lax.rsqrt(mean_square + norm_eps)[:, None] * post_gain[None, :]
    hidden = (residual + normed).astype(jnp.bfloat16)
    return (hidden[:tok_rows], hidden[tok_rows:], new_cache)


def solution(mesh):
    placed = (
        P("blk", "kv"),
        P(None, "blk", "kv"),
        P("blk", "kv"),
        P("blk", "kv"),
        P(None, "blk", "kv"),
        P("blk", "kv"),
        P("kv", None),
        P("kv"),
        P(None, "blk", None, "kv"),
        P(),
        P(None, "blk", None, "kv"),
        P(),
        P(),
        P(),
        P(),
    )
    return jax.shard_map(
        body,
        mesh=mesh,
        in_specs=placed,
        out_specs=(P("blk", "kv"), P("blk", "kv"), P(None, "blk", None, "kv")),
        check_vma=False,
    )
```

profile of v0, /device:TPU:2, one launch (start us, length us, event | category | flops | bytes accessed | tf_op | source)
XLA Modules:
  0.0 656.7 jit_solution(15037850193555876869)
XLA Ops:
  8.7 3.9 copy.90
  12.6 42.1 %all-gather = bf16[32,2,512]{2,1,0:T(2,128)(2,1)S(1)} all-gather(bf16[1,2,512]{2,1,0:T(2,128)(2,1)S(1)} %bitcast.118), channel_id=1, replica_groups=mesh['kv'=8,'blk'=32] {'blk'}, dimensions={0}, use_global_device_ids=true | all-gather | bytes 67584 | tf_op jit(solution)/shard_map/all_gather | solution.py:144
  55.2 42.4 %all_gather.11 = bf16[2,64,256]{2,0,1:T(2,128)(2,1)S(1)} all-gather(bf16[2,2,256]{2,0,1:T(2,128)(2,1)S(1)} %copy.88), channel_id=1, replica_groups=mesh['kv'=8,'blk'=32] {'blk'}, dimensions={1}, use_global_device_ids=true | all-gather | bytes 67584 | tf_op jit(solution)/shard_map/all_gather | solution.py:145
  103.9 9.7 %reshape.292 = bf16[6,1024,2,2,128]{4,3,2,1,0:T(2,128)(2,1)} reshape(bf16[6144,512]{1,0:T(8,128)(2,1)} %all-gather.3.cloned.1.call-done) | data formatting | bytes 12582912 | tf_op jit(solution)/shard_map/reshape | solution.py:118
  113.6 49.5 %while.15 = (s32[]{:T(128)}, bf16[6,1024,2,2,128]{4,1,3,2,0:T(8,128)(2,1)}, bf16[6,1024,2,2]{1,3,2,0:T(2,128)(2,1)S(1)}, s32[6,1024]{1,0:T(8,128)S(1)}, bf16[6,1...) while((s32[]{:T(128)}, ...), condition=%wide.region_6.7_spmd.clone, body=%wide.region_4.6_spmd.clone.sunk | while | flops 818278400 | bytes 19439220 | solution.py:128
  118.6 3.2 bitcast_dynamic-update-slice_fusion.4
  135.1 3.2 bitcast_dynamic-update-slice_fusion.4
  143.3 3.2 bitcast_dynamic-update-slice_fusion.4
  151.6 3.2 bitcast_dynamic-update-slice_fusion.4
  159.8 3.2 bitcast_dynamic-update-slice_fusion.4
  163.1 5.8 copy.117
  168.9 6.3 reshape.304
  175.2 6.1 copy.85
  186.0 125.5 %all-reduce.1 = bf16[64,2,2]{2,0,1:T(8,128)(2,1)S(1)} all-reduce(bf16[64,2,2]{2,0,1:T(8,128)(2,1)S(1)} %convolution_convert_fusion.2), channel_id=5, replica_groups=mesh['kv'=8,'blk'=32] {'blk'}, use_global_device_ids=true, to_apply=%region_14.15.clone | all-reduce | flops 256 | bytes 1024
  313.7 8.1 %collective-permute-done.1 = bf16[2,192,256]{2,1,0:T(8,128)(2,1)S(1)} collective-permute-done((bf16[2,192,256]{2,1,0:T(8,128)(2,1)S(1)}, bf16[2,192,256]{2,1,0:T(8,128)(2,1)S(1)}, u32[]{:S(2)}, u32[]{:S(2)}) %collective-permute-start.1) | collective-permute-done | bytes 196640 | tf_op jit(solution)/shard_map/ppermute | solution.py:23
  323.9 7.8 %collective-permute-done.2 = bf16[2,192,256]{2,1,0:T(8,128)(2,1)S(1)} collective-permute-done((bf16[2,192,256]{2,1,0:T(8,128)(2,1)S(1)}, bf16[2,192,256]{2,1,0:T(8,128)(2,1)S(1)}, u32[]{:S(2)}, u32[]{:S(2)}) %collective-permute-start.2) | collective-permute-done | bytes 196640 | tf_op jit(solution)/shard_map/ppermute | solution.py:23
  333.9 9.5 %all-reduce.4.cloned.1.call-done = bf16[64,2,2,128]{3,0,2,1:T(8,128)(2,1)} async-done(((bf16[64,2,2,128]{3,0,2,1:T(8,128)(2,1)}), bf16[64,2,2,128]{3,0,2,1:T(8,128)(2,1)}) %all-reduce.4.cloned.1.call-update) | async-done | bytes 65552
  345.4 3.9 fusion.10
  349.2 99.7 %reduce-scatter.12.cloned.1.call-done = bf16[192,4]{1,0:T(8,128)(2,1)} async-done(((bf16[6144,4]{1,0:T(8,128)(2,1)}), bf16[192,4]{1,0:T(8,128)(2,1)}) %reduce-scatter.12.cloned.1.call-update) | async-done | bytes 1552
  449.9 109.7 %reduce-scatter.10.cloned.1.call-done = bf16[192,2,2,128]{3,0,2,1:T(8,128)(2,1)} async-done(((bf16[6144,2,2,128]{3,0,2,1:T(8,128)(2,1)}), bf16[192,2,2,128]{3,0,2,1:T(8,128)(2,1)}) %reduce-scatter.10.cloned.1.call-update) | async-done | bytes 196624 | tf_op jit(solution)/shard_map/reduce_scatter | solution.py:132
  562.8 4.7 convolution_convert_fusion
  567.5 4.0 copy.115
  574.2 56.4 %reduce-scatter.14.cloned.1.call-done = bf16[576,194]{1,0:T(8,128)(2,1)} async-done(((bf16[4608,194]{1,0:T(8,128)(2,1)}), bf16[576,194]{1,0:T(8,128)(2,1)}) %reduce-scatter.14.cloned.1.call-update) | async-done | bytes 223504
  631.8 16.9 %psum.7 = f32[194]{0:T(256)S(1)} all-reduce(f32[194]{0:T(256)S(1)} %fusion.32), channel_id=1, replica_groups=mesh['kv'=8,'blk'=32] {'kv'}, use_global_device_ids=true, to_apply=%region_17.18 | all-reduce | flops 194 | bytes 1552 | tf_op jit(solution)/shard_map/psum | solution.py:205
  (146 shorter events, 63.3 us)
Async XLA Ops:
  7.2 5.4 copy-start.6
  7.2 47.6 %copy-start.7 = (s32[512]{0:T(512)S(1)}, s32[512]{0:T(512)}, u32[]{:S(2)}) copy-start(s32[512]{0:T(512)} %param.28) | copy-start | bytes 6148
  7.2 90.3 %copy-start.10 = (s32[64]{0:T(128)S(1)}, s32[64]{0:T(128)}, u32[]{:S(2)}) copy-start(s32[64]{0:T(128)} %param.31) | copy-start | bytes 772
  7.2 96.7 %all-gather.3.cloned.1.call-start = ((), (), s32[]{:S(2)}) async-start(), calls=%async_computation.3 | async-start | bytes 6488064 | tf_op jit(solution)/shard_map/all_gather | solution.py:108
  7.9 335.4 %all-reduce.4.cloned.1.call-start = ((), (), s32[]{:S(2)}) async-start(), calls=%async_computation.7 | async-start | bytes 131072
  100.6 2.4 copy-start.11
  100.6 2.5 copy-start.8
  100.6 2.8 copy-start.9
  100.6 3.0 copy-start.1
  102.9 346.0 %reduce-scatter.12.cloned.1.call-start = ((), (), s32[]{:S(2)}) async-start(), calls=%async_computation.5 | async-start | bytes 1622016
  175.1 384.5 %reduce-scatter.10.cloned.1.call-start = ((), (), s32[]{:S(2)}) async-start(), calls=%async_computation.4 | async-start | bytes 6488064 | tf_op jit(solution)/shard_map/reduce_scatter | solution.py:132
  181.2 0.9 copy-start.3
  181.2 3.2 copy-start
  181.2 3.3 copy-start.12
  181.3 449.3 %reduce-scatter.14.cloned.1.call-start = ((), (), s32[]{:S(2)}) async-start(), calls=%async_computation.6 | async-start | bytes 2654208
  182.2 129.5 %collective-permute-start = (bf16[2,192,256]{2,1,0:T(8,128)(2,1)S(1)}, bf16[2,192,256]{2,1,0:T(8,128)(2,1)S(1)}, u32[]{:S(2)}, u32[]{:S(2)}) collective-permute-start(bf16[2,192,256]{2,1,0:T(8,128)(2,1)S(1)} %copy-done.3), channel_id=1, source_target_pairs={{0,1},{1,2},{2,3},{3,4},{4,5},{5,6},{6,7},{7,8},{8,9},{9,10},{10,1... | collective-permute-start | bytes 589832 | tf_op jit(solution)/shard_map/ppermute | solution.py:23
  311.7 10.1 %collective-permute-start.1 = (bf16[2,192,256]{2,1,0:T(8,128)(2,1)S(1)}, bf16[2,192,256]{2,1,0:T(8,128)(2,1)S(1)}, u32[]{:S(2)}, u32[]{:S(2)}) collective-permute-start(bf16[2,192,256]{2,1,0:T(8,128)(2,1)S(1)} %collective-permute-done), channel_id=1, source_target_pairs={{0,1},{1,2},{2,3},{3,4},{4,5},{5,6},{6,7},{7,8},{8,9},{9,10},{10,1... | collective-permute-start | bytes 589832 | tf_op jit(solution)/shard_map/ppermute | solution.py:23
  321.8 10.0 %collective-permute-start.2 = (bf16[2,192,256]{2,1,0:T(8,128)(2,1)S(1)}, bf16[2,192,256]{2,1,0:T(8,128)(2,1)S(1)}, u32[]{:S(2)}, u32[]{:S(2)}) collective-permute-start(bf16[2,192,256]{2,1,0:T(8,128)(2,1)S(1)} %collective-permute-done.1), channel_id=1, source_target_pairs={{0,1},{1,2},{2,3},{3,4},{4,5},{5,6},{6,7},{7,8},{8,9},{9,10},{10,1... | collective-permute-start | bytes 589832 | tf_op jit(solution)/shard_map/ppermute | solution.py:23
  331.8 12.4 %collective-permute-start.3 = (bf16[2,192,256]{2,1,0:T(8,128)(2,1)S(1)}, bf16[2,192,256]{2,1,0:T(8,128)(2,1)S(1)}, u32[]{:S(2)}, u32[]{:S(2)}) collective-permute-start(bf16[2,192,256]{2,1,0:T(8,128)(2,1)S(1)} %collective-permute-done.2), channel_id=1, source_target_pairs={{0,1},{1,2},{2,3},{3,4},{4,5},{5,6},{6,7},{7,8},{8,9},{9,10},{10,1... | collective-permute-start | bytes 589832 | tf_op jit(solution)/shard_map/ppermute | solution.py:23
  571.5 77.2 %copy-start.2 = (bf16[192,576]{1,0:T(8,128)(2,1)S(1)}, bf16[192,576]{1,0:T(8,128)(2,1)}, u32[]{:S(2)}) copy-start(bf16[192,576]{1,0:T(8,128)(2,1)} %param.19) | copy-start | bytes 663556
  571.5 77.2 %copy-start.4 = (f32[576]{0:T(1024)S(1)}, f32[576]{0:T(1024)}, u32[]{:S(2)}) copy-start(f32[576]{0:T(1024)} %param.24) | copy-start | bytes 6916
  571.6 77.2 %copy-start.5 = (bf16[2,576]{1,0:T(2,128)(2,1)S(1)}, bf16[2,576]{1,0:T(2,128)(2,1)}, u32[]{:S(2)}) copy-start(bf16[2,576]{1,0:T(2,128)(2,1)} %param.22) | copy-start | bytes 6916
Sparse Core Ops, SparseCore 0:
  10.5 72.2 all-gather.2
  103.0 240.3 all-reduce.3
  347.8 101.0 reduce-scatter.11
  452.8 106.7 reduce-scatter.9
  571.7 58.8 reduce-scatter.13
where the time goes:
time: 658 us; the launch traced here: 657 us
  waiting for transfers between devices  292 us (44%)
  blocking collectives  227 us (34%)
  local copies, waits for them, and re-layouts  58.4 us (9%)
  matrix products  49.5 us (8%)
  between operations  14.8 us (2%)
  starting transfers between devices  8.36 us (1%)
  other arithmetic  6.68 us (1%)
    unnamed x8, waiting for transfers between devices  166 us
    unnamed x1, blocking collectives  126 us
    reduce_scatter x1, waiting for transfers between devices, body(): lax.psum_scatter(numer_all.astype(jnp.bfloat16), 'blk', scatter_dimension...  110 us
    all_gather x1, blocking collectives, body(): lax.all_gather(decode_key_value, 'blk', axis=1, tiled=True)  42.4 us
    all_gather x1, blocking collectives, body(): lax.all_gather(decode_query_rows, 'blk', axis=0, tiled=True)  42.1 us
    unnamed x43, local copies, waits for them, and re-layouts  27.1 us
    dot_general x7, matrix products, attend(): jnp.einsum('qhgk,khd->qhgd', weights.astype(jnp.bfloat16), value_rows, pr...  22.1 us
    dot_general x7, matrix products, attend(): jnp.einsum('qhgd,khd->qhgk', query_rows, key_rows, preferred_element_type...  19.9 us
  transfers between devices with their start and end apart: 9, of which 6 were waited for; matrix products, arithmetic and copies ran while one was open for 15% of the time, Pallas kernels for 0%

commit v1 on v0

--- a/solution.py
+++ b/solution.py
@@ -29,7 +29,7 @@
         * q_scale
     )
     capped = soft_cap * jnp.tanh(logits / soft_cap)
-    weights = jnp.where(visible[:, None, None, :], jnp.exp(capped), 0.0)
+    weights = jnp.where(visible, jnp.exp(capped), 0.0)
     denominator = jnp.sum(weights, axis=3)
     numerator = jnp.einsum(
         "qhgk,khd->qhgd",
@@ -38,10 +38,6 @@
         preferred_element_type=jnp.float32,
     )
     return (numerator, denominator)
-
-
-def earlier(block_rows):
-    return from_behind(block_rows, "blk", 1)
 
 
 def token_tables(lengths, prefix_ids, token_ids):
@@ -85,65 +81,66 @@
     q_heads = suffix_query.shape[1] // head_dim
     kv_heads = suffix_key_value.shape[2] // head_dim
     query_group_width = q_heads // kv_heads
+    blk_size = lax.axis_size("blk")
     my_index = lax.axis_index("blk")
+
+    local_pages = prefix_page_store.shape[1]
+    dq_rows = decode_query_rows.shape[0]
+    pieces = [
+        prefix_page_store.reshape(-1),
+        decode_query_rows.reshape(-1),
+        decode_key_value.reshape(-1),
+    ]
+    sizes = [piece.shape[0] for piece in pieces]
+    packed = jnp.concatenate(pieces)
+    gathered = lax.all_gather(packed, "blk", axis=0, tiled=False)
+    cut_a = sizes[0]
+    cut_b = cut_a + sizes[1]
+    pre_all = gathered[:, :cut_a].reshape(blk_size, 2, local_pages, page_len, kv_heads, head_dim)
+    all_dq = gathered[:, cut_a:cut_b].reshape(blk_size * dq_rows, q_heads * head_dim)
+    all_dkv = (
+        gathered[:, cut_b:]
+        .reshape(blk_size, 2, dq_rows, kv_heads * head_dim)
+        .transpose(1, 0, 2, 3)
+        .reshape(2, blk_size * dq_rows, kv_heads * head_dim)
+    )
+
+    look_back = 4
+    pieces_back = [from_behind(suffix_key_value, "blk", d) for d in range(look_back, 0, -1)]
+    window = jnp.concatenate(pieces_back + [suffix_key_value], axis=1)
+
     own_queries = suffix_query.reshape(tok_rows, kv_heads, query_group_width, head_dim)
     token_ids = my_index * tok_rows + jnp.arange(tok_rows, dtype=jnp.int32)
     tok_start, tok_prefix = token_tables(suffix_lengths, suffix_prefix, token_ids)
-    look_back = 4
-    pieces_back = [suffix_key_value]
-    for step in range(look_back):
-        pieces_back.insert(0, earlier(pieces_back[0]))
-    window = jnp.concatenate(pieces_back, axis=1)
     key_ids = (my_index - look_back) * tok_rows + jnp.arange(
         (look_back + 1) * tok_rows, dtype=jnp.int32
     )
     visible = (key_ids[None, :] >= tok_start[:, None]) & (key_ids[None, :] <= token_ids[:, None])
     window_keys = window[0].reshape((look_back + 1) * tok_rows, kv_heads, head_dim)
     window_values = window[1].reshape((look_back + 1) * tok_rows, kv_heads, head_dim)
-    own_numer, own_denom = attend(own_queries, window_keys, window_values, visible, q_scale)
+    own_numer, own_denom = attend(
+        own_queries, window_keys, window_values, visible[:, None, None, :], q_scale
+    )
+
     pool_pages = prefix_table.shape[0]
-    page_owner = inverse_rows(prefix_table, jnp.arange(pool_pages, dtype=jnp.int32)) // (
-        PREFIX_LENGTH // PAGE_TOKENS
-    )
-    all_queries = lax.all_gather(suffix_query, "blk", axis=0, tiled=True)
-    all_tokens = all_queries.shape[0]
-    all_ids = jnp.arange(all_tokens, dtype=jnp.int32)
-    unused_start, all_prefix = token_tables(suffix_lengths, suffix_prefix, all_ids)
-    local_pages = prefix_page_store.shape[1]
-    held_owner = lax.dynamic_slice_in_dim(page_owner, my_index * local_pages, local_pages, 0)
-    held_cols = jnp.repeat(held_owner, page_len)
-    held_keys = prefix_page_store[0].reshape(local_pages * page_len, kv_heads, head_dim)
-    held_values = prefix_page_store[1].reshape(local_pages * page_len, kv_heads, head_dim)
-    block_rows = math.gcd(all_tokens, 1024)
-    query_blocks = all_queries.reshape(
-        all_tokens // block_rows, block_rows, kv_heads, query_group_width, head_dim
-    )
-    prefix_blocks = all_prefix.reshape(all_tokens // block_rows, block_rows)
-
-    def one_block(element):
-        block_queries, block_prefix = element
-        seen = block_prefix[:, None] == held_cols[None, :]
-        return attend(block_queries, held_keys, held_values, seen, q_scale)
-
-    numer_all, denom_all = lax.map(one_block, (query_blocks, prefix_blocks))
-    numer_all = numer_all.reshape(all_tokens, kv_heads, query_group_width, head_dim)
-    denom_all = denom_all.reshape(all_tokens, kv_heads, query_group_width)
-    pre_numer, pre_denom = (
-        lax.psum_scatter(
-            numer_all.astype(jnp.bfloat16), "blk", scatter_dimension=0, tiled=True
-        ).astype(jnp.float32),
-        lax.psum_scatter(
-            denom_all.astype(jnp.bfloat16), "blk", scatter_dimension=0, tiled=True
-        ).astype(jnp.float32),
-    )
+    per_prefix = PREFIX_LENGTH // PAGE_TOKENS
+    page_owner = inverse_rows(prefix_table, jnp.arange(pool_pages, dtype=jnp.int32)) // per_prefix
+    owner_grid = page_owner.reshape(blk_size, local_pages)
+    pre_numer = jnp.zeros((tok_rows, kv_heads, query_group_width, head_dim), jnp.float32)
+    pre_denom = jnp.zeros((tok_rows, kv_heads, query_group_width), jnp.float32)
+    for page in range(local_pages):
+        keys = pre_all[:, 0, page].reshape(blk_size * page_len, kv_heads, head_dim)
+        values = pre_all[:, 1, page].reshape(blk_size * page_len, kv_heads, head_dim)
+        cols = jnp.repeat(owner_grid[:, page], page_len)
+        seen = tok_prefix[:, None] == cols[None, :]
+        numer_c, denom_c = attend(own_queries, keys, values, seen[:, None, None, :], q_scale)
+        pre_numer = pre_numer + numer_c
+        pre_denom = pre_denom + denom_c
     suffix_attn = ((own_numer + pre_numer) / (own_denom + pre_denom)[..., None]).astype(
         jnp.bfloat16
     )
     suffix_attn = suffix_attn.reshape(tok_rows, q_heads * head_dim)
-    all_dq, all_dkv = (
-        lax.all_gather(decode_query_rows, "blk", axis=0, tiled=True),
-        lax.all_gather(decode_key_value, "blk", axis=1, tiled=True),
-    )
+
     slot_total = all_dq.shape[0]
     slot_pages = SLOT_CAPACITY // PAGE_TOKENS
     local_cache = decode_page_store.shape[1]
@@ -181,21 +178,15 @@
         preferred_element_type=jnp.float32,
     )
     slot_float = slot_hot.astype(jnp.float32)
-    slot_numer = jnp.einsum(
-        "ls,lhgd->shgd", slot_float, page_numer, precision=lax.Precision.HIGHEST
-    )
-    slot_denom = jnp.einsum("ls,lhg->shg", slot_float, page_denom, precision=lax.Precision.HIGHEST)
-    mine_numer, mine_denom = (
-        lax.psum_scatter(
-            slot_numer.astype(jnp.bfloat16), "blk", scatter_dimension=0, tiled=True
-        ).astype(jnp.float32),
-        lax.psum_scatter(
-            slot_denom.astype(jnp.bfloat16), "blk", scatter_dimension=0, tiled=True
-        ).astype(jnp.float32),
-    )
+    page_sums = jnp.concatenate([page_numer, page_denom[..., None]], axis=3)
+    slot_sums = jnp.einsum("ls,lhgd->shgd", slot_float, page_sums, precision=lax.Precision.HIGHEST)
+    mine_sums = lax.psum_scatter(slot_sums, "blk", scatter_dimension=0, tiled=True)
+    mine_numer = mine_sums[..., :head_dim]
+    mine_denom = mine_sums[..., head_dim]
     decode_attn = (mine_numer / mine_denom[..., None]).astype(jnp.bfloat16)
     decode_rows = decode_attn.shape[0]
     decode_attn = decode_attn.reshape(decode_rows, q_heads * head_dim)
+
     attention = jnp.concatenate([suffix_attn, decode_attn], axis=0)
     projected = jnp.dot(attention, out_weight, preferred_element_type=jnp.float32)
     residual = jnp.concatenate([suffix_resid, decode_resid], axis=0).astype(jnp.float32)

time: 658 us -> 544 us (0.83)
  blocking collectives: 227 us -> 16.9 us
  waiting for transfers between devices: 292 us -> 345 us
  local copies, waits for them, and re-layouts: 58.4 us -> 81.1 us
  starting transfers between devices: 8.36 us -> 17.9 us
    unnamed x1 -> x0, blocking collectives: 126 us -> none
    reduce_scatter x1 -> x0, waiting for transfers between devices: 110 us -> none  [body(): lax.psum_scatter(numer_all.astype(jnp.bfloat16), 'blk', scatter_dimension...]
    unnamed x8 -> x5, waiting for transfers between devices: 166 us -> 261 us
    all_gather x2 -> x0, blocking collectives: 84.4 us -> none  [the longest x1 42.4 us: body(): lax.all_gather(decode_key_value, 'blk', axis=1, tiled=True)]
    all_gather x1, waiting for transfers between devices: 0.01 us -> 65.3 us  [body(): gathered = lax.all_gather(packed, 'blk', axis=0, tiled=False)]
    slice x2 -> x12, local copies, waits for them, and re-layouts: 0.17 us -> 31.2 us  [the longest x4 17.3 us: body(): keys = pre_all[:, 0, page].reshape(blk_size * page_len, kv_heads, head_dim)]
    dynamic_slice x13 -> x0, local copies, waits for them, and re-layouts: 11.9 us -> none  [the longest x12 11.8 us: body(): numer_all, denom_all = lax.map(one_block, (query_blocks, prefix_blocks))]
    all_gather x0 -> x1, local copies, waits for them, and re-layouts: none -> 11.8 us  [body(): gathered = lax.all_gather(packed, 'blk', axis=0, tiled=False)]
  transfers between devices with their start and end apart: 9 -> 7, of which waited for: 6 -> 6; matrix products, arithmetic and copies ran while one was open for 15% -> 18% of each run, Pallas kernels for 0% -> 0%
where the time goes in v1:
time: 544 us; the launch traced here: 543 us
  waiting for transfers between devices  345 us (63%)
  local copies, waits for them, and re-layouts  81.1 us (15%)
  matrix products  55.1 us (10%)
  starting transfers between devices  17.9 us (3%)
  blocking collectives  16.9 us (3%)
  between operations  14.9 us (3%)
  other arithmetic  12.8 us (2%)
    unnamed x5, waiting for transfers between devices  261 us
    all_gather x1, waiting for transfers between devices, body(): gathered = lax.all_gather(packed, 'blk', axis=0, tiled=False)  65.3 us
    dot_general x4, matrix products, attend(): jnp.einsum('qhgd,khd->qhgk', query_rows, key_rows, preferred_element_type...  25.7 us
    dot_general x4, matrix products, attend(): jnp.einsum('qhgk,khd->qhgd', weights.astype(jnp.bfloat16), value_rows, pr...  20.8 us
    ppermute x4, waiting for transfers between devices, from_behind(): return lax.ppermute(block, axis, route)  18.1 us
    ppermute x4, starting transfers between devices, from_behind(): return lax.ppermute(block, axis, route)  17.6 us
    slice x4, local copies, waits for them, and re-layouts, body(): keys = pre_all[:, 0, page].reshape(blk_size * page_len, kv_heads, head_dim)  17.3 us
    psum x1, blocking collectives, body(): mean_square = lax.psum(jnp.sum(mine * mine, axis=1), 'kv') / D  16.9 us
  transfers between devices with their start and end apart: 7, of which 6 were waited for; matrix products, arithmetic and copies ran while one was open for 18% of the time, Pallas kernels for 0%

profile of v1, /device:TPU:2, one launch (start us, length us, event | category | flops | bytes accessed | tf_op | source)
XLA Modules:
  0.0 543.4 jit_solution(7102548860051849925)
XLA Ops:
  10.9 9.1 %collective-permute-start = (bf16[2,192,256]{2,1,0:T(8,128)(2,1)}, bf16[2,192,256]{2,1,0:T(8,128)(2,1)}, u32[]{:S(2)}, u32[]{:S(2)}) collective-permute-start(bf16[2,192,256]{2,1,0:T(8,128)(2,1)} %param.16), channel_id=1, source_target_pairs={{0,4},{1,5},{2,6},{3,7},{4,8},{5,9},{6,10},{7,11},{8,12},{9,13},{1... | collective-permute-start | bytes 589832 | tf_op jit(solution)/shard_map/ppermute | solution.py:23
  22.6 2.8 collective-permute-start.2
  25.4 3.2 collective-permute-start.3
  42.2 5.6 %collective-permute-done.1 = bf16[2,192,256]{2,1,0:T(8,128)(2,1)S(1)} collective-permute-done((bf16[2,192,256]{2,1,0:T(8,128)(2,1)}, bf16[2,192,256]{2,1,0:T(8,128)(2,1)S(1)}, u32[]{:S(2)}, u32[]{:S(2)}) %collective-permute-start.1) | collective-permute-done | bytes 196640 | tf_op jit(solution)/shard_map/ppermute | solution.py:23
  47.8 9.1 %collective-permute-done.2 = bf16[2,192,256]{2,1,0:T(8,128)(2,1)S(1)} collective-permute-done((bf16[2,192,256]{2,1,0:T(8,128)(2,1)}, bf16[2,192,256]{2,1,0:T(8,128)(2,1)S(1)}, u32[]{:S(2)}, u32[]{:S(2)}) %collective-permute-start.2) | collective-permute-done | bytes 196640 | tf_op jit(solution)/shard_map/ppermute | solution.py:23
  56.9 3.5 collective-permute-done.3
  61.5 3.4 fusion.15
  65.0 65.3 %all-gather.3.cloned.1.call-done = bf16[6356992]{0:T(1024)(128)(2,1)} async-done(((bf16[198656]{0:T(1024)(128)(2,1)}), bf16[6356992]{0:T(1024)(128)(2,1)}) %all-gather.3.cloned.1.call-update) | async-done | bytes 12714000 | tf_op jit(solution)/shard_map/all_gather | solution.py:96
  130.3 11.8 %reshape.371 = bf16[32,198656]{1,0:T(8,128)(2,1)} reshape(bf16[6356992]{0:T(1024)(128)(2,1)} %all-gather.3.cloned.1.call-done) | data formatting | bytes 25427968 | tf_op jit(solution)/shard_map/all_gather | solution.py:96
  143.0 10.4 %slice.82 = bf16[32,196608]{1,0:T(8,128)(2,1)} slice(bf16[32,198656]{1,0:T(8,128)(2,1)} %reshape.371), slice={[0:32], [0:196608]} | slice | bytes 25165824 | tf_op jit(solution)/shard_map/slice | solution.py:99
  163.8 16.1 %reshape.364 = bf16[32,2,3,128,2,128]{5,4,3,2,1,0:T(2,128)(2,1)} reshape(bf16[32,196608]{1,0:T(8,128)(2,1)} %slice.82) | data formatting | bytes 25165824 | tf_op jit(solution)/shard_map/reshape | solution.py:99
  179.9 15.7 %fusion.88 = (bf16[32,1,1,128,2,128]{5,4,3,2,1,0:T(2,128)(2,1)S(1)}, bf16[32,1,1,128,2,128]{5,4,3,2,1,0:T(2,128)(2,1)S(1)}, bf16[32,1,1,128,2,128]{5,4,3,2,1,0:T...) fusion(bf16[32,2,3,128,2,128]{5,4,3,2,1,0:T(2,128)(2,1)} %resha, ...), kind=kLoop, calls=%fused_computation.129 | loop fusion | bytes 25165824 | tf_op jit(solution)/shard_map/slice | solution.py:132
  199.4 7.4 %fusion.4 = (f32[192,2,2]{0,2,1:T(2,128)S(1)}, f32[2,4096,192,2]{1,2,3,0:T(8,128)}) fusion(pred[192,4096]{1,0:T(8,128)(4,1)S(1)} %copy-done.3, bf16[4096,2,128,1]{2,0,3,1:T(8,128)(2,1)S(1)} %bitcast.132, bf16[192,2,2,128]{3,2,1,0:T(2,128)(2,1)S(1)} %reshape.360), kind=kOutput, calls=%fused_computation.7 | convolution fusion | flops 817888512 | bytes 15666176 | tf_op jit(solution)/shard_map/qhgd,khd->qhgk/dot_general | solution.py:28
  206.7 6.5 %fusion.6 = f32[2,128,192,2]{1,2,3,0:T(8,128)S(1)} fusion(bf16[4096,2,128,1]{2,0,3,1:T(8,128)(2,1)S(1)} %bitcast.130, f32[2,4096,192,2]{1,2,3,0:T(8,128)} %get-tuple-element.42, pred[192,4096]{1,0:T(8,128)(4,1)S(1)} %copy-done.3), kind=kOutput, calls=%fused_computation.10 | convolution fusion | flops 817889280 | bytes 15859712 | tf_op jit(solution)/shard_map/qhgk,khd->qhgd/dot_general | solution.py:34
  213.3 7.6 %fusion.2 = (f32[192,2,2]{0,2,1:T(2,128)S(1)}, f32[2,4096,192,2]{1,2,3,0:T(8,128)}) fusion(pred[192,4096]{1,0:T(8,128)(4,1)S(1)} %copy-done.2, bf16[4096,2,128,1]{2,0,3,1:T(8,128)(2,1)S(1)} %bitcast.131, bf16[192,2,2,128]{3,2,1,0:T(2,128)(2,1)S(1)} %reshape.360), kind=kOutput, calls=%fused_computation.5 | convolution fusion | flops 817888512 | bytes 15666176 | tf_op jit(solution)/shard_map/qhgd,khd->qhgk/dot_general | solution.py:28
  220.9 6.5 %fusion.8 = f32[2,128,192,2]{1,2,3,0:T(8,128)S(1)} fusion(bf16[4096,2,128,1]{2,0,3,1:T(8,128)(2,1)S(1)} %bitcast.128, f32[2,4096,192,2]{1,2,3,0:T(8,128)} %get-tuple-element.46, pred[192,4096]{1,0:T(8,128)(4,1)S(1)} %copy-done.2), kind=kOutput, calls=%fused_computation.11 | convolution fusion | flops 817889280 | bytes 15859712 | tf_op jit(solution)/shard_map/qhgk,khd->qhgd/dot_general | solution.py:34
  227.4 7.4 %fusion = (f32[192,2,2]{0,2,1:T(2,128)S(1)}, f32[2,4096,192,2]{1,2,3,0:T(8,128)}) fusion(pred[192,4096]{1,0:T(8,128)(4,1)S(1)} %copy-done.1, bf16[4096,2,128,1]{2,0,3,1:T(8,128)(2,1)S(1)} %bitcast.129, bf16[192,2,2,128]{3,2,1,0:T(2,128)(2,1)S(1)} %reshape.360), kind=kOutput, calls=%fused_computation.3 | convolution fusion | flops 817888512 | bytes 15666176 | tf_op jit(solution)/shard_map/qhgd,khd->qhgk/dot_general | solution.py:28
  234.7 6.8 %fusion.29 = f32[2,128,192,2]{1,2,3,0:T(8,128)S(1)} fusion(f32[2,128,192,2]{1,2,3,0:T(8,128)S(1)} %fusion.6, f32[2,128,192,2]{1,2,3,0:T(8,128)S(1)} %fusion.8, bf16[4096,2,128,1]{2,0,3,1:T(8,128)(2,1)S(1)} %bitcast.127, f32[2,4096,192,2]{1,2,3,0:T(8,128)} %get-tuple-element.44, pred[192,4096]{1,0:T(8,128)(4,1)S(1)} %copy-done.1), kind=kOutput, calls=%fused_computation.28 | convolution fusion | flops 818085888 | bytes 16646144 | tf_op jit(solution)/shard_map/qhgk,khd->qhgd/dot_general | solution.py:34
  242.9 192.4 %all-reduce.3.cloned.1.call-done = f32[64,2,2,129]{3,0,2,1:T(8,128)} async-done(((f32[64,2,2,129]{3,0,2,1:T(8,128)}), f32[64,2,2,129]{3,0,2,1:T(8,128)}) %all-reduce.3.cloned.1.call-update) | async-done | bytes 132112
  437.0 4.7 convolution_convert_fusion
  441.7 4.0 copy.138
  445.8 2.6 copy.117
  448.4 68.8 %reduce-scatter.5.cloned.1.call-done = bf16[576,194]{1,0:T(8,128)(2,1)} async-done(((bf16[4608,194]{1,0:T(8,128)(2,1)}), bf16[576,194]{1,0:T(8,128)(2,1)}) %reduce-scatter.5.cloned.1.call-update) | async-done | bytes 223504
  518.5 16.9 %psum.7 = f32[194]{0:T(256)S(1)} all-reduce(f32[194]{0:T(256)S(1)} %fusion.43), channel_id=1, replica_groups=mesh['kv'=8,'blk'=32] {'kv'}, use_global_device_ids=true, to_apply=%region_14.15 | all-reduce | flops 194 | bytes 1552 | tf_op jit(solution)/shard_map/psum | solution.py:196
  (116 shorter events, 41.1 us)
Async XLA Ops:
  7.2 30.4 %copy-start = (bf16[2,16,128,256]{3,2,1,0:T(8,128)(2,1)S(1)}, bf16[2,16,128,256]{3,2,1,0:T(8,128)(2,1)}, u32[]{:S(2)}) copy-start(bf16[2,16,128,256]{3,2,1,0:T(8,128)(2,1)} %param.25) | copy-start | bytes 6291460
  7.2 123.1 %all-gather.3.cloned.1.call-start = ((), (), s32[]{:S(2)}) async-start(), calls=%async_computation.1 | async-start | bytes 13111296 | tf_op jit(solution)/shard_map/all_gather | solution.py:96
  10.9 424.5 %all-reduce.3.cloned.1.call-start = ((), (), s32[]{:S(2)}) async-start(), calls=%async_computation.3 | async-start | bytes 524288
  10.9 30.3 %collective-permute-start = (bf16[2,192,256]{2,1,0:T(8,128)(2,1)}, bf16[2,192,256]{2,1,0:T(8,128)(2,1)}, u32[]{:S(2)}, u32[]{:S(2)}) collective-permute-start(bf16[2,192,256]{2,1,0:T(8,128)(2,1)} %param.16), channel_id=1, source_target_pairs={{0,4},{1,5},{2,6},{3,7},{4,8},{5,9},{6,10},{7,11},{8,12},{9,13},{1... | collective-permute-start | bytes 589832 | tf_op jit(solution)/shard_map/ppermute | solution.py:23
  20.0 27.8 %collective-permute-start.1 = (bf16[2,192,256]{2,1,0:T(8,128)(2,1)}, bf16[2,192,256]{2,1,0:T(8,128)(2,1)S(1)}, u32[]{:S(2)}, u32[]{:S(2)}) collective-permute-start(bf16[2,192,256]{2,1,0:T(8,128)(2,1)} %param.16), channel_id=1, source_target_pairs={{0,3},{1,4},{2,5},{3,6},{4,7},{5,8},{6,9},{7,10},{8,11},{9,12},{10... | collective-permute-start | bytes 589832 | tf_op jit(solution)/shard_map/ppermute | solution.py:23
  22.6 34.3 %collective-permute-start.2 = (bf16[2,192,256]{2,1,0:T(8,128)(2,1)}, bf16[2,192,256]{2,1,0:T(8,128)(2,1)S(1)}, u32[]{:S(2)}, u32[]{:S(2)}) collective-permute-start(bf16[2,192,256]{2,1,0:T(8,128)(2,1)} %param.16), channel_id=1, source_target_pairs={{0,2},{1,3},{2,4},{3,5},{4,6},{5,7},{6,8},{7,9},{8,10},{9,11},{10,... | collective-permute-start | bytes 589832 | tf_op jit(solution)/shard_map/ppermute | solution.py:23
  25.4 35.0 %collective-permute-start.3 = (bf16[2,192,256]{2,1,0:T(8,128)(2,1)}, bf16[2,192,256]{2,1,0:T(8,128)(2,1)S(1)}, u32[]{:S(2)}, u32[]{:S(2)}) collective-permute-start(bf16[2,192,256]{2,1,0:T(8,128)(2,1)} %param.16), channel_id=1, source_target_pairs={{0,1},{1,2},{2,3},{3,4},{4,5},{5,6},{6,7},{7,8},{8,9},{9,10},{10,1... | collective-permute-start | bytes 589832 | tf_op jit(solution)/shard_map/ppermute | solution.py:23
  32.3 122.1 %copy-start.13 = (s32[16]{0:T(128)}, s32[16]{0:T(128)S(1)}, u32[]{:S(2)}) copy-start(s32[16]{0:T(128)S(1)} %and_select_fusion.3) | copy-start | bytes 196
  34.9 5.0 copy-start.6
  34.9 5.1 copy-start.14
  37.5 22.9 %copy-start.7 = (bf16[2,192,256]{2,1,0:T(8,128)(2,1)S(1)}, bf16[2,192,256]{2,1,0:T(8,128)(2,1)}, u32[]{:S(2)}) copy-start(bf16[2,192,256]{2,1,0:T(8,128)(2,1)} %param.16) | copy-start | bytes 589828
  157.0 0.7 copy-start.8
  157.0 0.7 copy-start.9
  163.6 353.6 %reduce-scatter.5.cloned.1.call-start = ((), (), s32[]{:S(2)}) async-start(), calls=%async_computation.2 | async-start | bytes 2654208
  198.2 1.1 copy-start.3
  206.7 6.5 %copy-start.2 = (pred[192,4096]{1,0:T(8,128)(4,1)S(1)}, pred[192,4096]{1,0:T(8,128)(4,1)}, u32[]{:S(2)}) copy-start(pred[192,4096]{1,0:T(8,128)(4,1)} %get-tuple-element.35) | copy-start | bytes 2359300
  220.9 6.5 %copy-start.1 = (pred[192,4096]{1,0:T(8,128)(4,1)S(1)}, pred[192,4096]{1,0:T(8,128)(4,1)}, u32[]{:S(2)}) copy-start(pred[192,4096]{1,0:T(8,128)(4,1)} %get-tuple-element.34) | copy-start | bytes 2359300
  234.7 6.8 %copy-start.11 = (f32[192,2,2]{0,2,1:T(2,128)S(1)}, f32[192,2,2]{0,2,1:T(2,128)}, u32[]{:S(2)}) copy-start(f32[192,2,2]{0,2,1:T(2,128)} %get-tuple-element.39) | copy-start | bytes 9220
  234.7 6.8 %copy-start.4 = (bf16[960,2,128]{2,1,0:T(2,128)(2,1)S(1)}, bf16[960,2,128]{2,1,0:T(2,128)(2,1)}, u32[]{:S(2)}) copy-start(bf16[960,2,128]{2,1,0:T(2,128)(2,1)} %reshape_squeeze.30) | copy-start | bytes 1474564
  234.7 6.8 %copy-start.15 = (f32[2,960,192,2]{1,2,3,0:T(8,128)S(1)}, f32[2,960,192,2]{1,2,3,0:T(8,128)}, u32[]{:S(2)}) copy-start(f32[2,960,192,2]{1,2,3,0:T(8,128)} %get-tuple-element.40) | copy-start | bytes 8847364
  445.8 89.6 %copy-start.5 = (bf16[192,576]{1,0:T(8,128)(2,1)S(1)}, bf16[192,576]{1,0:T(8,128)(2,1)}, u32[]{:S(2)}) copy-start(bf16[192,576]{1,0:T(8,128)(2,1)} %param.17) | copy-start | bytes 663556
  445.8 89.6 %copy-start.10 = (f32[576]{0:T(1024)S(1)}, f32[576]{0:T(1024)}, u32[]{:S(2)}) copy-start(f32[576]{0:T(1024)} %param.22) | copy-start | bytes 6916
  445.8 89.6 %copy-start.12 = (bf16[2,576]{1,0:T(2,128)(2,1)S(1)}, bf16[2,576]{1,0:T(2,128)(2,1)}, u32[]{:S(2)}) copy-start(bf16[2,576]{1,0:T(2,128)(2,1)} %param.20) | copy-start | bytes 6916
Sparse Core Ops, SparseCore 0:
  11.0 119.2 all-gather.2
  163.7 271.5 all-reduce.2
  445.9 71.2 reduce-scatter.4

commit v2 on v1

--- a/solution.py
+++ b/solution.py
@@ -86,23 +86,26 @@
 
     local_pages = prefix_page_store.shape[1]
     dq_rows = decode_query_rows.shape[0]
-    pieces = [
-        prefix_page_store.reshape(-1),
-        decode_query_rows.reshape(-1),
-        decode_key_value.reshape(-1),
-    ]
-    sizes = [piece.shape[0] for piece in pieces]
-    packed = jnp.concatenate(pieces)
+    kv_width = kv_heads * head_dim
+    held_rows = local_pages * page_len
+    dq_lines = decode_query_rows.size // kv_width
+    dkv_lines = decode_key_value.size // kv_width
+    extra_lines = 16
+    extra = jnp.zeros((2, extra_lines, kv_width), jnp.bfloat16)
+    extra = extra.at[0, :dq_lines].set(decode_query_rows.reshape(dq_lines, kv_width))
+    extra = extra.at[1, :dkv_lines].set(decode_key_value.reshape(dkv_lines, kv_width))
+    packed = jnp.concatenate([prefix_page_store.reshape(2, held_rows, kv_width), extra], axis=1)
     gathered = lax.all_gather(packed, "blk", axis=0, tiled=False)
-    cut_a = sizes[0]
-    cut_b = cut_a + sizes[1]
-    pre_all = gathered[:, :cut_a].reshape(blk_size, 2, local_pages, page_len, kv_heads, head_dim)
-    all_dq = gathered[:, cut_a:cut_b].reshape(blk_size * dq_rows, q_heads * head_dim)
+    all_keys = gathered[:, 0, :held_rows].reshape(blk_size * held_rows, kv_heads, head_dim)
+    all_values = gathered[:, 1, :held_rows].reshape(blk_size * held_rows, kv_heads, head_dim)
+    all_dq = gathered[:, 0, held_rows : held_rows + dq_lines].reshape(
+        blk_size * dq_rows, q_heads * head_dim
+    )
     all_dkv = (
-        gathered[:, cut_b:]
-        .reshape(blk_size, 2, dq_rows, kv_heads * head_dim)
+        gathered[:, 1, held_rows : held_rows + dkv_lines]
+        .reshape(blk_size, 2, dq_rows, kv_width)
         .transpose(1, 0, 2, 3)
-        .reshape(2, blk_size * dq_rows, kv_heads * head_dim)
+        .reshape(2, blk_size * dq_rows, kv_width)
     )
 
     look_back = 4
@@ -125,15 +128,17 @@
     pool_pages = prefix_table.shape[0]
     per_prefix = PREFIX_LENGTH // PAGE_TOKENS
     page_owner = inverse_rows(prefix_table, jnp.arange(pool_pages, dtype=jnp.int32)) // per_prefix
-    owner_grid = page_owner.reshape(blk_size, local_pages)
+    key_owner = jnp.repeat(page_owner, page_len)
     pre_numer = jnp.zeros((tok_rows, kv_heads, query_group_width, head_dim), jnp.float32)
     pre_denom = jnp.zeros((tok_rows, kv_heads, query_group_width), jnp.float32)
-    for page in range(local_pages):
-        keys = pre_all[:, 0, page].reshape(blk_size * page_len, kv_heads, head_dim)
-        values = pre_all[:, 1, page].reshape(blk_size * page_len, kv_heads, head_dim)
-        cols = jnp.repeat(owner_grid[:, page], page_len)
-        seen = tok_prefix[:, None] == cols[None, :]
-        numer_c, denom_c = attend(own_queries, keys, values, seen[:, None, None, :], q_scale)
+    chunks = 3
+    chunk_keys = all_keys.shape[0] // chunks
+    for chunk in range(chunks):
+        span = slice(chunk * chunk_keys, (chunk + 1) * chunk_keys)
+        seen = tok_prefix[:, None] == key_owner[span][None, :]
+        numer_c, denom_c = attend(
+            own_queries, all_keys[span], all_values[span], seen[:, None, None, :], q_scale
+        )
         pre_numer = pre_numer + numer_c
         pre_denom = pre_denom + denom_c
     suffix_attn = ((own_numer + pre_numer) / (own_denom + pre_denom)[..., None]).astype(
@@ -180,7 +185,8 @@
     slot_float = slot_hot.astype(jnp.float32)
     page_sums = jnp.concatenate([page_numer, page_denom[..., None]], axis=3)
     slot_sums = jnp.einsum("ls,lhgd->shgd", slot_float, page_sums, precision=lax.Precision.HIGHEST)
-    mine_sums = lax.psum_scatter(slot_sums, "blk", scatter_dimension=0, tiled=True)
+    slot_sums = slot_sums.reshape((blk_size, slot_total // blk_size) + slot_sums.shape[1:])
+    mine_sums = jnp.sum(lax.all_to_all(slot_sums, "blk", 0, 0, tiled=False), axis=0)
     mine_numer = mine_sums[..., :head_dim]
     mine_denom = mine_sums[..., head_dim]
     decode_attn = (mine_numer / mine_denom[..., None]).astype(jnp.bfloat16)
@@ -190,9 +196,11 @@
     attention = jnp.concatenate([suffix_attn, decode_attn], axis=0)
     projected = jnp.dot(attention, out_weight, preferred_element_type=jnp.float32)
     residual = jnp.concatenate([suffix_resid, decode_resid], axis=0).astype(jnp.float32)
-    mine = lax.psum_scatter(
-        projected.astype(jnp.bfloat16), "kv", scatter_dimension=1, tiled=True
-    ).astype(jnp.float32)
+    kv_size = lax.axis_size("kv")
+    shares = projected.astype(jnp.bfloat16).reshape(projected.shape[0], kv_size, -1)
+    mine = jnp.sum(
+        lax.all_to_all(shares, "kv", 1, 1, tiled=False).astype(jnp.float32), axis=1
+    )
     mean_square = lax.psum(jnp.sum(mine * mine, axis=1), "kv") / D
     normed = mine * lax.rsqrt(mean_square + norm_eps)[:, None] * post_gain[None, :]
     hidden = (residual + normed).astype(jnp.bfloat16)

time: 544 us -> 307 us (0.56)
  waiting for transfers between devices: 345 us -> 104 us
  starting transfers between devices: 17.9 us -> 38.6 us
  local copies, waits for them, and re-layouts: 81.1 us -> 63.3 us
    unnamed x5 -> x1, waiting for transfers between devices: 261 us -> 0.02 us
    all_to_all x0 -> x2, waiting for transfers between devices: none -> 24.2 us  [the longest x1 24.2 us: body(): lax.all_to_all(shares, 'kv', 1, 1, tiled=False).astype(jnp.float32)]
    another operation x1 -> x6, local copies, waits for them, and re-layouts: 0.74 us -> 21.8 us  [the longest x1 9.73 us: body(): gathered[:, 0, :held_rows].reshape(blk_size * held_rows, kv_heads, head_dim)]
    all_to_all x0 -> x2, starting transfers between devices: none -> 20.9 us  [the longest x1 16.1 us: body(): lax.all_to_all(slot_sums, 'blk', 0, 0, tiled=False)]
    all_gather x1 -> x0, local copies, waits for them, and re-layouts: 11.8 us -> none  [body(): gathered = lax.all_gather(packed, 'blk', axis=0, tiled=False)]
    unnamed x44 -> x34, local copies, waits for them, and re-layouts: 15.7 us -> 5.08 us
    reshape x4 -> x5, local copies, waits for them, and re-layouts: 16.2 us -> 8.32 us  [the longest x2 7.39 us: body(): projected.astype(jnp.bfloat16).reshape(projected.shape[0], kv_size, -1)]
    all_gather x1, waiting for transfers between devices: 65.3 us -> 59.2 us  [body(): gathered = lax.all_gather(packed, 'blk', axis=0, tiled=False)]
  transfers between devices with their start and end apart: 7 -> 7, of which waited for: 6 -> 5; matrix products, arithmetic and copies ran while one was open for 18% -> 31% of each run, Pallas kernels for 0% -> 0%
where the time goes in v2:
time: 307 us; the launch traced here: 306 us
  waiting for transfers between devices  104 us (34%)
  local copies, waits for them, and re-layouts  63.3 us (21%)
  matrix products  53.2 us (17%)
  starting transfers between devices  38.6 us (13%)
  blocking collectives  17.4 us (6%)
  other arithmetic  14.5 us (5%)
  between operations  14.4 us (5%)
    all_gather x1, waiting for transfers between devices, body(): gathered = lax.all_gather(packed, 'blk', axis=0, tiled=False)  59.2 us
    dot_general x4, matrix products, attend(): jnp.einsum('qhgd,khd->qhgk', query_rows, key_rows, preferred_element_type...  24.9 us
    all_to_all x1, waiting for transfers between devices, body(): lax.all_to_all(shares, 'kv', 1, 1, tiled=False).astype(jnp.float32)  24.2 us
    dot_general x4, matrix products, attend(): jnp.einsum('qhgk,khd->qhgd', weights.astype(jnp.bfloat16), value_rows, pr...  21.7 us
    ppermute x4, waiting for transfers between devices, from_behind(): return lax.ppermute(block, axis, route)  20.7 us
    ppermute x4, starting transfers between devices, from_behind(): return lax.ppermute(block, axis, route)  17.7 us
    psum x1, blocking collectives, body(): mean_square = lax.psum(jnp.sum(mine * mine, axis=1), 'kv') / D  17.4 us
    all_to_all x1, starting transfers between devices, body(): lax.all_to_all(slot_sums, 'blk', 0, 0, tiled=False)  16.1 us
  transfers between devices with their start and end apart: 7, of which 5 were waited for; matrix products, arithmetic and copies ran while one was open for 31% of the time, Pallas kernels for 0%

profile of v2, /device:TPU:2, one launch (start us, length us, event | category | flops | bytes accessed | tf_op | source)
XLA Modules:
  0.0 305.7 jit_solution(1728882166277414351)
XLA Ops:
  10.6 9.2 %collective-permute-start = (bf16[2,192,256]{2,1,0:T(8,128)(2,1)}, bf16[2,192,256]{2,1,0:T(8,128)(2,1)S(1)}, u32[]{:S(2)}, u32[]{:S(2)}) collective-permute-start(bf16[2,192,256]{2,1,0:T(8,128)(2,1)} %param.20), channel_id=1, source_target_pairs={{0,4},{1,5},{2,6},{3,7},{4,8},{5,9},{6,10},{7,11},{8,12},{9,13},{1... | collective-permute-start | bytes 589832 | tf_op jit(solution)/shard_map/ppermute | solution.py:23
  25.2 3.2 %collective-permute-start.3 = (bf16[2,192,256]{2,1,0:T(8,128)(2,1)}, bf16[2,192,256]{2,1,0:T(8,128)(2,1)S(1)}, u32[]{:S(2)}, u32[]{:S(2)}) collective-permute-start(bf16[2,192,256]{2,1,0:T(8,128)(2,1)} %param.20), channel_id=1, source_target_pairs={{0,1},{1,2},{2,3},{3,4},{4,5},{5,6},{6,7},{7,8},{8,9},{9,10},{10,1... | collective-permute-start | bytes 589832 | tf_op jit(solution)/shard_map/ppermute | solution.py:23
  39.6 8.0 %collective-permute-done.1 = bf16[2,192,256]{2,1,0:T(8,128)(2,1)S(1)} collective-permute-done((bf16[2,192,256]{2,1,0:T(8,128)(2,1)}, bf16[2,192,256]{2,1,0:T(8,128)(2,1)S(1)}, u32[]{:S(2)}, u32[]{:S(2)}) %collective-permute-start.1) | collective-permute-done | bytes 196640 | tf_op jit(solution)/shard_map/ppermute | solution.py:23
  47.6 9.3 %collective-permute-done.2 = bf16[2,192,256]{2,1,0:T(8,128)(2,1)S(1)} collective-permute-done((bf16[2,192,256]{2,1,0:T(8,128)(2,1)}, bf16[2,192,256]{2,1,0:T(8,128)(2,1)S(1)}, u32[]{:S(2)}, u32[]{:S(2)}) %collective-permute-start.2) | collective-permute-done | bytes 196640 | tf_op jit(solution)/shard_map/ppermute | solution.py:23
  56.9 3.4 %collective-permute-done.3 = bf16[2,192,256]{2,1,0:T(8,128)(2,1)S(1)} collective-permute-done((bf16[2,192,256]{2,1,0:T(8,128)(2,1)}, bf16[2,192,256]{2,1,0:T(8,128)(2,1)S(1)}, u32[]{:S(2)}, u32[]{:S(2)}) %collective-permute-start.3) | collective-permute-done | bytes 196640 | tf_op jit(solution)/shard_map/ppermute | solution.py:23
  63.8 59.2 %all-gather.3.cloned.1.call-done = bf16[64,400,256]{2,1,0:T(8,128)(2,1)} async-done(((bf16[2,400,256]{2,1,0:T(8,128)(2,1)}), bf16[64,400,256]{2,1,0:T(8,128)(2,1)}) %all-gather.3.cloned.1.call-update) | async-done | bytes 13107216 | tf_op jit(solution)/shard_map/all_gather | solution.py:98
  124.0 10.5 %fusion.83 = (bf16[32,1,384,256]{3,2,1,0:T(8,128)(2,1)}, bf16[32,1,384,256]{3,2,1,0:T(8,128)(2,1)}) fusion(bf16[32,2,400,256]{3,2,1,0:T(8,128)(2,1)} %bitcast.140), kind=kLoop, calls=%fused_computation.126 | loop fusion | bytes 25165824 | tf_op jit(solution)/shard_map/slice | solution.py:100
  140.6 16.1 %all-to-all-start = ((f32[32,2,2,2,129]{4,1,3,2,0:T(2,128)}), f32[32,2,2,2,129]{4,1,3,2,0:T(2,128)S(1)}, u32[]{:S(2)}, u32[]{:S(2)}) async-start(f32[32,2,2,2,129]{4,1,3,2,0:T(2,128)} %copy.146), calls=%async_computation | async-start | bytes 524288 | tf_op jit(solution)/shard_map/all_to_all | solution.py:189
  156.7 9.7 %reshape.446 = bf16[12288,2,128]{2,1,0:T(2,128)(2,1)} reshape(bf16[32,1,384,256]{3,2,1,0:T(8,128)(2,1)} %get-tuple-element.47) | data formatting | bytes 12582912 | tf_op jit(solution)/shard_map/reshape;squeeze | solution.py:99
  166.4 7.5 %fusion.86 = (bf16[4096,2,128]{2,1,0:T(2,128)(2,1)}, bf16[4096,2,128]{2,1,0:T(2,128)(2,1)}, bf16[4096,2,128]{2,1,0:T(2,128)(2,1)}) fusion(bf16[12288,2,128]{2,1,0:T(2,128)(2,1)} %reshape.446), kind=kLoop, calls=%fused_computation.129 | loop fusion | bytes 12582912 | tf_op jit(solution)/shard_map/slice | solution.py:140
  173.9 9.7 %reshape.445 = bf16[12288,2,128]{2,1,0:T(2,128)(2,1)} reshape(bf16[32,1,384,256]{3,2,1,0:T(8,128)(2,1)} %get-tuple-element.46) | data formatting | bytes 12582912 | tf_op jit(solution)/shard_map/reshape;squeeze | solution.py:100
  183.7 6.2 %fusion.85 = (bf16[4096,2,128]{2,1,0:T(2,128)(2,1)S(1)}, bf16[4096,2,128]{2,1,0:T(2,128)(2,1)S(1)}, bf16[4096,2,128]{2,1,0:T(2,128)(2,1)S(1)}) fusion(bf16[12288,2,128]{2,1,0:T(2,128)(2,1)} %reshape.445), kind=kLoop, calls=%fused_computation.128 | loop fusion | bytes 12582912 | tf_op jit(solution)/shard_map/slice | solution.py:140
  189.9 7.8 %fusion.4 = (f32[192,2,2]{0,2,1:T(2,128)S(1)}, f32[2,4096,192,2]{1,2,3,0:T(8,128)}) fusion(pred[192,4096]{1,0:T(8,128)(4,1)S(1)} %copy-done.6, bf16[192,2,2,128]{3,2,1,0:T(2,128)(2,1)S(1)} %reshape.424, bf16[4096,2,128]{2,1,0:T(2,128)(2,1)S(1)} %copy-done.3), kind=kOutput, calls=%fused_computation.7 | convolution fusion | flops 817888512 | bytes 15666176 | tf_op jit(solution)/shard_map/qhgd,khd->qhgk/dot_general | solution.py:28
  197.7 6.7 %fusion.6 = f32[2,128,192,2]{1,2,3,0:T(8,128)S(1)} fusion(f32[2,4096,192,2]{1,2,3,0:T(8,128)} %get-tuple-element.71, pred[192,4096]{1,0:T(8,128)(4,1)S(1)} %copy-done.6, bf16[4096,2,128]{2,1,0:T(2,128)(2,1)S(1)} %get-tuple-element.52), kind=kOutput, calls=%fused_computation.10 | convolution fusion | flops 817889280 | bytes 15859712 | tf_op jit(solution)/shard_map/qhgk,khd->qhgd/dot_general | solution.py:34
  204.4 7.8 %fusion.2 = (f32[192,2,2]{0,2,1:T(2,128)S(1)}, f32[2,4096,192,2]{1,2,3,0:T(8,128)}) fusion(pred[192,4096]{1,0:T(8,128)(4,1)S(1)} %copy-done.5, bf16[192,2,2,128]{3,2,1,0:T(2,128)(2,1)S(1)} %reshape.424, bf16[4096,2,128]{2,1,0:T(2,128)(2,1)S(1)} %copy-done.2), kind=kOutput, calls=%fused_computation.5 | convolution fusion | flops 817888512 | bytes 15666176 | tf_op jit(solution)/shard_map/qhgd,khd->qhgk/dot_general | solution.py:28
  212.2 6.7 %fusion.8 = f32[2,128,192,2]{1,2,3,0:T(8,128)S(1)} fusion(f32[2,4096,192,2]{1,2,3,0:T(8,128)} %get-tuple-element.75, pred[192,4096]{1,0:T(8,128)(4,1)S(1)} %copy-done.5, bf16[4096,2,128]{2,1,0:T(2,128)(2,1)S(1)} %get-tuple-element.51), kind=kOutput, calls=%fused_computation.11 | convolution fusion | flops 817889280 | bytes 15859712 | tf_op jit(solution)/shard_map/qhgk,khd->qhgd/dot_general | solution.py:34
  218.9 8.0 %fusion = (f32[192,2,2]{0,2,1:T(2,128)S(1)}, f32[2,4096,192,2]{1,2,3,0:T(8,128)}) fusion(pred[192,4096]{1,0:T(8,128)(4,1)S(1)} %copy-done.4, bf16[192,2,2,128]{3,2,1,0:T(2,128)(2,1)S(1)} %reshape.424, bf16[4096,2,128]{2,1,0:T(2,128)(2,1)S(1)} %copy-done.1), kind=kOutput, calls=%fused_computation.3 | convolution fusion | flops 817888512 | bytes 15666176 | tf_op jit(solution)/shard_map/qhgd,khd->qhgk/dot_general | solution.py:28
  226.9 6.6 %fusion.38 = bf16[192,2,2,128]{3,0,2,1:T(8,128)(2,1)S(1)} fusion(f32[2,128,192,2]{1,2,3,0:T(8,128)S(1)} %copy-done.13, f32[2,128,192,2]{1,2,3,0:T(8,128)S(1)} %fusion.6, f32[2,128,192,2]{1,2,3,0:T(8,128)S(1)} %fusion.8, f32[2,4096,192,2]{1,2,3,0:T(8,128)} %get-tuple-element.73, pred[192,4096]{1,0:T(8,128)(4,1)S(1)} %copy-done.4, ...), kind=kOutput, calls=%fused_computation.40 | convolution fusion | flops 818380800 | bytes 16845824 | tf_op jit(solution)/shard_map/qhgk,khd->qhgd/dot_general | solution.py:34
  234.1 4.7 %convolution_convert_fusion = bf16[194,4608]{1,0:T(8,128)(2,1)} fusion(bf16[512,4608]{1,0:T(8,128)(2,1)} %param.25, bf16[2,512]{1,0:T(2,128)(2,1)S(1)} %bitcast.149, bf16[192,512]{1,0:T(8,128)(2,1)S(1)} %reshape.428), kind=kOutput, calls=%fused_computation.9 | convolution fusion | flops 916698112 | bytes 6705152 | tf_op jit(solution)/shard_map/dot_general | solution.py:197
  238.9 4.3 %reshape.433 = bf16[194,8,576]{2,1,0:T(8,128)(2,1)} reshape(bf16[194,4608]{1,0:T(8,128)(2,1)} %convolution_convert_fusion) | data formatting | bytes 3575808 | tf_op jit(solution)/shard_map/reshape | solution.py:200
  243.1 3.1 %copy.150 = bf16[194,8,576]{2,0,1:T(8,128)(2,1)} copy(bf16[194,8,576]{2,1,0:T(8,128)(2,1)} %reshape.433) | data formatting | bytes 3575808 | tf_op jit(solution)/shard_map/reshape | solution.py:200
  246.2 4.8 %all-to-all-start.1 = ((bf16[194,8,576]{2,0,1:T(8,128)(2,1)}), bf16[194,8,576]{2,0,1:T(8,128)(2,1)}, u32[]{:S(2)}, u32[]{:S(2)}) async-start(bf16[194,8,576]{2,0,1:T(8,128)(2,1)} %copy.150), calls=%async_computation.1 | async-start | bytes 4096000 | tf_op jit(solution)/shard_map/all_to_all | solution.py:202
  253.6 24.2 %all-to-all-done.1 = bf16[194,8,576]{2,0,1:T(8,128)(2,1)} async-done(((bf16[194,8,576]{2,0,1:T(8,128)(2,1)}), bf16[194,8,576]{2,0,1:T(8,128)(2,1)}, u32[]{:S(2)}, u32[]{:S(2)}) %all-to-all-start.1) | async-done | bytes 1787936 | tf_op jit(solution)/shard_map/all_to_all | solution.py:202
  279.9 17.4 %psum.7 = f32[194]{0:T(256)S(1)} all-reduce(f32[194]{0:T(256)S(1)} %multiply_reduce_fusion), channel_id=1, replica_groups=mesh['kv'=8,'blk'=32] {'kv'}, use_global_device_ids=true, to_apply=%region_14.15 | all-reduce | flops 194 | bytes 1552 | tf_op jit(solution)/shard_map/psum | solution.py:204
  (105 shorter events, 37.0 us)
Async XLA Ops:
  7.2 30.0 %copy-start = (bf16[2,16,128,256]{3,2,1,0:T(8,128)(2,1)S(1)}, bf16[2,16,128,256]{3,2,1,0:T(8,128)(2,1)}, u32[]{:S(2)}) copy-start(bf16[2,16,128,256]{3,2,1,0:T(8,128)(2,1)} %param.29) | copy-start | bytes 6291460
  7.2 115.9 %all-gather.3.cloned.1.call-start = ((), (), s32[]{:S(2)}) async-start(), calls=%async_computation.2 | async-start | bytes 13516800 | tf_op jit(solution)/shard_map/all_gather | solution.py:98
  10.6 28.9 %copy-start.8 = (bf16[192,512]{1,0:T(8,128)(2,1)S(1)}, bf16[192,512]{1,0:T(8,128)(2,1)}, u32[]{:S(2)}) copy-start(bf16[192,512]{1,0:T(8,128)(2,1)} %param.19) | copy-start | bytes 589828
  10.6 29.0 %collective-permute-start = (bf16[2,192,256]{2,1,0:T(8,128)(2,1)}, bf16[2,192,256]{2,1,0:T(8,128)(2,1)S(1)}, u32[]{:S(2)}, u32[]{:S(2)}) collective-permute-start(bf16[2,192,256]{2,1,0:T(8,128)(2,1)} %param.20), channel_id=1, source_target_pairs={{0,4},{1,5},{2,6},{3,7},{4,8},{5,9},{6,10},{7,11},{8,12},{9,13},{1... | collective-permute-start | bytes 589832 | tf_op jit(solution)/shard_map/ppermute | solution.py:23
  19.8 27.8 %collective-permute-start.1 = (bf16[2,192,256]{2,1,0:T(8,128)(2,1)}, bf16[2,192,256]{2,1,0:T(8,128)(2,1)S(1)}, u32[]{:S(2)}, u32[]{:S(2)}) collective-permute-start(bf16[2,192,256]{2,1,0:T(8,128)(2,1)} %param.20), channel_id=1, source_target_pairs={{0,3},{1,4},{2,5},{3,6},{4,7},{5,8},{6,9},{7,10},{8,11},{9,12},{10... | collective-permute-start | bytes 589832 | tf_op jit(solution)/shard_map/ppermute | solution.py:23
  22.4 34.5 %collective-permute-start.2 = (bf16[2,192,256]{2,1,0:T(8,128)(2,1)}, bf16[2,192,256]{2,1,0:T(8,128)(2,1)S(1)}, u32[]{:S(2)}, u32[]{:S(2)}) collective-permute-start(bf16[2,192,256]{2,1,0:T(8,128)(2,1)} %param.20), channel_id=1, source_target_pairs={{0,2},{1,3},{2,4},{3,5},{4,6},{5,7},{6,8},{7,9},{8,10},{9,11},{10,... | collective-permute-start | bytes 589832 | tf_op jit(solution)/shard_map/ppermute | solution.py:23
  25.2 35.2 %collective-permute-start.3 = (bf16[2,192,256]{2,1,0:T(8,128)(2,1)}, bf16[2,192,256]{2,1,0:T(8,128)(2,1)S(1)}, u32[]{:S(2)}, u32[]{:S(2)}) collective-permute-start(bf16[2,192,256]{2,1,0:T(8,128)(2,1)} %param.20), channel_id=1, source_target_pairs={{0,1},{1,2},{2,3},{3,4},{4,5},{5,6},{6,7},{7,8},{8,9},{9,10},{10,1... | collective-permute-start | bytes 589832 | tf_op jit(solution)/shard_map/ppermute | solution.py:23
  34.5 25.9 %copy-start.9 = (bf16[2,192,256]{2,1,0:T(8,128)(2,1)S(1)}, bf16[2,192,256]{2,1,0:T(8,128)(2,1)}, u32[]{:S(2)}) copy-start(bf16[2,192,256]{2,1,0:T(8,128)(2,1)} %param.20) | copy-start | bytes 589828
  39.5 21.2 %copy-start.10 = (pred[192,960]{1,0:T(8,128)(4,1)S(1)}, pred[192,960]{1,0:T(8,128)(4,1)}, u32[]{:S(2)}) copy-start(pred[192,960]{1,0:T(8,128)(4,1)} %compare_and_fusion) | copy-start | bytes 552964
  140.6 93.2 %all-to-all-start = ((f32[32,2,2,2,129]{4,1,3,2,0:T(2,128)}), f32[32,2,2,2,129]{4,1,3,2,0:T(2,128)S(1)}, u32[]{:S(2)}, u32[]{:S(2)}) async-start(f32[32,2,2,2,129]{4,1,3,2,0:T(2,128)} %copy.146), calls=%async_computation | async-start | bytes 524288 | tf_op jit(solution)/shard_map/all_to_all | solution.py:189
  183.7 6.2 %copy-start.3 = (bf16[4096,2,128]{2,1,0:T(2,128)(2,1)S(1)}, bf16[4096,2,128]{2,1,0:T(2,128)(2,1)}, u32[]{:S(2)}) copy-start(bf16[4096,2,128]{2,1,0:T(2,128)(2,1)} %get-tuple-element.55) | copy-start | bytes 6291460
  183.7 6.2 %copy-start.6 = (pred[192,4096]{1,0:T(8,128)(4,1)S(1)}, pred[192,4096]{1,0:T(8,128)(4,1)}, u32[]{:S(2)}) copy-start(pred[192,4096]{1,0:T(8,128)(4,1)} %get-tuple-element.62) | copy-start | bytes 2359300
  197.7 6.7 %copy-start.2 = (bf16[4096,2,128]{2,1,0:T(2,128)(2,1)S(1)}, bf16[4096,2,128]{2,1,0:T(2,128)(2,1)}, u32[]{:S(2)}) copy-start(bf16[4096,2,128]{2,1,0:T(2,128)(2,1)} %get-tuple-element.54) | copy-start | bytes 6291460
  197.7 6.7 %copy-start.5 = (pred[192,4096]{1,0:T(8,128)(4,1)S(1)}, pred[192,4096]{1,0:T(8,128)(4,1)}, u32[]{:S(2)}) copy-start(pred[192,4096]{1,0:T(8,128)(4,1)} %get-tuple-element.61) | copy-start | bytes 2359300
  212.2 6.7 %copy-start.1 = (bf16[4096,2,128]{2,1,0:T(2,128)(2,1)S(1)}, bf16[4096,2,128]{2,1,0:T(2,128)(2,1)}, u32[]{:S(2)}) copy-start(bf16[4096,2,128]{2,1,0:T(2,128)(2,1)} %get-tuple-element.53) | copy-start | bytes 6291460
  212.2 6.7 %copy-start.4 = (pred[192,4096]{1,0:T(8,128)(4,1)S(1)}, pred[192,4096]{1,0:T(8,128)(4,1)}, u32[]{:S(2)}) copy-start(pred[192,4096]{1,0:T(8,128)(4,1)} %get-tuple-element.60) | copy-start | bytes 2359300
  218.9 8.0 %copy-start.13 = (f32[2,128,192,2]{1,2,3,0:T(8,128)S(1)}, f32[2,128,192,2]{1,2,3,0:T(8,128)}, u32[]{:S(2)}) copy-start(f32[2,128,192,2]{1,2,3,0:T(8,128)} %fusion.20) | copy-start | bytes 1179652
  246.2 31.6 %all-to-all-start.1 = ((bf16[194,8,576]{2,0,1:T(8,128)(2,1)}), bf16[194,8,576]{2,0,1:T(8,128)(2,1)}, u32[]{:S(2)}, u32[]{:S(2)}) async-start(bf16[194,8,576]{2,0,1:T(8,128)(2,1)} %copy.150), calls=%async_computation.1 | async-start | bytes 4096000 | tf_op jit(solution)/shard_map/all_to_all | solution.py:202
  251.0 46.4 %copy-start.7 = (bf16[192,576]{1,0:T(8,128)(2,1)S(1)}, bf16[192,576]{1,0:T(8,128)(2,1)}, u32[]{:S(2)}) copy-start(bf16[192,576]{1,0:T(8,128)(2,1)} %param.21) | copy-start | bytes 663556
  251.0 46.4 %copy-start.11 = (f32[576]{0:T(1024)S(1)}, f32[576]{0:T(1024)}, u32[]{:S(2)}) copy-start(f32[576]{0:T(1024)} %param.26) | copy-start | bytes 6916
  251.0 46.3 %copy-start.12 = (bf16[2,576]{1,0:T(2,128)(2,1)S(1)}, bf16[2,576]{1,0:T(2,128)(2,1)}, u32[]{:S(2)}) copy-start(bf16[2,576]{1,0:T(2,128)(2,1)} %param.24) | copy-start | bytes 6916
Sparse Core Ops, SparseCore 0:
  10.7 112.2 all-gather.2

commit v3 on v2

--- a/solution.py
+++ b/solution.py
@@ -36,6 +36,19 @@
         weights.astype(jnp.bfloat16),
         value_rows,
         preferred_element_type=jnp.float32,
+    )
+    return (numerator, denominator)
+
+
+def attend_rows(query_rows, key_rows, value_rows, visible, q_scale):
+    logits = (
+        jnp.dot(query_rows, key_rows.T, preferred_element_type=jnp.float32) * q_scale
+    )
+    capped = soft_cap * jnp.tanh(logits / soft_cap)
+    weights = jnp.where(visible, jnp.exp(capped), 0.0)
+    denominator = jnp.sum(weights, axis=1)
+    numerator = jnp.dot(
+        weights.astype(jnp.bfloat16), value_rows, preferred_element_type=jnp.float32
     )
     return (numerator, denominator)
 
@@ -96,8 +109,6 @@
     extra = extra.at[1, :dkv_lines].set(decode_key_value.reshape(dkv_lines, kv_width))
     packed = jnp.concatenate([prefix_page_store.reshape(2, held_rows, kv_width), extra], axis=1)
     gathered = lax.all_gather(packed, "blk", axis=0, tiled=False)
-    all_keys = gathered[:, 0, :held_rows].reshape(blk_size * held_rows, kv_heads, head_dim)
-    all_values = gathered[:, 1, :held_rows].reshape(blk_size * held_rows, kv_heads, head_dim)
     all_dq = gathered[:, 0, held_rows : held_rows + dq_lines].reshape(
         blk_size * dq_rows, q_heads * head_dim
     )
@@ -129,18 +140,30 @@
     per_prefix = PREFIX_LENGTH // PAGE_TOKENS
     page_owner = inverse_rows(prefix_table, jnp.arange(pool_pages, dtype=jnp.int32)) // per_prefix
     key_owner = jnp.repeat(page_owner, page_len)
-    pre_numer = jnp.zeros((tok_rows, kv_heads, query_group_width, head_dim), jnp.float32)
-    pre_denom = jnp.zeros((tok_rows, kv_heads, query_group_width), jnp.float32)
+    row_prefix = jnp.repeat(tok_prefix, query_group_width)
     chunks = 3
-    chunk_keys = all_keys.shape[0] // chunks
-    for chunk in range(chunks):
-        span = slice(chunk * chunk_keys, (chunk + 1) * chunk_keys)
-        seen = tok_prefix[:, None] == key_owner[span][None, :]
-        numer_c, denom_c = attend(
-            own_queries, all_keys[span], all_values[span], seen[:, None, None, :], q_scale
-        )
-        pre_numer = pre_numer + numer_c
-        pre_denom = pre_denom + denom_c
+    chunk_keys = blk_size * held_rows // chunks
+    head_numer = []
+    head_denom = []
+    for head in range(kv_heads):
+        lanes = slice(head * head_dim, (head + 1) * head_dim)
+        head_keys = gathered[:, 0, :held_rows, lanes].reshape(blk_size * held_rows, head_dim)
+        head_values = gathered[:, 1, :held_rows, lanes].reshape(blk_size * held_rows, head_dim)
+        head_queries = own_queries[:, head].reshape(tok_rows * query_group_width, head_dim)
+        numer_h = jnp.zeros((tok_rows * query_group_width, head_dim), jnp.float32)
+        denom_h = jnp.zeros((tok_rows * query_group_width,), jnp.float32)
+        for chunk in range(chunks):
+            span = slice(chunk * chunk_keys, (chunk + 1) * chunk_keys)
+            seen = row_prefix[:, None] == key_owner[span][None, :]
+            numer_c, denom_c = attend_rows(
+                head_queries, head_keys[span], head_values[span], seen, q_scale
+            )
+            numer_h = numer_h + numer_c
+            denom_h = denom_h + denom_c
+        head_numer.append(numer_h.reshape(tok_rows, query_group_width, head_dim))
+        head_denom.append(denom_h.reshape(tok_rows, query_group_width))
+    pre_numer = jnp.stack(head_numer, axis=1)
+    pre_denom = jnp.stack(head_denom, axis=1)
     suffix_attn = ((own_numer + pre_numer) / (own_denom + pre_denom)[..., None]).astype(
         jnp.bfloat16
     )

time: 307 us -> 267 us (0.87)
  local copies, waits for them, and re-layouts: 63.3 us -> 32.2 us
  matrix products: 53.2 us -> 47.5 us
  other arithmetic: 14.5 us -> 11.2 us
    dot_general x0 -> x12, matrix products: none -> 37 us  [the longest x6 22.1 us: attend_rows(): jnp.dot(query_rows, key_rows.T, preferred_element_type=jnp.float32)]
    dot_general x4 -> x1, matrix products: 24.9 us -> 2.8 us  [attend(): jnp.einsum('qhgd,khd->qhgk', query_rows, key_rows, preferred_element_type...]
    dot_general x4 -> x1, matrix products: 21.7 us -> 1.06 us  [attend(): jnp.einsum('qhgk,khd->qhgd', weights.astype(jnp.bfloat16), value_rows, pr...]
    another operation x5, local copies, waits for them, and re-layouts: 21.7 us -> 2.29 us  [the longest x1 9.73 us: body(): gathered[:, 0, :held_rows].reshape(blk_size * held_rows, kv_heads, head_dim)]
    slice x4 -> x3, local copies, waits for them, and re-layouts: 24.3 us -> 8.44 us  [the longest x1 7.59 us: body(): gathered[:, 1, :held_rows, lanes].reshape(blk_size * held_rows, head_dim)]
    unnamed x34 -> x30, local copies, waits for them, and re-layouts: 5.08 us -> 6.97 us
  transfers between devices with their start and end apart: 7 -> 7, of which waited for: 5 -> 4; matrix products, arithmetic and copies ran while one was open for 31% -> 13% of each run, Pallas kernels for 0% -> 0%
where the time goes in v3:
time: 267 us
  waiting for transfers between devices  105 us (39%)
  matrix products  47.5 us (18%)
  starting transfers between devices  38.5 us (14%)
  local copies, waits for them, and re-layouts  32.2 us (12%)
  blocking collectives  17.4 us (7%)
  between operations  14.6 us (5%)
  other arithmetic  11.2 us (4%)
    all_gather x1, waiting for transfers between devices, body(): gathered = lax.all_gather(packed, 'blk', axis=0, tiled=False)  58.2 us
    all_to_all x1, waiting for transfers between devices, body(): lax.all_to_all(shares, 'kv', 1, 1, tiled=False).astype(jnp.float32)  24.2 us
    ppermute x4, waiting for transfers between devices, from_behind(): return lax.ppermute(block, axis, route)  22.7 us
    dot_general x6, matrix products, attend_rows(): jnp.dot(query_rows, key_rows.T, preferred_element_type=jnp.float32)  22.1 us
    ppermute x4, starting transfers between devices, from_behind(): return lax.ppermute(block, axis, route)  17.6 us
    psum x1, blocking collectives, body(): mean_square = lax.psum(jnp.sum(mine * mine, axis=1), 'kv') / D  17.4 us
    all_to_all x1, starting transfers between devices, body(): lax.all_to_all(slot_sums, 'blk', 0, 0, tiled=False)  16 us
    dot_general x6, matrix products, attend_rows(): jnp.dot(weights.astype(jnp.bfloat16), value_rows, preferred_element_type=...  14.9 us
  transfers between devices with their start and end apart: 7, of which 4 were waited for; matrix products, arithmetic and copies ran while one was open for 13% of the time, Pallas kernels for 0%

profile of v3, /device:TPU:2, one launch (start us, length us, event | category | flops | bytes accessed | tf_op | source)
XLA Modules:
  0.0 266.5 jit_solution(6861845821407239159)
XLA Ops:
  10.6 5.2 %collective-permute-start.2 = (bf16[2,192,256]{2,1,0:T(8,128)(2,1)}, bf16[2,192,256]{2,1,0:T(8,128)(2,1)S(1)}, u32[]{:S(2)}, u32[]{:S(2)}) collective-permute-start(bf16[2,192,256]{2,1,0:T(8,128)(2,1)} %param.20), channel_id=1, source_target_pairs={{0,2},{1,3},{2,4},{3,5},{4,6},{5,7},{6,8},{7,9},{8,10},{9,11},{10,... | collective-permute-start | bytes 589832 | tf_op jit(solution)/shard_map/ppermute | solution.py:23
  15.7 5.6 %collective-permute-start.1 = (bf16[2,192,256]{2,1,0:T(8,128)(2,1)}, bf16[2,192,256]{2,1,0:T(8,128)(2,1)S(1)}, u32[]{:S(2)}, u32[]{:S(2)}) collective-permute-start(bf16[2,192,256]{2,1,0:T(8,128)(2,1)} %param.20), channel_id=1, source_target_pairs={{0,3},{1,4},{2,5},{3,6},{4,7},{5,8},{6,9},{7,10},{8,11},{9,12},{10... | collective-permute-start | bytes 589832 | tf_op jit(solution)/shard_map/ppermute | solution.py:23
  21.3 3.7 %collective-permute-start = (bf16[2,192,256]{2,1,0:T(8,128)(2,1)}, bf16[2,192,256]{2,1,0:T(8,128)(2,1)}, u32[]{:S(2)}, u32[]{:S(2)}) collective-permute-start(bf16[2,192,256]{2,1,0:T(8,128)(2,1)} %param.20), channel_id=1, source_target_pairs={{0,4},{1,5},{2,6},{3,7},{4,8},{5,9},{6,10},{7,11},{8,12},{9,13},{1... | collective-permute-start | bytes 589832 | tf_op jit(solution)/shard_map/ppermute | solution.py:23
  25.0 3.2 %collective-permute-start.3 = (bf16[2,192,256]{2,1,0:T(8,128)(2,1)}, bf16[2,192,256]{2,1,0:T(8,128)(2,1)S(1)}, u32[]{:S(2)}, u32[]{:S(2)}) collective-permute-start(bf16[2,192,256]{2,1,0:T(8,128)(2,1)} %param.20), channel_id=1, source_target_pairs={{0,1},{1,2},{2,3},{3,4},{4,5},{5,6},{6,7},{7,8},{8,9},{9,10},{10,1... | collective-permute-start | bytes 589832 | tf_op jit(solution)/shard_map/ppermute | solution.py:23
  38.1 22.1 %collective-permute-done = bf16[2,192,256]{2,1,0:T(8,128)(2,1)} collective-permute-done((bf16[2,192,256]{2,1,0:T(8,128)(2,1)}, bf16[2,192,256]{2,1,0:T(8,128)(2,1)}, u32[]{:S(2)}, u32[]{:S(2)}) %collective-permute-start) | collective-permute-done | bytes 196640 | tf_op jit(solution)/shard_map/ppermute | solution.py:23
  65.8 58.2 %all-gather.3.cloned.1.call-done = bf16[64,400,256]{2,1,0:T(8,128)(2,1)} async-done(((bf16[2,400,256]{2,1,0:T(8,128)(2,1)}), bf16[64,400,256]{2,1,0:T(8,128)(2,1)}) %all-gather.3.cloned.1.call-update) | async-done | bytes 13107216 | tf_op jit(solution)/shard_map/all_gather | solution.py:111
  125.0 7.6 %fusion.83 = (bf16[32,1,384,128]{3,2,1,0:T(8,128)(2,1)}, bf16[32,1,384,128]{3,2,1,0:T(8,128)(2,1)}, bf16[32,1,384,128]{3,2,1,0:T(8,128)(2,1)S(1)}, bf16[32,1,384,128]{3,2,1,0:T(8,128)(2,1)S(1)}) fusion(bf16[32,2,400,256]{3,2,1,0:T(8,128)(2,1)} %bitcast.97), kind=kLoop, calls=%fused_computation.121 | loop fusion | bytes 25165824 | tf_op jit(solution)/shard_map/slice | solution.py:151
  132.6 3.8 %fusion.90 = (f32[384]{0:T(512)S(1)}, bf16[384,4096]{0,1:T(8,128)(2,1)}) fusion(bf16[384,128]{1,0:T(8,128)(2,1)S(1)} %bitcast.121, bf16[12288,128]{1,0:T(8,128)(2,1)S(1)} %bitcast.109, s32[4096]{0:T(1024)S(1)} %get-tuple-element.77, s32[384]{0:T(512)S(1)} %eq.56), kind=kOutput, calls=%fused_computation.128 | convolution fusion | flops 412089984 | bytes 4312576 | tf_op jit(solution)/shard_map/dot_general | solution.py:45
  136.3 3.7 %fusion.91 = (f32[384]{0:T(512)S(1)}, bf16[384,4096]{0,1:T(8,128)(2,1)}) fusion(bf16[384,128]{1,0:T(8,128)(2,1)S(1)} %bitcast.122, bf16[12288,128]{1,0:T(8,128)(2,1)S(1)} %bitcast.110, s32[4096]{0:T(1024)S(1)} %broadcast_bitcast_fusion.2, s32[384]{0:T(512)S(1)} %eq.56), kind=kOutput, calls=%fused_computation.129 | convolution fusion | flops 412089984 | bytes 4312576 | tf_op jit(solution)/shard_map/dot_general | solution.py:45
  140.0 3.6 %fusion.93 = (f32[384]{0:T(512)S(1)}, bf16[384,4096]{0,1:T(8,128)(2,1)}) fusion(bf16[384,128]{1,0:T(8,128)(2,1)S(1)} %bitcast.118, bf16[12288,128]{1,0:T(8,128)(2,1)S(1)} %bitcast.106, s32[4096]{0:T(1024)S(1)} %get-tuple-element.77, s32[384]{0:T(512)S(1)} %eq.56), kind=kOutput, calls=%fused_computation.131 | convolution fusion | flops 412089984 | bytes 4312576 | tf_op jit(solution)/shard_map/dot_general | solution.py:45
  143.7 3.7 %fusion.94 = (f32[384]{0:T(512)S(1)}, bf16[384,4096]{0,1:T(8,128)(2,1)}) fusion(bf16[384,128]{1,0:T(8,128)(2,1)S(1)} %bitcast.119, bf16[12288,128]{1,0:T(8,128)(2,1)S(1)} %bitcast.107, s32[4096]{0:T(1024)S(1)} %broadcast_bitcast_fusion.2, s32[384]{0:T(512)S(1)} %eq.56), kind=kOutput, calls=%fused_computation.132 | convolution fusion | flops 412089984 | bytes 4312576 | tf_op jit(solution)/shard_map/dot_general | solution.py:45
  147.3 3.7 %fusion.92 = (f32[384]{0:T(512)S(1)}, bf16[384,4096]{0,1:T(8,128)(2,1)}) fusion(bf16[384,128]{1,0:T(8,128)(2,1)S(1)} %bitcast.123, bf16[12288,128]{1,0:T(8,128)(2,1)S(1)} %bitcast.111, s32[4096]{0:T(1024)S(1)} %get-tuple-element.78, s32[384]{0:T(512)S(1)} %eq.56), kind=kOutput, calls=%fused_computation.130 | convolution fusion | flops 412089984 | bytes 4312576 | tf_op jit(solution)/shard_map/dot_general | solution.py:45
  151.0 3.7 %fusion.95 = (f32[384]{0:T(512)S(1)}, bf16[384,4096]{0,1:T(8,128)(2,1)}) fusion(bf16[384,128]{1,0:T(8,128)(2,1)S(1)} %bitcast.120, bf16[12288,128]{1,0:T(8,128)(2,1)S(1)} %bitcast.108, s32[4096]{0:T(1024)S(1)} %get-tuple-element.78, s32[384]{0:T(512)S(1)} %eq.56), kind=kOutput, calls=%fused_computation.133 | convolution fusion | flops 412089984 | bytes 4312576 | tf_op jit(solution)/shard_map/dot_general | solution.py:45
  160.7 16.0 %all-to-all-start = ((f32[32,2,2,2,129]{4,1,3,2,0:T(2,128)}), f32[32,2,2,2,129]{4,1,3,2,0:T(2,128)S(1)}, u32[]{:S(2)}, u32[]{:S(2)}) async-start(f32[32,2,2,2,129]{4,1,3,2,0:T(2,128)} %copy.105), calls=%async_computation | async-start | bytes 524288 | tf_op jit(solution)/shard_map/all_to_all | solution.py:212
  177.0 3.3 %fusion = f32[384,128]{1,0:T(8,128)S(1)} fusion(bf16[384,4096]{0,1:T(8,128)(2,1)} %get-tuple-element.66, bf16[12288,128]{1,0:T(8,128)(2,1)} %bitcast.101), kind=kOutput, calls=%fused_computation.9 | convolution fusion | flops 402653184 | bytes 4390912 | tf_op jit(solution)/shard_map/dot_general | solution.py:50
  180.4 3.1 %fusion.2 = f32[384,128]{1,0:T(8,128)S(1)} fusion(bf16[384,4096]{0,1:T(8,128)(2,1)} %get-tuple-element.70, bf16[12288,128]{1,0:T(8,128)(2,1)S(1)} %bitcast.102), kind=kOutput, calls=%fused_computation.11 | convolution fusion | flops 402653184 | bytes 4390912 | tf_op jit(solution)/shard_map/dot_general | solution.py:50
  184.8 3.3 %fusion.6 = f32[384,128]{1,0:T(8,128)S(1)} fusion(bf16[384,4096]{0,1:T(8,128)(2,1)} %get-tuple-element.72, bf16[12288,128]{1,0:T(8,128)(2,1)} %bitcast.98), kind=kOutput, calls=%fused_computation.15 | convolution fusion | flops 402653184 | bytes 4390912 | tf_op jit(solution)/shard_map/dot_general | solution.py:50
  188.1 3.1 %fusion.8 = f32[384,128]{1,0:T(8,128)S(1)} fusion(bf16[384,4096]{0,1:T(8,128)(2,1)} %get-tuple-element.76, bf16[12288,128]{1,0:T(8,128)(2,1)S(1)} %bitcast.99), kind=kOutput, calls=%fused_computation.17 | convolution fusion | flops 402653184 | bytes 4390912 | tf_op jit(solution)/shard_map/dot_general | solution.py:50
  194.9 4.7 %convolution_convert_fusion = bf16[194,4608]{1,0:T(8,128)(2,1)} fusion(bf16[512,4608]{1,0:T(8,128)(2,1)} %param.25, bf16[2,512]{1,0:T(2,128)(2,1)S(1)} %bitcast.126, bf16[192,512]{1,0:T(8,128)(2,1)S(1)} %reshape.430), kind=kOutput, calls=%fused_computation.6 | convolution fusion | flops 916698112 | bytes 6705152 | tf_op jit(solution)/shard_map/dot_general | solution.py:220
  199.7 4.3 %reshape.435 = bf16[194,8,576]{2,1,0:T(8,128)(2,1)} reshape(bf16[194,4608]{1,0:T(8,128)(2,1)} %convolution_convert_fusion) | data formatting | bytes 3575808 | tf_op jit(solution)/shard_map/reshape | solution.py:223
  204.0 3.1 %copy.109 = bf16[194,8,576]{2,0,1:T(8,128)(2,1)} copy(bf16[194,8,576]{2,1,0:T(8,128)(2,1)} %reshape.435) | data formatting | bytes 3575808 | tf_op jit(solution)/shard_map/reshape | solution.py:223
  207.1 4.8 %all-to-all-start.1 = ((bf16[194,8,576]{2,0,1:T(8,128)(2,1)}), bf16[194,8,576]{2,0,1:T(8,128)(2,1)}, u32[]{:S(2)}, u32[]{:S(2)}) async-start(bf16[194,8,576]{2,0,1:T(8,128)(2,1)} %copy.109), calls=%async_computation.1 | async-start | bytes 4096000 | tf_op jit(solution)/shard_map/all_to_all | solution.py:225
  214.5 24.2 %all-to-all-done.1 = bf16[194,8,576]{2,0,1:T(8,128)(2,1)} async-done(((bf16[194,8,576]{2,0,1:T(8,128)(2,1)}), bf16[194,8,576]{2,0,1:T(8,128)(2,1)}, u32[]{:S(2)}, u32[]{:S(2)}) %all-to-all-start.1) | async-done | bytes 1787936 | tf_op jit(solution)/shard_map/all_to_all | solution.py:225
  240.7 17.4 %psum.7 = f32[194]{0:T(256)S(1)} all-reduce(f32[194]{0:T(256)S(1)} %multiply_reduce_fusion), channel_id=1, replica_groups=mesh['kv'=8,'blk'=32] {'kv'}, use_global_device_ids=true, to_apply=%region_17.18 | all-reduce | flops 194 | bytes 1552 | tf_op jit(solution)/shard_map/psum | solution.py:227
  (113 shorter events, 36.9 us)
Async XLA Ops:
  7.2 28.6 %copy-start.4 = (bf16[2,16,128,256]{3,2,1,0:T(8,128)(2,1)S(1)}, bf16[2,16,128,256]{3,2,1,0:T(8,128)(2,1)}, u32[]{:S(2)}) copy-start(bf16[2,16,128,256]{3,2,1,0:T(8,128)(2,1)} %param.29) | copy-start | bytes 6291460
  7.2 116.8 %all-gather.3.cloned.1.call-start = ((), (), s32[]{:S(2)}) async-start(), calls=%async_computation.2 | async-start | bytes 13516800 | tf_op jit(solution)/shard_map/all_gather | solution.py:111
  10.6 50.6 %collective-permute-start.2 = (bf16[2,192,256]{2,1,0:T(8,128)(2,1)}, bf16[2,192,256]{2,1,0:T(8,128)(2,1)S(1)}, u32[]{:S(2)}, u32[]{:S(2)}) collective-permute-start(bf16[2,192,256]{2,1,0:T(8,128)(2,1)} %param.20), channel_id=1, source_target_pairs={{0,2},{1,3},{2,4},{3,5},{4,6},{5,7},{6,8},{7,9},{8,10},{9,11},{10,... | collective-permute-start | bytes 589832 | tf_op jit(solution)/shard_map/ppermute | solution.py:23
  15.7 45.4 %collective-permute-start.1 = (bf16[2,192,256]{2,1,0:T(8,128)(2,1)}, bf16[2,192,256]{2,1,0:T(8,128)(2,1)S(1)}, u32[]{:S(2)}, u32[]{:S(2)}) collective-permute-start(bf16[2,192,256]{2,1,0:T(8,128)(2,1)} %param.20), channel_id=1, source_target_pairs={{0,3},{1,4},{2,5},{3,6},{4,7},{5,8},{6,9},{7,10},{8,11},{9,12},{10... | collective-permute-start | bytes 589832 | tf_op jit(solution)/shard_map/ppermute | solution.py:23
  21.3 38.9 %collective-permute-start = (bf16[2,192,256]{2,1,0:T(8,128)(2,1)}, bf16[2,192,256]{2,1,0:T(8,128)(2,1)}, u32[]{:S(2)}, u32[]{:S(2)}) collective-permute-start(bf16[2,192,256]{2,1,0:T(8,128)(2,1)} %param.20), channel_id=1, source_target_pairs={{0,4},{1,5},{2,6},{3,7},{4,8},{5,9},{6,10},{7,11},{8,12},{9,13},{1... | collective-permute-start | bytes 589832 | tf_op jit(solution)/shard_map/ppermute | solution.py:23
  25.0 36.8 %collective-permute-start.3 = (bf16[2,192,256]{2,1,0:T(8,128)(2,1)}, bf16[2,192,256]{2,1,0:T(8,128)(2,1)S(1)}, u32[]{:S(2)}, u32[]{:S(2)}) collective-permute-start(bf16[2,192,256]{2,1,0:T(8,128)(2,1)} %param.20), channel_id=1, source_target_pairs={{0,1},{1,2},{2,3},{3,4},{4,5},{5,6},{6,7},{7,8},{8,9},{9,10},{10,1... | collective-permute-start | bytes 589832 | tf_op jit(solution)/shard_map/ppermute | solution.py:23
  34.6 27.2 %copy-start.7 = (bf16[2,192,256]{2,1,0:T(8,128)(2,1)S(1)}, bf16[2,192,256]{2,1,0:T(8,128)(2,1)}, u32[]{:S(2)}) copy-start(bf16[2,192,256]{2,1,0:T(8,128)(2,1)} %param.20) | copy-start | bytes 589828
  125.0 7.6 %copy-start.8 = (bf16[192,1,2,128]{3,2,1,0:T(2,128)(2,1)S(1)}, bf16[192,1,2,128]{3,2,1,0:T(2,128)(2,1)}, u32[]{:S(2)}) copy-start(bf16[192,1,2,128]{3,2,1,0:T(2,128)(2,1)} %get-tuple-element.57) | copy-start | bytes 294916
  160.7 33.9 %all-to-all-start = ((f32[32,2,2,2,129]{4,1,3,2,0:T(2,128)}), f32[32,2,2,2,129]{4,1,3,2,0:T(2,128)S(1)}, u32[]{:S(2)}, u32[]{:S(2)}) async-start(f32[32,2,2,2,129]{4,1,3,2,0:T(2,128)} %copy.105), calls=%async_computation | async-start | bytes 524288 | tf_op jit(solution)/shard_map/all_to_all | solution.py:212
  177.0 3.4 %copy-start.1 = (bf16[32,1,384,128]{3,2,1,0:T(8,128)(2,1)S(1)}, bf16[32,1,384,128]{3,2,1,0:T(8,128)(2,1)}, u32[]{:S(2)}) copy-start(bf16[32,1,384,128]{3,2,1,0:T(8,128)(2,1)} %get-tuple-element.47) | copy-start | bytes 9437188
  180.4 3.1 %copy-start.3 = (bf16[384,4096]{0,1:T(8,128)(2,1)S(1)}, bf16[384,4096]{0,1:T(8,128)(2,1)}, u32[]{:S(2)}) copy-start(bf16[384,4096]{0,1:T(8,128)(2,1)} %get-tuple-element.68) | copy-start | bytes 9437188
  184.7 3.4 %copy-start = (bf16[32,1,384,128]{3,2,1,0:T(8,128)(2,1)S(1)}, bf16[32,1,384,128]{3,2,1,0:T(8,128)(2,1)}, u32[]{:S(2)}) copy-start(bf16[32,1,384,128]{3,2,1,0:T(8,128)(2,1)} %get-tuple-element.46) | copy-start | bytes 9437188
  188.1 3.1 %copy-start.2 = (bf16[384,4096]{0,1:T(8,128)(2,1)S(1)}, bf16[384,4096]{0,1:T(8,128)(2,1)}, u32[]{:S(2)}) copy-start(bf16[384,4096]{0,1:T(8,128)(2,1)} %get-tuple-element.74) | copy-start | bytes 9437188
  191.2 1.1 copy-start.5
  191.2 2.0 copy-start.11
  207.1 31.6 %all-to-all-start.1 = ((bf16[194,8,576]{2,0,1:T(8,128)(2,1)}), bf16[194,8,576]{2,0,1:T(8,128)(2,1)}, u32[]{:S(2)}, u32[]{:S(2)}) async-start(bf16[194,8,576]{2,0,1:T(8,128)(2,1)} %copy.109), calls=%async_computation.1 | async-start | bytes 4096000 | tf_op jit(solution)/shard_map/all_to_all | solution.py:225
  211.9 46.4 %copy-start.6 = (bf16[192,576]{1,0:T(8,128)(2,1)S(1)}, bf16[192,576]{1,0:T(8,128)(2,1)}, u32[]{:S(2)}) copy-start(bf16[192,576]{1,0:T(8,128)(2,1)} %param.21) | copy-start | bytes 663556
  211.9 46.4 %copy-start.9 = (f32[576]{0:T(1024)S(1)}, f32[576]{0:T(1024)}, u32[]{:S(2)}) copy-start(f32[576]{0:T(1024)} %param.26) | copy-start | bytes 6916
  211.9 46.3 %copy-start.10 = (bf16[2,576]{1,0:T(2,128)(2,1)S(1)}, bf16[2,576]{1,0:T(2,128)(2,1)}, u32[]{:S(2)}) copy-start(bf16[2,576]{1,0:T(2,128)(2,1)} %param.24) | copy-start | bytes 6916
Sparse Core Ops, SparseCore 0:
  10.7 113.2 all-gather.2

commit v4 on v3

--- a/solution.py
+++ b/solution.py
@@ -100,24 +100,34 @@
     local_pages = prefix_page_store.shape[1]
     dq_rows = decode_query_rows.shape[0]
     kv_width = kv_heads * head_dim
-    held_rows = local_pages * page_len
     dq_lines = decode_query_rows.size // kv_width
     dkv_lines = decode_key_value.size // kv_width
-    extra_lines = 16
-    extra = jnp.zeros((2, extra_lines, kv_width), jnp.bfloat16)
-    extra = extra.at[0, :dq_lines].set(decode_query_rows.reshape(dq_lines, kv_width))
-    extra = extra.at[1, :dkv_lines].set(decode_key_value.reshape(dkv_lines, kv_width))
-    packed = jnp.concatenate([prefix_page_store.reshape(2, held_rows, kv_width), extra], axis=1)
-    gathered = lax.all_gather(packed, "blk", axis=0, tiled=False)
-    all_dq = gathered[:, 0, held_rows : held_rows + dq_lines].reshape(
-        blk_size * dq_rows, q_heads * head_dim
-    )
+    dec_local = jnp.concatenate(
+        [
+            decode_query_rows.reshape(dq_lines, kv_width),
+            decode_key_value.reshape(dkv_lines, kv_width),
+        ],
+        axis=0,
+    )
+    dec_all = lax.all_to_all(
+        jnp.broadcast_to(dec_local[None], (blk_size,) + dec_local.shape), "blk", 0, 0, tiled=False
+    )
+    all_dq = dec_all[:, :dq_lines].reshape(blk_size * dq_rows, q_heads * head_dim)
     all_dkv = (
-        gathered[:, 1, held_rows : held_rows + dkv_lines]
+        dec_all[:, dq_lines:]
         .reshape(blk_size, 2, dq_rows, kv_width)
         .transpose(1, 0, 2, 3)
         .reshape(2, blk_size * dq_rows, kv_width)
     )
+
+    gathered_pages = []
+    for page in range(local_pages):
+        piece = (
+            prefix_page_store[:, page]
+            .reshape(2, page_len, kv_heads, head_dim)
+            .transpose(0, 2, 1, 3)
+        )
+        gathered_pages.append(lax.all_gather(piece, "blk", axis=0, tiled=False))
 
     look_back = 4
     pieces_back = [from_behind(suffix_key_value, "blk", d) for d in range(look_back, 0, -1)]
@@ -139,29 +149,27 @@
     pool_pages = prefix_table.shape[0]
     per_prefix = PREFIX_LENGTH // PAGE_TOKENS
     page_owner = inverse_rows(prefix_table, jnp.arange(pool_pages, dtype=jnp.int32)) // per_prefix
-    key_owner = jnp.repeat(page_owner, page_len)
+    owner_grid = page_owner.reshape(blk_size, local_pages)
     row_prefix = jnp.repeat(tok_prefix, query_group_width)
-    chunks = 3
-    chunk_keys = blk_size * held_rows // chunks
-    head_numer = []
-    head_denom = []
-    for head in range(kv_heads):
-        lanes = slice(head * head_dim, (head + 1) * head_dim)
-        head_keys = gathered[:, 0, :held_rows, lanes].reshape(blk_size * held_rows, head_dim)
-        head_values = gathered[:, 1, :held_rows, lanes].reshape(blk_size * held_rows, head_dim)
-        head_queries = own_queries[:, head].reshape(tok_rows * query_group_width, head_dim)
-        numer_h = jnp.zeros((tok_rows * query_group_width, head_dim), jnp.float32)
-        denom_h = jnp.zeros((tok_rows * query_group_width,), jnp.float32)
-        for chunk in range(chunks):
-            span = slice(chunk * chunk_keys, (chunk + 1) * chunk_keys)
-            seen = row_prefix[:, None] == key_owner[span][None, :]
-            numer_c, denom_c = attend_rows(
-                head_queries, head_keys[span], head_values[span], seen, q_scale
-            )
-            numer_h = numer_h + numer_c
-            denom_h = denom_h + denom_c
-        head_numer.append(numer_h.reshape(tok_rows, query_group_width, head_dim))
-        head_denom.append(denom_h.reshape(tok_rows, query_group_width))
+    rows_q = tok_rows * query_group_width
+    sums = [
+        (jnp.zeros((rows_q, head_dim), jnp.float32), jnp.zeros((rows_q,), jnp.float32))
+        for head in range(kv_heads)
+    ]
+    for page in range(local_pages):
+        page_block = gathered_pages[page]
+        if page > 0:
+            sums, page_block = lax.optimization_barrier((sums, page_block))
+        key_owner = jnp.repeat(owner_grid[:, page], page_len)
+        seen = row_prefix[:, None] == key_owner[None, :]
+        for head in range(kv_heads):
+            head_queries = own_queries[:, head].reshape(rows_q, head_dim)
+            head_keys = page_block[:, 0, head].reshape(blk_size * page_len, head_dim)
+            head_values = page_block[:, 1, head].reshape(blk_size * page_len, head_dim)
+            numer_c, denom_c = attend_rows(head_queries, head_keys, head_values, seen, q_scale)
+            sums[head] = (sums[head][0] + numer_c, sums[head][1] + denom_c)
+    head_numer = [numer.reshape(tok_rows, query_group_width, head_dim) for numer, _ in sums]
+    head_denom = [denom.reshape(tok_rows, query_group_width) for _, denom in sums]
     pre_numer = jnp.stack(head_numer, axis=1)
     pre_denom = jnp.stack(head_denom, axis=1)
     suffix_attn = ((own_numer + pre_numer) / (own_denom + pre_denom)[..., None]).astype(
@@ -224,7 +232,11 @@
     mine = jnp.sum(
         lax.all_to_all(shares, "kv", 1, 1, tiled=False).astype(jnp.float32), axis=1
     )
-    mean_square = lax.psum(jnp.sum(mine * mine, axis=1), "kv") / D
+    squares = jnp.sum(mine * mine, axis=1)
+    square_parts = lax.all_to_all(
+        jnp.broadcast_to(squares[None], (kv_size,) + squares.shape), "kv", 0, 0, tiled=False
+    )
+    mean_square = jnp.sum(square_parts, axis=0) / D
     normed = mine * lax.rsqrt(mean_square + norm_eps)[:, None] * post_gain[None, :]
     hidden = (residual + normed).astype(jnp.bfloat16)
     return (hidden[:tok_rows], hidden[tok_rows:], new_cache)

time: 267 us -> 294 us (1.10)
  local copies, waits for them, and re-layouts: 32.2 us -> 46.2 us
  blocking collectives: 17.4 us -> 30.9 us
  matrix products: 47.5 us -> 40.4 us
  waiting for transfers between devices: 105 us -> 108 us
    all_gather x1 -> x3, waiting for transfers between devices: 58.2 us -> 97.9 us  [body(): gathered_pages.append(lax.all_gather(piece, 'blk', axis=0, tiled=False))]
    all_to_all x0 -> x1, blocking collectives: none -> 30.9 us  [body(): lax.all_to_all(shares, 'kv', 1, 1, tiled=False).astype(jnp.float32)]
    ppermute x4, waiting for transfers between devices: 22.7 us -> 0.01 us  [from_behind(): return lax.ppermute(block, axis, route)]
    all_to_all x1 -> x2, waiting for transfers between devices: 24.2 us -> 3.52 us  [the longest x1 3.52 us: body(): lax.all_to_all(jnp.broadcast_to(squares[None], (kv_size,) + squares.shape...]
    psum x1 -> x0, blocking collectives: 17.4 us -> none  [body(): mean_square = lax.psum(jnp.sum(mine * mine, axis=1), 'kv') / D]
    all_to_all x1 -> x2, starting transfers between devices: 4.79 us -> 12.9 us  [the longest x1 9.52 us: body(): lax.all_to_all(jnp.broadcast_to(dec_local[None], (blk_size,) + dec_local....]
    all_to_all x1, waiting for transfers between devices: 0.01 us -> 7.02 us  [body(): lax.all_to_all(slot_sums, 'blk', 0, 0, tiled=False)]
    dot_general x6, matrix products: 14.9 us -> 8.35 us  [attend_rows(): jnp.dot(weights.astype(jnp.bfloat16), value_rows, preferred_element_type=...]
  transfers between devices with their start and end apart: 7 -> 10, of which waited for: 4 -> 4; matrix products, arithmetic and copies ran while one was open for 13% -> 20% of each run, Pallas kernels for 0% -> 0%
where the time goes in v4:
time: 294 us; the launch traced here: 293 us
  waiting for transfers between devices  108 us (37%)
  local copies, waits for them, and re-layouts  46.2 us (16%)
  starting transfers between devices  40.6 us (14%)
  matrix products  40.4 us (14%)
  blocking collectives  30.9 us (11%)
  between operations  14.5 us (5%)
  other arithmetic  11.6 us (4%)
    all_gather x3, waiting for transfers between devices, body(): gathered_pages.append(lax.all_gather(piece, 'blk', axis=0, tiled=False))  97.9 us
    all_to_all x1, blocking collectives, body(): lax.all_to_all(shares, 'kv', 1, 1, tiled=False).astype(jnp.float32)  30.9 us
    dot_general x6, matrix products, attend_rows(): jnp.dot(query_rows, key_rows.T, preferred_element_type=jnp.float32)  18.7 us
    ppermute x4, starting transfers between devices, from_behind(): return lax.ppermute(block, axis, route)  17.7 us
    all_to_all x1, starting transfers between devices, body(): lax.all_to_all(slot_sums, 'blk', 0, 0, tiled=False)  9.9 us
    slice x3, local copies, waits for them, and re-layouts, body(): head_keys = page_block[:, 0, head].reshape(blk_size * page_len, head_dim)  9.65 us
    all_to_all x1, starting transfers between devices, body(): lax.all_to_all(jnp.broadcast_to(dec_local[None], (blk_size,) + dec_local....  9.52 us
    dot_general x6, matrix products, attend_rows(): jnp.dot(weights.astype(jnp.bfloat16), value_rows, preferred_element_type=...  8.35 us
  transfers between devices with their start and end apart: 10, of which 4 were waited for; matrix products, arithmetic and copies ran while one was open for 20% of the time, Pallas kernels for 0%

profile of v4, /device:TPU:2, one launch (start us, length us, event | category | flops | bytes accessed | tf_op | source)
XLA Modules:
  0.0 292.7 jit_solution(5225809413626750952)
XLA Ops:
  10.3 9.2 %collective-permute-start = (bf16[2,192,256]{2,1,0:T(8,128)(2,1)}, bf16[2,192,256]{2,1,0:T(8,128)(2,1)}, u32[]{:S(2)}, u32[]{:S(2)}) collective-permute-start(bf16[2,192,256]{2,1,0:T(8,128)(2,1)} %param.16), channel_id=1, source_target_pairs={{0,4},{1,5},{2,6},{3,7},{4,8},{5,9},{6,10},{7,11},{8,12},{9,13},{1... | collective-permute-start | bytes 589832 | tf_op jit(solution)/shard_map/ppermute | solution.py:23
  19.5 2.5 collective-permute-start.1
  22.1 2.8 collective-permute-start.2
  24.9 3.2 %collective-permute-start.3 = (bf16[2,192,256]{2,1,0:T(8,128)(2,1)}, bf16[2,192,256]{2,1,0:T(8,128)(2,1)S(1)}, u32[]{:S(2)}, u32[]{:S(2)}) collective-permute-start(bf16[2,192,256]{2,1,0:T(8,128)(2,1)} %param.16), channel_id=1, source_target_pairs={{0,1},{1,2},{2,3},{3,4},{4,5},{5,6},{6,7},{7,8},{8,9},{9,10},{10,1... | collective-permute-start | bytes 589832 | tf_op jit(solution)/shard_map/ppermute | solution.py:23
  30.1 9.5 %all-to-all-start = ((bf16[32,8,256]{2,1,0:T(8,128)(2,1)}), bf16[32,8,256]{2,1,0:T(8,128)(2,1)S(1)}, u32[]{:S(2)}, u32[]{:S(2)}) async-start(bf16[32,8,256]{2,1,0:T(8,128)(2,1)} %broadcast_in_dim.71), calls=%async_computation | async-start | bytes 262144 | tf_op jit(solution)/shard_map/all_to_all | solution.py:112
  67.3 9.9 %all-to-all-start.1 = ((f32[32,2,2,2,129]{4,1,3,2,0:T(2,128)}), f32[32,2,2,2,129]{4,1,3,2,0:T(2,128)S(1)}, u32[]{:S(2)}, u32[]{:S(2)}) async-start(f32[32,2,2,2,129]{4,1,3,2,0:T(2,128)} %copy.180), calls=%async_computation.1 | async-start | bytes 524288 | tf_op jit(solution)/shard_map/all_to_all | solution.py:220
  77.2 4.4 %fusion.12 = (f32[192,2,2]{0,2,1:T(2,128)}, f32[2,960,192,2]{1,2,3,0:T(8,128)}) fusion(pred[192,960]{1,0:T(8,128)(4,1)S(1)} %compare_and_fusion, bf16[192,2,2,128]{3,2,1,0:T(2,128)(2,1)S(1)} %reshape.309, bf16[960,2,128,1]{2,1,0,3:T(2,128)(2,1)} %bitcast.145), kind=kOutput, calls=%fused_computation.21 | convolution fusion | flops 191692032 | bytes 3824640 | tf_op jit(solution)/shard_map/qhgd,khd->qhgk/dot_general | solution.py:28
  81.6 7.0 %all-to-all-done.1 = f32[32,2,2,2,129]{4,1,3,2,0:T(2,128)S(1)} async-done(((f32[32,2,2,2,129]{4,1,3,2,0:T(2,128)}), f32[32,2,2,2,129]{4,1,3,2,0:T(2,128)S(1)}, u32[]{:S(2)}, u32[]{:S(2)}) %all-to-all-start.1) | async-done | bytes 132128 | tf_op jit(solution)/shard_map/all_to_all | solution.py:220
  89.5 2.8 fusion.73
  92.4 2.5 fusion.79
  95.9 2.5 fusion.80
  99.4 47.9 %all-gather.9.cloned.1.call-done = bf16[64,2,128,128]{3,2,1,0:T(8,128)(2,1)} async-done(((bf16[2,2,128,128]{3,2,1,0:T(8,128)(2,1)}), bf16[64,2,128,128]{3,2,1,0:T(8,128)(2,1)}) %all-gather.9.cloned.1.call-update) | async-done | bytes 4194320 | tf_op jit(solution)/shard_map/all_gather | solution.py:130
  147.3 2.8 fusion.72
  158.4 50.0 %all-gather.11.cloned.1.call-done = bf16[64,2,128,128]{3,2,1,0:T(8,128)(2,1)} async-done(((bf16[2,2,128,128]{3,2,1,0:T(8,128)(2,1)}), bf16[64,2,128,128]{3,2,1,0:T(8,128)(2,1)}) %all-gather.11.cloned.1.call-update) | async-done | bytes 4194320 | tf_op jit(solution)/shard_map/all_gather | solution.py:130
  208.4 4.1 %fusion.71 = (bf16[32,1,1,128,128]{4,3,2,1,0:T(8,128)(2,1)S(1)}, bf16[32,1,1,128,128]{4,3,2,1,0:T(8,128)(2,1)S(1)}, bf16[32,1,1,128,128]{4,3,2,1,0:T(8,128)(2,1)}, bf16[32,1,1,128,128]{4,3,2,1,0:T(8,128)(2,1)}) fusion(bf16[32,2,2,128,128]{4,3,2,1,0:T(8,128)(2,1)} %bitcast.123), kind=kLoop, calls=%fused_computation.111 | loop fusion | bytes 8388608 | tf_op jit(solution)/shard_map/slice | solution.py:167
  212.5 3.6 %fusion.85 = (f32[384]{0:T(512)S(1)}, bf16[384,4096]{1,0:T(8,128)(2,1)}) fusion(bf16[4096,128]{1,0:T(8,128)(2,1)S(1)} %bitcast.136, bf16[384,128]{1,0:T(8,128)(2,1)S(1)} %bitcast.152, s32[4096]{0:T(1024)S(1)} %copy-done.11, s32[384]{0:T(512)S(1)} %copy-done.22), kind=kOutput, calls=%fused_computation.125 | convolution fusion | flops 412089984 | bytes 4312064 | tf_op jit(solution)/shard_map/dot_general | solution.py:45
  219.7 5.1 %fusion.84 = (f32[384]{0:T(512)S(1)}, bf16[384,4096]{1,0:T(8,128)(2,1)}) fusion(bf16[4096,128]{1,0:T(8,128)(2,1)} %bitcast.133, bf16[384,128]{1,0:T(8,128)(2,1)} %bitcast.147, s32[4096]{0:T(1024)S(1)} %copy-done.11, s32[384]{0:T(512)} %eq.107), kind=kOutput, calls=%fused_computation.124 | convolution fusion | flops 412089984 | bytes 4312064 | tf_op jit(solution)/shard_map/dot_general | solution.py:45
  226.6 3.3 %fusion.29 = f32[384,128]{1,0:T(8,128)S(1)} fusion(f32[384,128]{1,0:T(8,128)S(1)} %fusion.23, bf16[4096,128]{1,0:T(8,128)(2,1)} %bitcast.128, bf16[384,4096]{1,0:T(8,128)(2,1)} %get-tuple-element.86), kind=kOutput, calls=%fused_computation.30 | convolution fusion | flops 402702336 | bytes 4587520 | tf_op jit(solution)/shard_map/dot_general | solution.py:50
  232.4 4.7 %convolution_convert_fusion = bf16[194,4608]{1,0:T(8,128)(2,1)} fusion(bf16[512,4608]{1,0:T(8,128)(2,1)} %param.21, bf16[2,512]{1,0:T(2,128)(2,1)S(1)} %bitcast.155, bf16[192,512]{1,0:T(8,128)(2,1)S(1)} %reshape.310), kind=kOutput, calls=%fused_computation.6 | convolution fusion | flops 916698112 | bytes 6705152 | tf_op jit(solution)/shard_map/dot_general | solution.py:228
  237.2 4.3 %reshape.319 = bf16[194,8,576]{2,1,0:T(8,128)(2,1)} reshape(bf16[194,4608]{1,0:T(8,128)(2,1)} %convolution_convert_fusion) | data formatting | bytes 3575808 | tf_op jit(solution)/shard_map/reshape | solution.py:231
  243.3 30.9 %all_to_all.21 = bf16[194,8,576]{2,0,1:T(8,128)(2,1)S(1)} all-to-all(bf16[194,8,576]{2,0,1:T(8,128)(2,1)S(1)} %copy.184), channel_id=1, replica_groups=mesh['kv'=8,'blk'=32] {'kv'}, dimensions={1} | all-to-all | bytes 3575808 | tf_op jit(solution)/shard_map/all_to_all | solution.py:233
  275.2 3.3 %all-to-all-start.3 = ((f32[8,1,194]{2,1,0:T(1,128)}), f32[8,1,194]{2,1,0:T(1,128)S(1)}, u32[]{:S(2)}, u32[]{:S(2)}) async-start(f32[8,1,194]{2,1,0:T(1,128)} %broadcast_in_dim.121), calls=%async_computation.3 | async-start | bytes 16384 | tf_op jit(solution)/shard_map/all_to_all | solution.py:236
  278.6 2.6 copy.186
  281.2 3.5 %all-to-all-done.3 = f32[8,1,194]{2,1,0:T(1,128)S(1)} async-done(((f32[8,1,194]{2,1,0:T(1,128)}), f32[8,1,194]{2,1,0:T(1,128)S(1)}, u32[]{:S(2)}, u32[]{:S(2)}) %all-to-all-start.3) | async-done | bytes 6240 | tf_op jit(solution)/shard_map/all_to_all | solution.py:236
  (165 shorter events, 55.7 us)
Async XLA Ops:
  7.2 43.8 %copy-start.1 = (bf16[2,16,128,256]{3,2,1,0:T(8,128)(2,1)S(1)}, bf16[2,16,128,256]{3,2,1,0:T(8,128)(2,1)}, u32[]{:S(2)}) copy-start(bf16[2,16,128,256]{3,2,1,0:T(8,128)(2,1)} %param.25) | copy-start | bytes 6291460
  7.2 82.4 %all-gather.7.cloned.1.call-start = ((), (), s32[]{:S(2)}) async-start(), calls=%async_computation.4 | async-start | bytes 4325376 | tf_op jit(solution)/shard_map/all_gather | solution.py:130
  9.3 138.0 %all-gather.9.cloned.1.call-start = ((), (), s32[]{:S(2)}) async-start(), calls=%async_computation.5 | async-start | bytes 4325376 | tf_op jit(solution)/shard_map/all_gather | solution.py:130
  10.3 45.0 %copy-start.4 = (bf16[2,192,256]{2,1,0:T(8,128)(2,1)S(1)}, bf16[2,192,256]{2,1,0:T(8,128)(2,1)}, u32[]{:S(2)}) copy-start(bf16[2,192,256]{2,1,0:T(8,128)(2,1)} %param.16) | copy-start | bytes 589828
  10.3 43.0 %collective-permute-start = (bf16[2,192,256]{2,1,0:T(8,128)(2,1)}, bf16[2,192,256]{2,1,0:T(8,128)(2,1)}, u32[]{:S(2)}, u32[]{:S(2)}) collective-permute-start(bf16[2,192,256]{2,1,0:T(8,128)(2,1)} %param.16), channel_id=1, source_target_pairs={{0,4},{1,5},{2,6},{3,7},{4,8},{5,9},{6,10},{7,11},{8,12},{9,13},{1... | collective-permute-start | bytes 589832 | tf_op jit(solution)/shard_map/ppermute | solution.py:23
  19.5 34.7 %collective-permute-start.1 = (bf16[2,192,256]{2,1,0:T(8,128)(2,1)}, bf16[2,192,256]{2,1,0:T(8,128)(2,1)}, u32[]{:S(2)}, u32[]{:S(2)}) collective-permute-start(bf16[2,192,256]{2,1,0:T(8,128)(2,1)} %param.16), channel_id=1, source_target_pairs={{0,3},{1,4},{2,5},{3,6},{4,7},{5,8},{6,9},{7,10},{8,11},{9,12},{10... | collective-permute-start | bytes 589832 | tf_op jit(solution)/shard_map/ppermute | solution.py:23
  22.1 33.1 %collective-permute-start.2 = (bf16[2,192,256]{2,1,0:T(8,128)(2,1)}, bf16[2,192,256]{2,1,0:T(8,128)(2,1)S(1)}, u32[]{:S(2)}, u32[]{:S(2)}) collective-permute-start(bf16[2,192,256]{2,1,0:T(8,128)(2,1)} %param.16), channel_id=1, source_target_pairs={{0,2},{1,3},{2,4},{3,5},{4,6},{5,7},{6,8},{7,9},{8,10},{9,11},{10,... | collective-permute-start | bytes 589832 | tf_op jit(solution)/shard_map/ppermute | solution.py:23
  24.9 30.4 %collective-permute-start.3 = (bf16[2,192,256]{2,1,0:T(8,128)(2,1)}, bf16[2,192,256]{2,1,0:T(8,128)(2,1)S(1)}, u32[]{:S(2)}, u32[]{:S(2)}) collective-permute-start(bf16[2,192,256]{2,1,0:T(8,128)(2,1)} %param.16), channel_id=1, source_target_pairs={{0,1},{1,2},{2,3},{3,4},{4,5},{5,6},{6,7},{7,8},{8,9},{9,10},{10,1... | collective-permute-start | bytes 589832 | tf_op jit(solution)/shard_map/ppermute | solution.py:23
  30.1 27.1 %all-to-all-start = ((bf16[32,8,256]{2,1,0:T(8,128)(2,1)}), bf16[32,8,256]{2,1,0:T(8,128)(2,1)S(1)}, u32[]{:S(2)}, u32[]{:S(2)}) async-start(bf16[32,8,256]{2,1,0:T(8,128)(2,1)} %broadcast_in_dim.71), calls=%async_computation | async-start | bytes 262144 | tf_op jit(solution)/shard_map/all_to_all | solution.py:112
  39.7 168.7 %all-gather.11.cloned.1.call-start = ((), (), s32[]{:S(2)}) async-start(), calls=%async_computation.6 | async-start | bytes 4325376 | tf_op jit(solution)/shard_map/all_gather | solution.py:130
  46.1 12.2 %copy-start.24 = (s32[16]{0:T(128)}, s32[16]{0:T(128)S(1)}, u32[]{:S(2)}) copy-start(s32[16]{0:T(128)S(1)} %and_select_fusion.3) | copy-start | bytes 196
  49.2 27.9 %copy-start.5 = (pred[192,960]{1,0:T(8,128)(4,1)}, pred[192,960]{1,0:T(8,128)(4,1)S(1)}, u32[]{:S(2)}) copy-start(pred[192,960]{1,0:T(8,128)(4,1)S(1)} %compare_and_fusion) | copy-start | bytes 552964
  67.3 21.4 %all-to-all-start.1 = ((f32[32,2,2,2,129]{4,1,3,2,0:T(2,128)}), f32[32,2,2,2,129]{4,1,3,2,0:T(2,128)S(1)}, u32[]{:S(2)}, u32[]{:S(2)}) async-start(f32[32,2,2,2,129]{4,1,3,2,0:T(2,128)} %copy.180), calls=%async_computation.1 | async-start | bytes 524288 | tf_op jit(solution)/shard_map/all_to_all | solution.py:220
  208.4 4.1 %copy-start.22 = (s32[384]{0:T(512)S(1)}, s32[384]{0:T(512)}, u32[]{:S(2)}) copy-start(s32[384]{0:T(512)} %eq.107) | copy-start | bytes 4612
  219.7 5.2 %copy-start.15 = (f32[384]{0:T(512)S(1)}, f32[384]{0:T(512)}, u32[]{:S(2)}) copy-start(f32[384]{0:T(512)} %add.137) | copy-start | bytes 4612
  226.6 4.4 %copy-start.17 = (f32[192,1,2]{0,2,1:T(2,128)S(1)}, f32[192,1,2]{0,2,1:T(2,128)}, u32[]{:S(2)}) copy-start(f32[192,1,2]{0,2,1:T(2,128)} %copy.169) | copy-start | bytes 4612
  226.6 4.4 %copy-start.19 = (f32[192,2,2]{0,2,1:T(2,128)S(1)}, f32[192,2,2]{0,2,1:T(2,128)}, u32[]{:S(2)}) copy-start(f32[192,2,2]{0,2,1:T(2,128)} %get-tuple-element.81) | copy-start | bytes 9220
  226.6 4.4 %copy-start.2 = (bf16[960,2,128]{2,1,0:T(2,128)(2,1)S(1)}, bf16[960,2,128]{2,1,0:T(2,128)(2,1)}, u32[]{:S(2)}) copy-start(bf16[960,2,128]{2,1,0:T(2,128)(2,1)} %reshape_squeeze.67) | copy-start | bytes 1474564
  226.6 4.4 %copy-start.6 = (pred[192,960]{1,0:T(8,128)(4,1)S(1)}, pred[192,960]{1,0:T(8,128)(4,1)}, u32[]{:S(2)}) copy-start(pred[192,960]{1,0:T(8,128)(4,1)} %copy-done.5) | copy-start | bytes 552964
  226.6 4.4 %copy-start.25 = (f32[2,960,192,2]{1,2,3,0:T(8,128)S(1)}, f32[2,960,192,2]{1,2,3,0:T(8,128)}, u32[]{:S(2)}) copy-start(f32[2,960,192,2]{1,2,3,0:T(8,128)} %get-tuple-element.82) | copy-start | bytes 8847364
  274.2 10.6 %copy-start.3 = (bf16[192,576]{1,0:T(8,128)(2,1)S(1)}, bf16[192,576]{1,0:T(8,128)(2,1)}, u32[]{:S(2)}) copy-start(bf16[192,576]{1,0:T(8,128)(2,1)} %param.17) | copy-start | bytes 663556
  274.2 10.6 %copy-start.18 = (f32[576]{0:T(1024)S(1)}, f32[576]{0:T(1024)}, u32[]{:S(2)}) copy-start(f32[576]{0:T(1024)} %param.22) | copy-start | bytes 6916
  274.2 10.6 %copy-start.20 = (bf16[2,576]{1,0:T(2,128)(2,1)S(1)}, bf16[2,576]{1,0:T(2,128)(2,1)}, u32[]{:S(2)}) copy-start(bf16[2,576]{1,0:T(2,128)(2,1)} %param.20) | copy-start | bytes 6916
  275.2 9.5 %all-to-all-start.3 = ((f32[8,1,194]{2,1,0:T(1,128)}), f32[8,1,194]{2,1,0:T(1,128)S(1)}, u32[]{:S(2)}, u32[]{:S(2)}) async-start(f32[8,1,194]{2,1,0:T(1,128)} %broadcast_in_dim.121), calls=%async_computation.3 | async-start | bytes 16384 | tf_op jit(solution)/shard_map/all_to_all | solution.py:236
  (12 other events, 34.2 us)
Sparse Core Ops, SparseCore 0:
  10.5 75.2 all-gather.6
  88.4 58.9 all-gather.8
  149.9 58.4 all-gather.10

commit v5 on v4

--- a/solution.py
+++ b/solution.py
@@ -120,14 +120,9 @@
         .reshape(2, blk_size * dq_rows, kv_width)
     )
 
-    gathered_pages = []
-    for page in range(local_pages):
-        piece = (
-            prefix_page_store[:, page]
-            .reshape(2, page_len, kv_heads, head_dim)
-            .transpose(0, 2, 1, 3)
-        )
-        gathered_pages.append(lax.all_gather(piece, "blk", axis=0, tiled=False))
+    held_rows = local_pages * page_len
+    piece = prefix_page_store.reshape(2, held_rows, kv_heads, head_dim).transpose(0, 2, 1, 3)
+    gathered = lax.all_gather(piece, "blk", axis=0, tiled=False)
 
     look_back = 4
     pieces_back = [from_behind(suffix_key_value, "blk", d) for d in range(look_back, 0, -1)]
@@ -149,25 +144,27 @@
     pool_pages = prefix_table.shape[0]
     per_prefix = PREFIX_LENGTH // PAGE_TOKENS
     page_owner = inverse_rows(prefix_table, jnp.arange(pool_pages, dtype=jnp.int32)) // per_prefix
-    owner_grid = page_owner.reshape(blk_size, local_pages)
+    key_owner = jnp.repeat(page_owner, page_len)
     row_prefix = jnp.repeat(tok_prefix, query_group_width)
     rows_q = tok_rows * query_group_width
-    sums = [
-        (jnp.zeros((rows_q, head_dim), jnp.float32), jnp.zeros((rows_q,), jnp.float32))
-        for head in range(kv_heads)
-    ]
-    for page in range(local_pages):
-        page_block = gathered_pages[page]
-        if page > 0:
-            sums, page_block = lax.optimization_barrier((sums, page_block))
-        key_owner = jnp.repeat(owner_grid[:, page], page_len)
-        seen = row_prefix[:, None] == key_owner[None, :]
-        for head in range(kv_heads):
-            head_queries = own_queries[:, head].reshape(rows_q, head_dim)
-            head_keys = page_block[:, 0, head].reshape(blk_size * page_len, head_dim)
-            head_values = page_block[:, 1, head].reshape(blk_size * page_len, head_dim)
-            numer_c, denom_c = attend_rows(head_queries, head_keys, head_values, seen, q_scale)
-            sums[head] = (sums[head][0] + numer_c, sums[head][1] + denom_c)
+    chunks = 3
+    chunk_keys = blk_size * held_rows // chunks
+    sums = []
+    for head in range(kv_heads):
+        head_queries = own_queries[:, head].reshape(rows_q, head_dim)
+        head_keys = gathered[:, 0, head].reshape(blk_size * held_rows, head_dim)
+        head_values = gathered[:, 1, head].reshape(blk_size * held_rows, head_dim)
+        numer_h = jnp.zeros((rows_q, head_dim), jnp.float32)
+        denom_h = jnp.zeros((rows_q,), jnp.float32)
+        for chunk in range(chunks):
+            span = slice(chunk * chunk_keys, (chunk + 1) * chunk_keys)
+            seen = row_prefix[:, None] == key_owner[span][None, :]
+            numer_c, denom_c = attend_rows(
+                head_queries, head_keys[span], head_values[span], seen, q_scale
+            )
+            numer_h = numer_h + numer_c
+            denom_h = denom_h + denom_c
+        sums.append((numer_h, denom_h))
     head_numer = [numer.reshape(tok_rows, query_group_width, head_dim) for numer, _ in sums]
     head_denom = [denom.reshape(tok_rows, query_group_width) for _, denom in sums]
     pre_numer = jnp.stack(head_numer, axis=1)
@@ -225,13 +222,15 @@
     decode_attn = decode_attn.reshape(decode_rows, q_heads * head_dim)
 
     attention = jnp.concatenate([suffix_attn, decode_attn], axis=0)
-    projected = jnp.dot(attention, out_weight, preferred_element_type=jnp.float32)
+    kv_size = lax.axis_size("kv")
+    projected_t = jnp.einsum(
+        "ko,rk->or", out_weight, attention, preferred_element_type=jnp.float32
+    )
     residual = jnp.concatenate([suffix_resid, decode_resid], axis=0).astype(jnp.float32)
-    kv_size = lax.axis_size("kv")
-    shares = projected.astype(jnp.bfloat16).reshape(projected.shape[0], kv_size, -1)
+    shares = projected_t.astype(jnp.bfloat16).reshape(kv_size, -1, projected_t.shape[1])
     mine = jnp.sum(
-        lax.all_to_all(shares, "kv", 1, 1, tiled=False).astype(jnp.float32), axis=1
-    )
+        lax.all_to_all(shares, "kv", 0, 0, tiled=False).astype(jnp.float32), axis=0
+    ).T
     squares = jnp.sum(mine * mine, axis=1)
     square_parts = lax.all_to_all(
         jnp.broadcast_to(squares[None], (kv_size,) + squares.shape), "kv", 0, 0, tiled=False

time: 294 us -> 246 us (0.84)
  waiting for transfers between devices: 108 us -> 61 us
  matrix products: 40.4 us -> 49 us
  local copies, waits for them, and re-layouts: 46.2 us -> 38.2 us
  blocking collectives: 30.9 us -> 33.9 us
    all_gather x3 -> x1, waiting for transfers between devices: 97.9 us -> 32.6 us  [body(): gathered = lax.all_gather(piece, 'blk', axis=0, tiled=False)]
    ppermute x4, waiting for transfers between devices: 0.01 us -> 9.94 us  [from_behind(): return lax.ppermute(block, axis, route)]
    all_to_all x1, waiting for transfers between devices: 7.02 us -> 14 us  [body(): lax.all_to_all(slot_sums, 'blk', 0, 0, tiled=False)]
    dot_general x6, matrix products: 8.35 us -> 14.6 us  [attend_rows(): jnp.dot(weights.astype(jnp.bfloat16), value_rows, preferred_element_type=...]
    another operation x5 -> x1, local copies, waits for them, and re-layouts: 5.49 us -> 0.74 us  [the longest x4 4.76 us: body(): pre_denom = jnp.stack(head_denom, axis=1)]
    slice x5 -> x2, local copies, waits for them, and re-layouts: 11.1 us -> 7.64 us  [the longest x1 7.57 us: body(): head_values = gathered[:, 1, head].reshape(blk_size * held_rows, head_dim)]
    all_to_all x1, blocking collectives: 30.9 us -> 33.9 us  [body(): lax.all_to_all(shares, 'kv', 0, 0, tiled=False).astype(jnp.float32)]
    reshape x2 -> x3, local copies, waits for them, and re-layouts: 6.1 us -> 7.33 us  [the longest x2 6.1 us: body(): projected_t.astype(jnp.bfloat16).reshape(kv_size, -1, projected_t.shape[1])]
  transfers between devices with their start and end apart: 10 -> 8, of which waited for: 4 -> 6; matrix products, arithmetic and copies ran while one was open for 20% -> 14% of each run, Pallas kernels for 0% -> 0%
where the time goes in v5:
time: 246 us; the launch traced here: 245 us
  waiting for transfers between devices  61 us (25%)
  matrix products  49 us (20%)
  starting transfers between devices  39.6 us (16%)
  local copies, waits for them, and re-layouts  38.2 us (16%)
  blocking collectives  33.9 us (14%)
  between operations  14.6 us (6%)
  other arithmetic  9.19 us (4%)
    all_to_all x1, blocking collectives, body(): lax.all_to_all(shares, 'kv', 0, 0, tiled=False).astype(jnp.float32)  33.9 us
    all_gather x1, waiting for transfers between devices, body(): gathered = lax.all_gather(piece, 'blk', axis=0, tiled=False)  32.6 us
    dot_general x6, matrix products, attend_rows(): jnp.dot(query_rows, key_rows.T, preferred_element_type=jnp.float32)  21.5 us
    ppermute x4, starting transfers between devices, from_behind(): return lax.ppermute(block, axis, route)  17.6 us
    dot_general x6, matrix products, attend_rows(): jnp.dot(weights.astype(jnp.bfloat16), value_rows, preferred_element_type=...  14.6 us
    all_to_all x1, waiting for transfers between devices, body(): lax.all_to_all(slot_sums, 'blk', 0, 0, tiled=False)  14 us
    ppermute x4, waiting for transfers between devices, from_behind(): return lax.ppermute(block, axis, route)  9.94 us
    all_to_all x1, starting transfers between devices, body(): lax.all_to_all(jnp.broadcast_to(dec_local[None], (blk_size,) + dec_local....  9.52 us
  transfers between devices with their start and end apart: 8, of which 6 were waited for; matrix products, arithmetic and copies ran while one was open for 14% of the time, Pallas kernels for 0%

profile of v5, /device:TPU:2, one launch (start us, length us, event | category | flops | bytes accessed | tf_op | source)
XLA Modules:
  0.0 245.4 jit_solution(9762800242206504811)
XLA Ops:
  9.3 5.2 %collective-permute-start.2 = (bf16[2,192,256]{2,1,0:T(8,128)(2,1)}, bf16[2,192,256]{2,1,0:T(8,128)(2,1)S(1)}, u32[]{:S(2)}, u32[]{:S(2)}) collective-permute-start(bf16[2,192,256]{2,1,0:T(8,128)(2,1)} %param.16), channel_id=1, source_target_pairs={{0,2},{1,3},{2,4},{3,5},{4,6},{5,7},{6,8},{7,9},{8,10},{9,11},{10,... | collective-permute-start | bytes 589832 | tf_op jit(solution)/shard_map/ppermute | solution.py:23
  14.5 5.6 %collective-permute-start.1 = (bf16[2,192,256]{2,1,0:T(8,128)(2,1)}, bf16[2,192,256]{2,1,0:T(8,128)(2,1)S(1)}, u32[]{:S(2)}, u32[]{:S(2)}) collective-permute-start(bf16[2,192,256]{2,1,0:T(8,128)(2,1)} %param.16), channel_id=1, source_target_pairs={{0,3},{1,4},{2,5},{3,6},{4,7},{5,8},{6,9},{7,10},{8,11},{9,12},{10... | collective-permute-start | bytes 589832 | tf_op jit(solution)/shard_map/ppermute | solution.py:23
  20.0 3.7 %collective-permute-start = (bf16[2,192,256]{2,1,0:T(8,128)(2,1)}, bf16[2,192,256]{2,1,0:T(8,128)(2,1)}, u32[]{:S(2)}, u32[]{:S(2)}) collective-permute-start(bf16[2,192,256]{2,1,0:T(8,128)(2,1)} %param.16), channel_id=1, source_target_pairs={{0,4},{1,5},{2,6},{3,7},{4,8},{5,9},{6,10},{7,11},{8,12},{9,13},{1... | collective-permute-start | bytes 589832 | tf_op jit(solution)/shard_map/ppermute | solution.py:23
  23.7 3.2 %collective-permute-start.3 = (bf16[2,192,256]{2,1,0:T(8,128)(2,1)}, bf16[2,192,256]{2,1,0:T(8,128)(2,1)S(1)}, u32[]{:S(2)}, u32[]{:S(2)}) collective-permute-start(bf16[2,192,256]{2,1,0:T(8,128)(2,1)} %param.16), channel_id=1, source_target_pairs={{0,1},{1,2},{2,3},{3,4},{4,5},{5,6},{6,7},{7,8},{8,9},{9,10},{10,1... | collective-permute-start | bytes 589832 | tf_op jit(solution)/shard_map/ppermute | solution.py:23
  29.0 9.5 %all-to-all-start = ((bf16[32,8,256]{2,1,0:T(8,128)(2,1)}), bf16[32,8,256]{2,1,0:T(8,128)(2,1)S(1)}, u32[]{:S(2)}, u32[]{:S(2)}) async-start(bf16[32,8,256]{2,1,0:T(8,128)(2,1)} %broadcast_in_dim.67), calls=%async_computation | async-start | bytes 262144 | tf_op jit(solution)/shard_map/all_to_all | solution.py:112
  50.8 7.9 %collective-permute-done = bf16[2,192,256]{2,1,0:T(8,128)(2,1)} collective-permute-done((bf16[2,192,256]{2,1,0:T(8,128)(2,1)}, bf16[2,192,256]{2,1,0:T(8,128)(2,1)}, u32[]{:S(2)}, u32[]{:S(2)}) %collective-permute-start) | collective-permute-done | bytes 196640 | tf_op jit(solution)/shard_map/ppermute | solution.py:23
  75.0 9.1 %all-to-all-start.1 = ((f32[32,2,2,2,129]{4,1,3,2,0:T(2,128)}), f32[32,2,2,2,129]{4,1,3,2,0:T(2,128)S(1)}, u32[]{:S(2)}, u32[]{:S(2)}) async-start(f32[32,2,2,2,129]{4,1,3,2,0:T(2,128)} %copy.132), calls=%async_computation.1 | async-start | bytes 524288 | tf_op jit(solution)/shard_map/all_to_all | solution.py:217
  84.1 3.9 %fusion.13 = (f32[192,2,2]{0,2,1:T(2,128)S(1)}, f32[2,960,192,2]{1,2,3,0:T(8,128)}) fusion(pred[192,960]{1,0:T(8,128)(4,1)S(1)} %compare_and_fusion, bf16[192,2,2,128]{3,2,1,0:T(2,128)(2,1)S(1)} %reshape.371, bf16[960,2,128,1]{2,1,0,3:T(2,128)(2,1)} %bitcast.113), kind=kOutput, calls=%fused_computation.22 | convolution fusion | flops 191692032 | bytes 3824640 | tf_op jit(solution)/shard_map/qhgd,khd->qhgk/dot_general | solution.py:28
  88.0 14.0 %all-to-all-done.1 = f32[32,2,2,2,129]{4,1,3,2,0:T(2,128)S(1)} async-done(((f32[32,2,2,2,129]{4,1,3,2,0:T(2,128)}), f32[32,2,2,2,129]{4,1,3,2,0:T(2,128)S(1)}, u32[]{:S(2)}, u32[]{:S(2)}) %all-to-all-start.1) | async-done | bytes 132128 | tf_op jit(solution)/shard_map/all_to_all | solution.py:217
  102.3 32.6 %all-gather.3.cloned.1.call-done = bf16[64,2,384,128]{3,2,1,0:T(8,128)(2,1)} async-done(((bf16[2,2,384,128]{3,2,1,0:T(8,128)(2,1)}), bf16[64,2,384,128]{3,2,1,0:T(8,128)(2,1)}) %all-gather.3.cloned.1.call-update) | async-done | bytes 12582928 | tf_op jit(solution)/shard_map/all_gather | solution.py:125
  135.0 7.6 %fusion.85 = (bf16[32,1,1,384,128]{4,3,2,1,0:T(8,128)(2,1)}, bf16[32,1,1,384,128]{4,3,2,1,0:T(8,128)(2,1)}, bf16[32,1,1,384,128]{4,3,2,1,0:T(8,128)(2,1)S(1)}, bf16[32,1,1,384,128]{4,3,2,1,0:T(8,128)(2,1)S(1)}) fusion(bf16[32,2,2,384,128]{4,3,2,1,0:T(8,128)(2,1)} %bitcast.94), kind=kLoop, calls=%fused_computation.122 | loop fusion | bytes 25165824 | tf_op jit(solution)/shard_map/slice | solution.py:156
  142.6 3.6 %fusion.92 = (f32[384]{0:T(512)S(1)}, bf16[384,4096]{1,0:T(8,128)(2,1)}) fusion(bf16[384,128]{1,0:T(8,128)(2,1)S(1)} %bitcast.118, bf16[12288,128]{1,0:T(8,128)(2,1)S(1)} %bitcast.106, s32[4096]{0:T(1024)S(1)} %copy-done.13, s32[384]{0:T(512)S(1)} %copy-done.17), kind=kOutput, calls=%fused_computation.129 | convolution fusion | flops 412089984 | bytes 4312576 | tf_op jit(solution)/shard_map/dot_general | solution.py:45
  146.2 3.6 %fusion.93 = (f32[384]{0:T(512)S(1)}, bf16[384,4096]{1,0:T(8,128)(2,1)}) fusion(bf16[384,128]{1,0:T(8,128)(2,1)S(1)} %bitcast.119, bf16[12288,128]{1,0:T(8,128)(2,1)S(1)} %bitcast.107, s32[4096]{0:T(1024)S(1)} %copy-done.12, s32[384]{0:T(512)S(1)} %copy-done.17), kind=kOutput, calls=%fused_computation.130 | convolution fusion | flops 412089984 | bytes 4312576 | tf_op jit(solution)/shard_map/dot_general | solution.py:45
  149.8 3.6 %fusion.95 = (f32[384]{0:T(512)S(1)}, bf16[384,4096]{1,0:T(8,128)(2,1)}) fusion(bf16[384,128]{1,0:T(8,128)(2,1)S(1)} %bitcast.115, bf16[12288,128]{1,0:T(8,128)(2,1)S(1)} %bitcast.103, s32[4096]{0:T(1024)S(1)} %copy-done.13, s32[384]{0:T(512)S(1)} %copy-done.17), kind=kOutput, calls=%fused_computation.132 | convolution fusion | flops 412089984 | bytes 4312576 | tf_op jit(solution)/shard_map/dot_general | solution.py:45
  153.4 3.6 %fusion.96 = (f32[384]{0:T(512)S(1)}, bf16[384,4096]{1,0:T(8,128)(2,1)}) fusion(bf16[384,128]{1,0:T(8,128)(2,1)S(1)} %bitcast.116, bf16[12288,128]{1,0:T(8,128)(2,1)S(1)} %bitcast.104, s32[4096]{0:T(1024)S(1)} %copy-done.12, s32[384]{0:T(512)S(1)} %copy-done.17), kind=kOutput, calls=%fused_computation.133 | convolution fusion | flops 412089984 | bytes 4312576 | tf_op jit(solution)/shard_map/dot_general | solution.py:45
  156.9 3.6 %fusion.94 = (f32[384]{0:T(512)S(1)}, bf16[384,4096]{1,0:T(8,128)(2,1)}) fusion(bf16[384,128]{1,0:T(8,128)(2,1)S(1)} %bitcast.120, bf16[12288,128]{1,0:T(8,128)(2,1)S(1)} %bitcast.108, s32[4096]{0:T(1024)S(1)} %copy-done.11, s32[384]{0:T(512)S(1)} %copy-done.17), kind=kOutput, calls=%fused_computation.131 | convolution fusion | flops 412089984 | bytes 4312576 | tf_op jit(solution)/shard_map/dot_general | solution.py:45
  160.6 3.6 %fusion.97 = (f32[384]{0:T(512)S(1)}, bf16[384,4096]{1,0:T(8,128)(2,1)}) fusion(bf16[384,128]{1,0:T(8,128)(2,1)S(1)} %bitcast.117, bf16[12288,128]{1,0:T(8,128)(2,1)S(1)} %bitcast.105, s32[4096]{0:T(1024)S(1)} %copy-done.11, s32[384]{0:T(512)S(1)} %copy-done.17), kind=kOutput, calls=%fused_computation.134 | convolution fusion | flops 412089984 | bytes 4312576 | tf_op jit(solution)/shard_map/dot_general | solution.py:45
  164.3 3.3 %fusion.1 = f32[384,128]{1,0:T(8,128)S(1)} fusion(bf16[384,4096]{1,0:T(8,128)(2,1)} %get-tuple-element.45, bf16[12288,128]{1,0:T(8,128)(2,1)} %bitcast.98), kind=kOutput, calls=%fused_computation.10 | convolution fusion | flops 402653184 | bytes 4390912 | tf_op jit(solution)/shard_map/dot_general | solution.py:50
  172.0 3.3 %fusion.7 = f32[384,128]{1,0:T(8,128)S(1)} fusion(bf16[384,4096]{1,0:T(8,128)(2,1)} %get-tuple-element.51, bf16[12288,128]{1,0:T(8,128)(2,1)} %bitcast.95), kind=kOutput, calls=%fused_computation.16 | convolution fusion | flops 402653184 | bytes 4390912 | tf_op jit(solution)/shard_map/dot_general | solution.py:50
  181.8 4.7 %fusion = bf16[4608,194]{0,1:T(8,128)(2,1)} fusion(bf16[512,4608]{1,0:T(8,128)(2,1)} %param.21, bf16[2,512]{1,0:T(2,128)(2,1)S(1)} %bitcast.123, bf16[192,512]{1,0:T(8,128)(2,1)S(1)} %reshape.373), kind=kOutput, calls=%fused_computation.7 | convolution fusion | flops 916698112 | bytes 6705152 | tf_op jit(solution)/shard_map/ko,rk->or/dot_general | solution.py:226
  186.5 4.3 %reshape.382 = bf16[8,576,194]{1,0,2:T(8,128)(2,1)} reshape(bf16[4608,194]{0,1:T(8,128)(2,1)} %fusion) | data formatting | bytes 3575808 | tf_op jit(solution)/shard_map/reshape | solution.py:230
  192.6 33.9 %all_to_all.21 = bf16[8,576,194]{1,2,0:T(8,128)(2,1)S(1)} all-to-all(bf16[8,576,194]{1,2,0:T(8,128)(2,1)S(1)} %copy.136), channel_id=1, replica_groups=mesh['kv'=8,'blk'=32] {'kv'}, dimensions={0} | all-to-all | bytes 3575808 | tf_op jit(solution)/shard_map/all_to_all | solution.py:232
  227.5 3.3 %all-to-all-start.3 = ((f32[8,1,194]{2,1,0:T(1,128)}), f32[8,1,194]{2,1,0:T(1,128)S(1)}, u32[]{:S(2)}, u32[]{:S(2)}) async-start(f32[8,1,194]{2,1,0:T(1,128)} %broadcast_in_dim.76), calls=%async_computation.3 | async-start | bytes 16384 | tf_op jit(solution)/shard_map/all_to_all | solution.py:235
  233.5 3.5 %all-to-all-done.3 = f32[8,1,194]{2,1,0:T(1,128)S(1)} async-done(((f32[8,1,194]{2,1,0:T(1,128)}), f32[8,1,194]{2,1,0:T(1,128)S(1)}, u32[]{:S(2)}, u32[]{:S(2)}) %all-to-all-start.3) | async-done | bytes 6240 | tf_op jit(solution)/shard_map/all_to_all | solution.py:235
  (134 shorter events, 50.7 us)
Async XLA Ops:
  7.2 41.3 %copy-start.4 = (bf16[2,16,128,256]{3,2,1,0:T(8,128)(2,1)S(1)}, bf16[2,16,128,256]{3,2,1,0:T(8,128)(2,1)}, u32[]{:S(2)}) copy-start(bf16[2,16,128,256]{3,2,1,0:T(8,128)(2,1)} %param.25) | copy-start | bytes 6291460
  7.2 127.8 %all-gather.3.cloned.1.call-start = ((), (), s32[]{:S(2)}) async-start(), calls=%async_computation.4 | async-start | bytes 12976128 | tf_op jit(solution)/shard_map/all_gather | solution.py:125
  9.3 50.4 %collective-permute-start.2 = (bf16[2,192,256]{2,1,0:T(8,128)(2,1)}, bf16[2,192,256]{2,1,0:T(8,128)(2,1)S(1)}, u32[]{:S(2)}, u32[]{:S(2)}) collective-permute-start(bf16[2,192,256]{2,1,0:T(8,128)(2,1)} %param.16), channel_id=1, source_target_pairs={{0,2},{1,3},{2,4},{3,5},{4,6},{5,7},{6,8},{7,9},{8,10},{9,11},{10,... | collective-permute-start | bytes 589832 | tf_op jit(solution)/shard_map/ppermute | solution.py:23
  14.5 45.2 %collective-permute-start.1 = (bf16[2,192,256]{2,1,0:T(8,128)(2,1)}, bf16[2,192,256]{2,1,0:T(8,128)(2,1)S(1)}, u32[]{:S(2)}, u32[]{:S(2)}) collective-permute-start(bf16[2,192,256]{2,1,0:T(8,128)(2,1)} %param.16), channel_id=1, source_target_pairs={{0,3},{1,4},{2,5},{3,6},{4,7},{5,8},{6,9},{7,10},{8,11},{9,12},{10... | collective-permute-start | bytes 589832 | tf_op jit(solution)/shard_map/ppermute | solution.py:23
  20.0 38.7 %collective-permute-start = (bf16[2,192,256]{2,1,0:T(8,128)(2,1)}, bf16[2,192,256]{2,1,0:T(8,128)(2,1)}, u32[]{:S(2)}, u32[]{:S(2)}) collective-permute-start(bf16[2,192,256]{2,1,0:T(8,128)(2,1)} %param.16), channel_id=1, source_target_pairs={{0,4},{1,5},{2,6},{3,7},{4,8},{5,9},{6,10},{7,11},{8,12},{9,13},{1... | collective-permute-start | bytes 589832 | tf_op jit(solution)/shard_map/ppermute | solution.py:23
  23.7 38.0 %collective-permute-start.3 = (bf16[2,192,256]{2,1,0:T(8,128)(2,1)}, bf16[2,192,256]{2,1,0:T(8,128)(2,1)S(1)}, u32[]{:S(2)}, u32[]{:S(2)}) collective-permute-start(bf16[2,192,256]{2,1,0:T(8,128)(2,1)} %param.16), channel_id=1, source_target_pairs={{0,1},{1,2},{2,3},{3,4},{4,5},{5,6},{6,7},{7,8},{8,9},{9,10},{10,1... | collective-permute-start | bytes 589832 | tf_op jit(solution)/shard_map/ppermute | solution.py:23
  29.0 35.6 %all-to-all-start = ((bf16[32,8,256]{2,1,0:T(8,128)(2,1)}), bf16[32,8,256]{2,1,0:T(8,128)(2,1)S(1)}, u32[]{:S(2)}, u32[]{:S(2)}) async-start(bf16[32,8,256]{2,1,0:T(8,128)(2,1)} %broadcast_in_dim.67), calls=%async_computation | async-start | bytes 262144 | tf_op jit(solution)/shard_map/all_to_all | solution.py:112
  42.8 22.8 %copy-start.18 = (s32[16]{0:T(128)}, s32[16]{0:T(128)S(1)}, u32[]{:S(2)}) copy-start(s32[16]{0:T(128)S(1)} %and_select_fusion.3) | copy-start | bytes 196
  46.7 15.0 %copy-start.7 = (bf16[2,192,256]{2,1,0:T(8,128)(2,1)S(1)}, bf16[2,192,256]{2,1,0:T(8,128)(2,1)}, u32[]{:S(2)}) copy-start(bf16[2,192,256]{2,1,0:T(8,128)(2,1)} %param.16) | copy-start | bytes 589828
  75.0 27.0 %all-to-all-start.1 = ((f32[32,2,2,2,129]{4,1,3,2,0:T(2,128)}), f32[32,2,2,2,129]{4,1,3,2,0:T(2,128)S(1)}, u32[]{:S(2)}, u32[]{:S(2)}) async-start(f32[32,2,2,2,129]{4,1,3,2,0:T(2,128)} %copy.132), calls=%async_computation.1 | async-start | bytes 524288 | tf_op jit(solution)/shard_map/all_to_all | solution.py:217
  135.0 7.6 %copy-start.9 = (bf16[192,1,2,128]{3,2,1,0:T(2,128)(2,1)S(1)}, bf16[192,1,2,128]{3,2,1,0:T(2,128)(2,1)}, u32[]{:S(2)}) copy-start(bf16[192,1,2,128]{3,2,1,0:T(2,128)(2,1)} %get-tuple-element.34) | copy-start | bytes 294916
  135.0 7.6 %copy-start.13 = (s32[4096]{0:T(1024)S(1)}, s32[4096]{0:T(1024)}, u32[]{:S(2)}) copy-start(s32[4096]{0:T(1024)} %get-tuple-element.56) | copy-start | bytes 49156
  135.0 7.6 %copy-start.17 = (s32[384]{0:T(512)S(1)}, s32[384]{0:T(512)}, u32[]{:S(2)}) copy-start(s32[384]{0:T(512)} %eq.56) | copy-start | bytes 4612
  142.6 3.6 %copy-start.12 = (s32[4096]{0:T(1024)S(1)}, s32[4096]{0:T(1024)}, u32[]{:S(2)}) copy-start(s32[4096]{0:T(1024)} %broadcast_bitcast_fusion.2) | copy-start | bytes 49156
  146.2 3.6 %copy-start.8 = (bf16[192,1,2,128]{3,2,1,0:T(2,128)(2,1)S(1)}, bf16[192,1,2,128]{3,2,1,0:T(2,128)(2,1)}, u32[]{:S(2)}) copy-start(bf16[192,1,2,128]{3,2,1,0:T(2,128)(2,1)} %get-tuple-element.33) | copy-start | bytes 294916
  153.4 3.6 %copy-start.11 = (s32[4096]{0:T(1024)S(1)}, s32[4096]{0:T(1024)}, u32[]{:S(2)}) copy-start(s32[4096]{0:T(1024)} %get-tuple-element.57) | copy-start | bytes 49156
  164.3 3.3 %copy-start.1 = (bf16[32,1,1,384,128]{4,3,2,1,0:T(8,128)(2,1)S(1)}, bf16[32,1,1,384,128]{4,3,2,1,0:T(8,128)(2,1)}, u32[]{:S(2)}) copy-start(bf16[32,1,1,384,128]{4,3,2,1,0:T(8,128)(2,1)} %get-tuple-element.26) | copy-start | bytes 9437188
  167.7 3.0 %copy-start.3 = (bf16[384,4096]{1,0:T(8,128)(2,1)S(1)}, bf16[384,4096]{1,0:T(8,128)(2,1)}, u32[]{:S(2)}) copy-start(bf16[384,4096]{1,0:T(8,128)(2,1)} %get-tuple-element.47) | copy-start | bytes 9437188
  172.0 3.3 %copy-start = (bf16[32,1,1,384,128]{4,3,2,1,0:T(8,128)(2,1)S(1)}, bf16[32,1,1,384,128]{4,3,2,1,0:T(8,128)(2,1)}, u32[]{:S(2)}) copy-start(bf16[32,1,1,384,128]{4,3,2,1,0:T(8,128)(2,1)} %get-tuple-element.25) | copy-start | bytes 9437188
  175.3 3.0 %copy-start.2 = (bf16[384,4096]{1,0:T(8,128)(2,1)S(1)}, bf16[384,4096]{1,0:T(8,128)(2,1)}, u32[]{:S(2)}) copy-start(bf16[384,4096]{1,0:T(8,128)(2,1)} %get-tuple-element.53) | copy-start | bytes 9437188
  226.5 10.6 %copy-start.6 = (bf16[192,576]{1,0:T(8,128)(2,1)S(1)}, bf16[192,576]{1,0:T(8,128)(2,1)}, u32[]{:S(2)}) copy-start(bf16[192,576]{1,0:T(8,128)(2,1)} %param.17) | copy-start | bytes 663556
  226.5 10.6 %copy-start.15 = (f32[576]{0:T(1024)S(1)}, f32[576]{0:T(1024)}, u32[]{:S(2)}) copy-start(f32[576]{0:T(1024)} %param.22) | copy-start | bytes 6916
  226.5 10.6 %copy-start.16 = (bf16[2,576]{1,0:T(2,128)(2,1)S(1)}, bf16[2,576]{1,0:T(2,128)(2,1)}, u32[]{:S(2)}) copy-start(bf16[2,576]{1,0:T(2,128)(2,1)} %param.20) | copy-start | bytes 6916
  227.5 9.5 %all-to-all-start.3 = ((f32[8,1,194]{2,1,0:T(1,128)}), f32[8,1,194]{2,1,0:T(1,128)S(1)}, u32[]{:S(2)}, u32[]{:S(2)}) async-start(f32[8,1,194]{2,1,0:T(1,128)} %broadcast_in_dim.76), calls=%async_computation.3 | async-start | bytes 16384 | tf_op jit(solution)/shard_map/all_to_all | solution.py:235
  (4 other events, 4.5 us)
Sparse Core Ops, SparseCore 0:
  10.5 124.3 all-gather.2

commit v6 on v5

--- a/solution.py
+++ b/solution.py
@@ -1,8 +1,11 @@
+import functools
 import math
 
 import jax
 import jax.numpy as jnp
 from jax import lax
+from jax.experimental import pallas as pl
+from jax.experimental.pallas import tpu as pltpu
 from jax.sharding import PartitionSpec as P
 
 D = 4608
@@ -15,6 +18,59 @@
 
 soft_cap = 50.0
 norm_eps = 1e-06
+
+
+def prefix_kernel(q_ref, k_ref, v_ref, own_ref, row_ref, num_ref, den_ref, *, q_scale, group):
+    step = pl.program_id(1)
+
+    @pl.when(step == 0)
+    def _():
+        num_ref[...] = jnp.zeros_like(num_ref)
+        den_ref[...] = jnp.zeros_like(den_ref)
+
+    q = q_ref[0]
+    rows = row_ref[...]
+    numer = num_ref[0]
+    denom = den_ref[0]
+    for part in range(group):
+        k = k_ref[part, 0, 0]
+        v = v_ref[part, 0, 0]
+        s = lax.dot_general(q, k, (((1,), (1,)), ((), ())), preferred_element_type=jnp.float32)
+        capped = soft_cap * jnp.tanh((s * q_scale) / soft_cap)
+        seen = rows == own_ref[part]
+        w = jnp.where(seen, jnp.exp(capped), 0.0)
+        denom = denom + jnp.sum(w, axis=1, keepdims=True)
+        numer = numer + jnp.dot(w.astype(jnp.bfloat16), v, preferred_element_type=jnp.float32)
+    num_ref[0] = numer
+    den_ref[0] = denom
+
+
+def prefix_attention(q_heads, gathered, key_owner, row_prefix, q_scale, group=4, interpret=False):
+    heads, rows_q, head_dim = q_heads.shape
+    sources, _, _, held_rows, _ = gathered.shape
+    steps = sources // group
+    kern = functools.partial(prefix_kernel, q_scale=q_scale, group=group)
+    return pl.pallas_call(
+        kern,
+        grid=(heads, steps),
+        in_specs=[
+            pl.BlockSpec((1, rows_q, head_dim), lambda h, j: (h, 0, 0)),
+            pl.BlockSpec((group, 1, 1, held_rows, head_dim), lambda h, j: (j, 0, h, 0, 0)),
+            pl.BlockSpec((group, 1, 1, held_rows, head_dim), lambda h, j: (j, 1, h, 0, 0)),
+            pl.BlockSpec((group, 1, held_rows), lambda h, j: (j, 0, 0)),
+            pl.BlockSpec((rows_q, 1), lambda h, j: (0, 0)),
+        ],
+        out_specs=[
+            pl.BlockSpec((1, rows_q, head_dim), lambda h, j: (h, 0, 0)),
+            pl.BlockSpec((1, rows_q, 1), lambda h, j: (h, 0, 0)),
+        ],
+        out_shape=[
+            jax.ShapeDtypeStruct((heads, rows_q, head_dim), jnp.float32),
+            jax.ShapeDtypeStruct((heads, rows_q, 1), jnp.float32),
+        ],
+        compiler_params=pltpu.CompilerParams(dimension_semantics=("parallel", "arbitrary")),
+        interpret=interpret,
+    )(q_heads, gathered, gathered, key_owner, row_prefix)
 
 
 def from_behind(block, axis, distance):
@@ -144,31 +200,15 @@
     pool_pages = prefix_table.shape[0]
     per_prefix = PREFIX_LENGTH // PAGE_TOKENS
     page_owner = inverse_rows(prefix_table, jnp.arange(pool_pages, dtype=jnp.int32)) // per_prefix
-    key_owner = jnp.repeat(page_owner, page_len)
-    row_prefix = jnp.repeat(tok_prefix, query_group_width)
+    key_owner = jnp.repeat(page_owner, page_len).reshape(blk_size, 1, held_rows)
+    row_prefix = jnp.repeat(tok_prefix, query_group_width)[:, None]
     rows_q = tok_rows * query_group_width
-    chunks = 3
-    chunk_keys = blk_size * held_rows // chunks
-    sums = []
-    for head in range(kv_heads):
-        head_queries = own_queries[:, head].reshape(rows_q, head_dim)
-        head_keys = gathered[:, 0, head].reshape(blk_size * held_rows, head_dim)
-        head_values = gathered[:, 1, head].reshape(blk_size * held_rows, head_dim)
-        numer_h = jnp.zeros((rows_q, head_dim), jnp.float32)
-        denom_h = jnp.zeros((rows_q,), jnp.float32)
-        for chunk in range(chunks):
-            span = slice(chunk * chunk_keys, (chunk + 1) * chunk_keys)
-            seen = row_prefix[:, None] == key_owner[span][None, :]
-            numer_c, denom_c = attend_rows(
-                head_queries, head_keys[span], head_values[span], seen, q_scale
-            )
-            numer_h = numer_h + numer_c
-            denom_h = denom_h + denom_c
-        sums.append((numer_h, denom_h))
-    head_numer = [numer.reshape(tok_rows, query_group_width, head_dim) for numer, _ in sums]
-    head_denom = [denom.reshape(tok_rows, query_group_width) for _, denom in sums]
-    pre_numer = jnp.stack(head_numer, axis=1)
-    pre_denom = jnp.stack(head_denom, axis=1)
+    q_by_head = own_queries.transpose(1, 0, 2, 3).reshape(kv_heads, rows_q, head_dim)
+    numer_p, denom_p = prefix_attention(q_by_head, gathered, key_owner, row_prefix, q_scale)
+    pre_numer = numer_p.reshape(kv_heads, tok_rows, query_group_width, head_dim).transpose(
+        1, 0, 2, 3
+    )
+    pre_denom = denom_p.reshape(kv_heads, tok_rows, query_group_width).transpose(1, 0, 2)
     suffix_attn = ((own_numer + pre_numer) / (own_denom + pre_denom)[..., None]).astype(
         jnp.bfloat16
     )

time: 246 us -> 227 us (0.923)
  matrix products: 49 us -> 13.5 us
  Pallas kernels: 0 us -> 24.1 us
  local copies, waits for them, and re-layouts: 38.2 us -> 24.8 us
  waiting for transfers between devices: 61 us -> 68.3 us
    dot_general x12 -> x0, matrix products: 36.2 us -> none  [the longest x6 21.5 us: attend_rows(): jnp.dot(query_rows, key_rows.T, preferred_element_type=jnp.float32)]
    pallas_call x0 -> x1, Pallas kernels: none -> 24.1 us  [prefix_attention(): pl.pallas_call(kern, grid=(heads, steps), in_specs=[pl.BlockSpec((1, rows...]
    slice x3 -> x0, local copies, waits for them, and re-layouts: 8.45 us -> none  [the longest x1 7.57 us: body(): head_values = gathered[:, 1, head].reshape(blk_size * held_rows, head_dim)]
    all_gather x1, waiting for transfers between devices: 32.6 us -> 35.3 us  [body(): gathered = lax.all_gather(piece, 'blk', axis=0, tiled=False)]
    all_to_all x1, waiting for transfers between devices: 14 us -> 16.5 us  [body(): lax.all_to_all(slot_sums, 'blk', 0, 0, tiled=False)]
    unnamed x47 -> x23, local copies, waits for them, and re-layouts: 7.54 us -> 5.06 us
  transfers between devices with their start and end apart: 8 -> 8, of which waited for: 6 -> 6; matrix products, arithmetic and copies ran while one was open for 14% -> 12% of each run, Pallas kernels for 0% -> 0%
where the time goes in v6:
time: 227 us; the launch traced here: 226 us
  waiting for transfers between devices  68.3 us (30%)
  starting transfers between devices  39.6 us (17%)
  blocking collectives  31.6 us (14%)
  local copies, waits for them, and re-layouts  24.8 us (11%)
  Pallas kernels  24.1 us (11%)
  between operations  14.4 us (6%)
  matrix products  13.5 us (6%)
  other arithmetic  9.7 us (4%)
    all_gather x1, waiting for transfers between devices, body(): gathered = lax.all_gather(piece, 'blk', axis=0, tiled=False)  35.3 us
    all_to_all x1, blocking collectives, body(): lax.all_to_all(shares, 'kv', 0, 0, tiled=False).astype(jnp.float32)  31.6 us
    pallas_call x1, Pallas kernels, prefix_attention(): pl.pallas_call(kern, grid=(heads, steps), in_specs=[pl.BlockSpec((1, rows...  24.1 us
    ppermute x4, starting transfers between devices, from_behind(): return lax.ppermute(block, axis, route)  17.6 us
    all_to_all x1, waiting for transfers between devices, body(): lax.all_to_all(slot_sums, 'blk', 0, 0, tiled=False)  16.5 us
    ppermute x4, waiting for transfers between devices, from_behind(): return lax.ppermute(block, axis, route)  12.1 us
    all_to_all x1, starting transfers between devices, body(): lax.all_to_all(jnp.broadcast_to(dec_local[None], (blk_size,) + dec_local....  9.52 us
    all_to_all x1, starting transfers between devices, body(): lax.all_to_all(slot_sums, 'blk', 0, 0, tiled=False)  9.06 us
  transfers between devices with their start and end apart: 8, of which 6 were waited for; matrix products, arithmetic and copies ran while one was open for 12% of the time, Pallas kernels for 0%

profile of v6, /device:TPU:2, one launch (start us, length us, event | category | flops | bytes accessed | tf_op | source)
XLA Modules:
  0.0 226.0 jit_solution(14823003541966319133)
XLA Ops:
  7.2 1.2 reshape.307
  9.3 5.2 %collective-permute-start.2 = (bf16[2,192,256]{2,1,0:T(8,128)(2,1)}, bf16[2,192,256]{2,1,0:T(8,128)(2,1)S(1)}, u32[]{:S(2)}, u32[]{:S(2)}) collective-permute-start(bf16[2,192,256]{2,1,0:T(8,128)(2,1)} %param.16), channel_id=1, source_target_pairs={{0,2},{1,3},{2,4},{3,5},{4,6},{5,7},{6,8},{7,9},{8,10},{9,11},{10,... | collective-permute-start | bytes 589832 | tf_op jit(solution)/shard_map/ppermute | solution.py:79
  14.5 5.6 %collective-permute-start.1 = (bf16[2,192,256]{2,1,0:T(8,128)(2,1)}, bf16[2,192,256]{2,1,0:T(8,128)(2,1)S(1)}, u32[]{:S(2)}, u32[]{:S(2)}) collective-permute-start(bf16[2,192,256]{2,1,0:T(8,128)(2,1)} %param.16), channel_id=1, source_target_pairs={{0,3},{1,4},{2,5},{3,6},{4,7},{5,8},{6,9},{7,10},{8,11},{9,12},{10... | collective-permute-start | bytes 589832 | tf_op jit(solution)/shard_map/ppermute | solution.py:79
  20.0 3.7 %collective-permute-start = (bf16[2,192,256]{2,1,0:T(8,128)(2,1)}, bf16[2,192,256]{2,1,0:T(8,128)(2,1)S(1)}, u32[]{:S(2)}, u32[]{:S(2)}) collective-permute-start(bf16[2,192,256]{2,1,0:T(8,128)(2,1)} %param.16), channel_id=1, source_target_pairs={{0,4},{1,5},{2,6},{3,7},{4,8},{5,9},{6,10},{7,11},{8,12},{9,13},{1... | collective-permute-start | bytes 589832 | tf_op jit(solution)/shard_map/ppermute | solution.py:79
  23.7 3.2 %collective-permute-start.3 = (bf16[2,192,256]{2,1,0:T(8,128)(2,1)}, bf16[2,192,256]{2,1,0:T(8,128)(2,1)S(1)}, u32[]{:S(2)}, u32[]{:S(2)}) collective-permute-start(bf16[2,192,256]{2,1,0:T(8,128)(2,1)} %param.16), channel_id=1, source_target_pairs={{0,1},{1,2},{2,3},{3,4},{4,5},{5,6},{6,7},{7,8},{8,9},{9,10},{10,1... | collective-permute-start | bytes 589832 | tf_op jit(solution)/shard_map/ppermute | solution.py:79
  29.0 9.5 %all-to-all-start = ((bf16[32,8,256]{2,1,0:T(8,128)(2,1)}), bf16[32,8,256]{2,1,0:T(8,128)(2,1)S(1)}, u32[]{:S(2)}, u32[]{:S(2)}) async-start(bf16[32,8,256]{2,1,0:T(8,128)(2,1)} %broadcast_in_dim.54), calls=%async_computation | async-start | bytes 262144 | tf_op jit(solution)/shard_map/all_to_all | solution.py:168
  47.3 2.4 %copy.165 = bf16[2,16,128,256]{2,3,1,0:T(8,128)(2,1)} copy(bf16[2,16,128,256]{3,2,1,0:T(8,128)(2,1)S(1)} %copy-done) | data formatting | bytes 4194304 | tf_op args[10]
  49.6 9.0 %collective-permute-done = bf16[2,192,256]{2,1,0:T(8,128)(2,1)S(1)} collective-permute-done((bf16[2,192,256]{2,1,0:T(8,128)(2,1)}, bf16[2,192,256]{2,1,0:T(8,128)(2,1)S(1)}, u32[]{:S(2)}, u32[]{:S(2)}) %collective-permute-start) | collective-permute-done | bytes 196640 | tf_op jit(solution)/shard_map/ppermute | solution.py:79
  58.7 3.1 %collective-permute-done.3 = bf16[2,192,256]{2,1,0:T(8,128)(2,1)S(1)} collective-permute-done((bf16[2,192,256]{2,1,0:T(8,128)(2,1)}, bf16[2,192,256]{2,1,0:T(8,128)(2,1)S(1)}, u32[]{:S(2)}, u32[]{:S(2)}) %collective-permute-start.3) | collective-permute-done | bytes 196640 | tf_op jit(solution)/shard_map/ppermute | solution.py:79
  65.2 2.5 %broadcast_select_fusion = bf16[2,16,128,256]{2,3,1,0:T(8,128)(2,1)S(1)} fusion(bf16[2,16,128,256]{2,3,1,0:T(8,128)(2,1)} %copy.165, pred[16,128]{1,0:T(8,128)(4,1)S(1)} %fusion.39, bf16[2,16,256]{2,1,0:T(8,128)(2,1)S(1)} %fusion.16), kind=kLoop, calls=%fused_computation.6 | loop fusion | flops 1048576 | bytes 4212736 | tf_op jit(solution)/shard_map/jit(_where)/select_n | solution.py:233
  70.7 9.1 %all-to-all-start.1 = ((f32[32,2,2,2,129]{4,1,3,2,0:T(2,128)}), f32[32,2,2,2,129]{4,1,3,2,0:T(2,128)S(1)}, u32[]{:S(2)}, u32[]{:S(2)}) async-start(f32[32,2,2,2,129]{4,1,3,2,0:T(2,128)} %copy.171), calls=%async_computation.1 | async-start | bytes 524288 | tf_op jit(solution)/shard_map/all_to_all | solution.py:257
  79.7 3.9 %fusion.1 = (f32[192,2,2]{0,2,1:T(2,128)S(1)}, f32[2,960,192,2]{1,2,3,0:T(8,128)}) fusion(pred[192,960]{1,0:T(8,128)(4,1)} %compare_and_fusion, bf16[192,2,2,128]{3,2,1,0:T(2,128)(2,1)S(1)} %reshape.305, bf16[960,2,128,1]{2,1,0,3:T(2,128)(2,1)} %bitcast.83), kind=kOutput, calls=%fused_computation.4 | convolution fusion | flops 191692032 | bytes 3824640 | tf_op jit(solution)/shard_map/qhgd,khd->qhgk/dot_general | solution.py:84
  83.6 16.5 %all-to-all-done.1 = f32[32,2,2,2,129]{4,1,3,2,0:T(2,128)S(1)} async-done(((f32[32,2,2,2,129]{4,1,3,2,0:T(2,128)}), f32[32,2,2,2,129]{4,1,3,2,0:T(2,128)S(1)}, u32[]{:S(2)}, u32[]{:S(2)}) %all-to-all-start.1) | async-done | bytes 132128 | tf_op jit(solution)/shard_map/all_to_all | solution.py:257
  100.4 35.3 %all-gather.3.cloned.1.call-done = bf16[64,2,384,128]{3,2,1,0:T(8,128)(2,1)} async-done(((bf16[2,2,384,128]{3,2,1,0:T(8,128)(2,1)}), bf16[64,2,384,128]{3,2,1,0:T(8,128)(2,1)}) %all-gather.3.cloned.1.call-update) | async-done | bytes 12582928 | tf_op jit(solution)/shard_map/all_gather | solution.py:181
  135.8 24.1 %shard_map.166 = (f32[2,384,128]{2,1,0:T(8,128)}, f32[2,384,1]{2,1,0:T(8,128)}) custom-call(bf16[2,384,128]{2,1,0:T(8,128)(2,1)} %bitcast.81, bf16[32,2,2,384,128]{4,3,2,1,0:T(8,128)(2,1)} %bitcast.76, bf16[32,2,2,384,128]{4,3,2,1,0:T(8,128)(2,1)} %bitcast.77, s32[32,1,384]{2,1,0:T(1,128)} %broadcast_in_dim.64.own_ref, s32[384,1]{1,0:T(8,128)} %broadcast_in_dim_reshape.4.row_ref), custom_call_target="tpu_custom_call" | custom-call | tf_op jit(solution)/shard_map/pallas_call | solution.py:53
  159.9 1.2 reduce.3
  161.4 3.0 %fusion.20 = bf16[192,2,2,128]{3,0,2,1:T(8,128)(2,1)S(1)} fusion(f32[2,960,192,2]{1,2,3,0:T(8,128)} %get-tuple-element.41, pred[192,960]{1,0:T(8,128)(4,1)S(1)} %copy-done.5, bf16[960,2,128,1]{2,1,0,3:T(2,128)(2,1)S(1)} %bitcast.82, f32[2,192,2,128]{3,2,1,0:T(2,128)} %bitcast.89, f32[192,2,2]{0,2,1:T(2,128)S(1)} %bitcast_add_fusion.1), kind=kOutput, calls=%fused_computation.20 | convolution fusion | flops 191987712 | bytes 4217856 | tf_op jit(solution)/shard_map/qhgk,khd->qhgd/dot_general | solution.py:90
  164.6 4.7 %fusion = bf16[4608,194]{0,1:T(8,128)(2,1)} fusion(bf16[512,4608]{1,0:T(8,128)(2,1)} %param.21, bf16[2,512]{1,0:T(2,128)(2,1)S(1)} %bitcast.87, bf16[192,512]{1,0:T(8,128)(2,1)S(1)} %reshape.310), kind=kOutput, calls=%fused_computation.1 | convolution fusion | flops 916698112 | bytes 6705152 | tf_op jit(solution)/shard_map/ko,rk->or/dot_general | solution.py:266
  169.4 4.3 %reshape.319 = bf16[8,576,194]{1,0,2:T(8,128)(2,1)} reshape(bf16[4608,194]{0,1:T(8,128)(2,1)} %fusion) | data formatting | bytes 3575808 | tf_op jit(solution)/shard_map/reshape | solution.py:270
  173.7 1.8 copy.175
  175.5 31.6 %all_to_all.21 = bf16[8,576,194]{1,2,0:T(8,128)(2,1)S(1)} all-to-all(bf16[8,576,194]{1,2,0:T(8,128)(2,1)S(1)} %copy.175), channel_id=1, replica_groups=mesh['kv'=8,'blk'=32] {'kv'}, dimensions={0} | all-to-all | bytes 3575808 | tf_op jit(solution)/shard_map/all_to_all | solution.py:272
  208.2 3.3 %all-to-all-start.3 = ((f32[8,1,194]{2,1,0:T(1,128)}), f32[8,1,194]{2,1,0:T(1,128)S(1)}, u32[]{:S(2)}, u32[]{:S(2)}) async-start(f32[8,1,194]{2,1,0:T(1,128)} %broadcast_in_dim.59), calls=%async_computation.3 | async-start | bytes 16384 | tf_op jit(solution)/shard_map/all_to_all | solution.py:275
  211.5 2.6 %copy.177 = bf16[2,16,128,256]{3,2,1,0:T(8,128)(2,1)} copy(bf16[2,16,128,256]{2,3,1,0:T(8,128)(2,1)S(1)} %broadcast_select_fusion) | data formatting | bytes 4194304
  214.1 3.5 %all-to-all-done.3 = f32[8,1,194]{2,1,0:T(1,128)S(1)} async-done(((f32[8,1,194]{2,1,0:T(1,128)}), f32[8,1,194]{2,1,0:T(1,128)S(1)}, u32[]{:S(2)}, u32[]{:S(2)}) %all-to-all-start.3) | async-done | bytes 6240 | tf_op jit(solution)/shard_map/all_to_all | solution.py:275
  (96 shorter events, 21.3 us)
Async XLA Ops:
  7.2 39.2 %copy-start.3 = (bf16[192,512]{1,0:T(8,128)(2,1)S(1)}, bf16[192,512]{1,0:T(8,128)(2,1)}, u32[]{:S(2)}) copy-start(bf16[192,512]{1,0:T(8,128)(2,1)} %param.15) | copy-start | bytes 589828
  7.2 40.1 %copy-start = (bf16[2,16,128,256]{3,2,1,0:T(8,128)(2,1)S(1)}, bf16[2,16,128,256]{3,2,1,0:T(8,128)(2,1)}, u32[]{:S(2)}) copy-start(bf16[2,16,128,256]{3,2,1,0:T(8,128)(2,1)} %param.25) | copy-start | bytes 6291460
  7.2 128.6 %all-gather.3.cloned.1.call-start = ((), (), s32[]{:S(2)}) async-start(), calls=%async_computation.4 | async-start | bytes 12976128 | tf_op jit(solution)/shard_map/all_gather | solution.py:181
  9.3 49.4 %collective-permute-start.2 = (bf16[2,192,256]{2,1,0:T(8,128)(2,1)}, bf16[2,192,256]{2,1,0:T(8,128)(2,1)S(1)}, u32[]{:S(2)}, u32[]{:S(2)}) collective-permute-start(bf16[2,192,256]{2,1,0:T(8,128)(2,1)} %param.16), channel_id=1, source_target_pairs={{0,2},{1,3},{2,4},{3,5},{4,6},{5,7},{6,8},{7,9},{8,10},{9,11},{10,... | collective-permute-start | bytes 589832 | tf_op jit(solution)/shard_map/ppermute | solution.py:79
  14.5 44.1 %collective-permute-start.1 = (bf16[2,192,256]{2,1,0:T(8,128)(2,1)}, bf16[2,192,256]{2,1,0:T(8,128)(2,1)S(1)}, u32[]{:S(2)}, u32[]{:S(2)}) collective-permute-start(bf16[2,192,256]{2,1,0:T(8,128)(2,1)} %param.16), channel_id=1, source_target_pairs={{0,3},{1,4},{2,5},{3,6},{4,7},{5,8},{6,9},{7,10},{8,11},{9,12},{10... | collective-permute-start | bytes 589832 | tf_op jit(solution)/shard_map/ppermute | solution.py:79
  20.0 38.6 %collective-permute-start = (bf16[2,192,256]{2,1,0:T(8,128)(2,1)}, bf16[2,192,256]{2,1,0:T(8,128)(2,1)S(1)}, u32[]{:S(2)}, u32[]{:S(2)}) collective-permute-start(bf16[2,192,256]{2,1,0:T(8,128)(2,1)} %param.16), channel_id=1, source_target_pairs={{0,4},{1,5},{2,6},{3,7},{4,8},{5,9},{6,10},{7,11},{8,12},{9,13},{1... | collective-permute-start | bytes 589832 | tf_op jit(solution)/shard_map/ppermute | solution.py:79
  23.7 38.0 %collective-permute-start.3 = (bf16[2,192,256]{2,1,0:T(8,128)(2,1)}, bf16[2,192,256]{2,1,0:T(8,128)(2,1)S(1)}, u32[]{:S(2)}, u32[]{:S(2)}) collective-permute-start(bf16[2,192,256]{2,1,0:T(8,128)(2,1)} %param.16), channel_id=1, source_target_pairs={{0,1},{1,2},{2,3},{3,4},{4,5},{5,6},{6,7},{7,8},{8,9},{9,10},{10,1... | collective-permute-start | bytes 589832 | tf_op jit(solution)/shard_map/ppermute | solution.py:79
  29.0 35.6 %all-to-all-start = ((bf16[32,8,256]{2,1,0:T(8,128)(2,1)}), bf16[32,8,256]{2,1,0:T(8,128)(2,1)S(1)}, u32[]{:S(2)}, u32[]{:S(2)}) async-start(bf16[32,8,256]{2,1,0:T(8,128)(2,1)} %broadcast_in_dim.54), calls=%async_computation | async-start | bytes 262144 | tf_op jit(solution)/shard_map/all_to_all | solution.py:168
  46.4 15.3 %copy-start.4 = (bf16[2,192,256]{2,1,0:T(8,128)(2,1)S(1)}, bf16[2,192,256]{2,1,0:T(8,128)(2,1)}, u32[]{:S(2)}) copy-start(bf16[2,192,256]{2,1,0:T(8,128)(2,1)} %param.16) | copy-start | bytes 589828
  70.7 29.5 %all-to-all-start.1 = ((f32[32,2,2,2,129]{4,1,3,2,0:T(2,128)}), f32[32,2,2,2,129]{4,1,3,2,0:T(2,128)S(1)}, u32[]{:S(2)}, u32[]{:S(2)}) async-start(f32[32,2,2,2,129]{4,1,3,2,0:T(2,128)} %copy.171), calls=%async_computation.1 | async-start | bytes 524288 | tf_op jit(solution)/shard_map/all_to_all | solution.py:257
  135.8 25.6 %copy-start.1 = (bf16[960,2,128]{2,1,0:T(2,128)(2,1)S(1)}, bf16[960,2,128]{2,1,0:T(2,128)(2,1)}, u32[]{:S(2)}) copy-start(bf16[960,2,128]{2,1,0:T(2,128)(2,1)} %reshape_squeeze.12) | copy-start | bytes 1474564
  135.8 25.6 %copy-start.5 = (pred[192,960]{1,0:T(8,128)(4,1)S(1)}, pred[192,960]{1,0:T(8,128)(4,1)}, u32[]{:S(2)}) copy-start(pred[192,960]{1,0:T(8,128)(4,1)} %compare_and_fusion) | copy-start | bytes 552964
  207.1 10.6 %copy-start.2 = (bf16[192,576]{1,0:T(8,128)(2,1)S(1)}, bf16[192,576]{1,0:T(8,128)(2,1)}, u32[]{:S(2)}) copy-start(bf16[192,576]{1,0:T(8,128)(2,1)} %param.17) | copy-start | bytes 663556
  207.1 10.6 %copy-start.6 = (f32[576]{0:T(1024)S(1)}, f32[576]{0:T(1024)}, u32[]{:S(2)}) copy-start(f32[576]{0:T(1024)} %param.22) | copy-start | bytes 6916
  207.1 10.6 %copy-start.7 = (bf16[2,576]{1,0:T(2,128)(2,1)S(1)}, bf16[2,576]{1,0:T(2,128)(2,1)}, u32[]{:S(2)}) copy-start(bf16[2,576]{1,0:T(2,128)(2,1)} %param.20) | copy-start | bytes 6916
  208.2 9.5 %all-to-all-start.3 = ((f32[8,1,194]{2,1,0:T(1,128)}), f32[8,1,194]{2,1,0:T(1,128)S(1)}, u32[]{:S(2)}, u32[]{:S(2)}) async-start(f32[8,1,194]{2,1,0:T(1,128)} %broadcast_in_dim.59), calls=%async_computation.3 | async-start | bytes 16384 | tf_op jit(solution)/shard_map/all_to_all | solution.py:275
Sparse Core Ops, SparseCore 0:
  10.5 125.1 all-gather.2

commit v7 on v6

--- a/solution.py
+++ b/solution.py
@@ -36,7 +36,7 @@
         k = k_ref[part, 0, 0]
         v = v_ref[part, 0, 0]
         s = lax.dot_general(q, k, (((1,), (1,)), ((), ())), preferred_element_type=jnp.float32)
-        capped = soft_cap * jnp.tanh((s * q_scale) / soft_cap)
+        capped = soft_cap * jnp.tanh(s * (q_scale / soft_cap))
         seen = rows == own_ref[part]
         w = jnp.where(seen, jnp.exp(capped), 0.0)
         denom = denom + jnp.sum(w, axis=1, keepdims=True)
@@ -45,7 +45,7 @@
     den_ref[0] = denom
 
 
-def prefix_attention(q_heads, gathered, key_owner, row_prefix, q_scale, group=4, interpret=False):
+def prefix_attention(q_heads, gathered, key_owner, row_prefix, q_scale, group=8):
     heads, rows_q, head_dim = q_heads.shape
     sources, _, _, held_rows, _ = gathered.shape
     steps = sources // group
@@ -69,7 +69,6 @@
             jax.ShapeDtypeStruct((heads, rows_q, 1), jnp.float32),
         ],
         compiler_params=pltpu.CompilerParams(dimension_semantics=("parallel", "arbitrary")),
-        interpret=interpret,
     )(q_heads, gathered, gathered, key_owner, row_prefix)
 
 
@@ -92,19 +91,6 @@
         weights.astype(jnp.bfloat16),
         value_rows,
         preferred_element_type=jnp.float32,
-    )
-    return (numerator, denominator)
-
-
-def attend_rows(query_rows, key_rows, value_rows, visible, q_scale):
-    logits = (
-        jnp.dot(query_rows, key_rows.T, preferred_element_type=jnp.float32) * q_scale
-    )
-    capped = soft_cap * jnp.tanh(logits / soft_cap)
-    weights = jnp.where(visible, jnp.exp(capped), 0.0)
-    denominator = jnp.sum(weights, axis=1)
-    numerator = jnp.dot(
-        weights.astype(jnp.bfloat16), value_rows, preferred_element_type=jnp.float32
     )
     return (numerator, denominator)
 

time: 227 us -> 224 us (0.987)
  Pallas kernels: 24.1 us -> 21.7 us
    pallas_call x1, Pallas kernels: 24.1 us -> 21.7 us  [prefix_attention(): pl.pallas_call(kern, grid=(heads, steps), in_specs=[pl.BlockSpec((1, rows...]
where the time goes in v7:
time: 224 us
  waiting for transfers between devices  68.3 us (30%)
  starting transfers between devices  39.6 us (18%)
  blocking collectives  31.6 us (14%)
  local copies, waits for them, and re-layouts  24.8 us (11%)
  Pallas kernels  21.7 us (10%)
  between operations  14.4 us (6%)
  matrix products  13.5 us (6%)
  other arithmetic  9.7 us (4%)
    all_gather x1, waiting for transfers between devices, body(): gathered = lax.all_gather(piece, 'blk', axis=0, tiled=False)  35.3 us
    all_to_all x1, blocking collectives, body(): lax.all_to_all(shares, 'kv', 0, 0, tiled=False).astype(jnp.float32)  31.6 us
    pallas_call x1, Pallas kernels, prefix_attention(): pl.pallas_call(kern, grid=(heads, steps), in_specs=[pl.BlockSpec((1, rows...  21.7 us
    ppermute x4, starting transfers between devices, from_behind(): return lax.ppermute(block, axis, route)  17.6 us
    all_to_all x1, waiting for transfers between devices, body(): lax.all_to_all(slot_sums, 'blk', 0, 0, tiled=False)  16.5 us
    ppermute x4, waiting for transfers between devices, from_behind(): return lax.ppermute(block, axis, route)  12.1 us
    all_to_all x1, starting transfers between devices, body(): lax.all_to_all(jnp.broadcast_to(dec_local[None], (blk_size,) + dec_local....  9.52 us
    all_to_all x1, starting transfers between devices, body(): lax.all_to_all(slot_sums, 'blk', 0, 0, tiled=False)  9.07 us
  transfers between devices with their start and end apart: 8, of which 6 were waited for; matrix products, arithmetic and copies ran while one was open for 12% of the time, Pallas kernels for 0%

profile of v7, /device:TPU:2, one launch (start us, length us, event | category | flops | bytes accessed | tf_op | source)
XLA Modules:
  0.0 223.6 jit_solution(7584626730751923641)
XLA Ops:
  7.2 1.2 reshape.307
  9.3 5.2 %collective-permute-start.2 = (bf16[2,192,256]{2,1,0:T(8,128)(2,1)}, bf16[2,192,256]{2,1,0:T(8,128)(2,1)S(1)}, u32[]{:S(2)}, u32[]{:S(2)}) collective-permute-start(bf16[2,192,256]{2,1,0:T(8,128)(2,1)} %param.16), channel_id=1, source_target_pairs={{0,2},{1,3},{2,4},{3,5},{4,6},{5,7},{6,8},{7,9},{8,10},{9,11},{10,... | collective-permute-start | bytes 589832 | tf_op jit(solution)/shard_map/ppermute | solution.py:78
  14.5 5.6 %collective-permute-start.1 = (bf16[2,192,256]{2,1,0:T(8,128)(2,1)}, bf16[2,192,256]{2,1,0:T(8,128)(2,1)S(1)}, u32[]{:S(2)}, u32[]{:S(2)}) collective-permute-start(bf16[2,192,256]{2,1,0:T(8,128)(2,1)} %param.16), channel_id=1, source_target_pairs={{0,3},{1,4},{2,5},{3,6},{4,7},{5,8},{6,9},{7,10},{8,11},{9,12},{10... | collective-permute-start | bytes 589832 | tf_op jit(solution)/shard_map/ppermute | solution.py:78
  20.0 3.7 %collective-permute-start = (bf16[2,192,256]{2,1,0:T(8,128)(2,1)}, bf16[2,192,256]{2,1,0:T(8,128)(2,1)S(1)}, u32[]{:S(2)}, u32[]{:S(2)}) collective-permute-start(bf16[2,192,256]{2,1,0:T(8,128)(2,1)} %param.16), channel_id=1, source_target_pairs={{0,4},{1,5},{2,6},{3,7},{4,8},{5,9},{6,10},{7,11},{8,12},{9,13},{1... | collective-permute-start | bytes 589832 | tf_op jit(solution)/shard_map/ppermute | solution.py:78
  23.7 3.2 %collective-permute-start.3 = (bf16[2,192,256]{2,1,0:T(8,128)(2,1)}, bf16[2,192,256]{2,1,0:T(8,128)(2,1)S(1)}, u32[]{:S(2)}, u32[]{:S(2)}) collective-permute-start(bf16[2,192,256]{2,1,0:T(8,128)(2,1)} %param.16), channel_id=1, source_target_pairs={{0,1},{1,2},{2,3},{3,4},{4,5},{5,6},{6,7},{7,8},{8,9},{9,10},{10,1... | collective-permute-start | bytes 589832 | tf_op jit(solution)/shard_map/ppermute | solution.py:78
  29.0 9.5 %all-to-all-start = ((bf16[32,8,256]{2,1,0:T(8,128)(2,1)}), bf16[32,8,256]{2,1,0:T(8,128)(2,1)S(1)}, u32[]{:S(2)}, u32[]{:S(2)}) async-start(bf16[32,8,256]{2,1,0:T(8,128)(2,1)} %broadcast_in_dim.54), calls=%async_computation | async-start | bytes 262144 | tf_op jit(solution)/shard_map/all_to_all | solution.py:154
  47.3 2.4 %copy.165 = bf16[2,16,128,256]{2,3,1,0:T(8,128)(2,1)} copy(bf16[2,16,128,256]{3,2,1,0:T(8,128)(2,1)S(1)} %copy-done) | data formatting | bytes 4194304 | tf_op args[10]
  49.6 9.0 %collective-permute-done = bf16[2,192,256]{2,1,0:T(8,128)(2,1)S(1)} collective-permute-done((bf16[2,192,256]{2,1,0:T(8,128)(2,1)}, bf16[2,192,256]{2,1,0:T(8,128)(2,1)S(1)}, u32[]{:S(2)}, u32[]{:S(2)}) %collective-permute-start) | collective-permute-done | bytes 196640 | tf_op jit(solution)/shard_map/ppermute | solution.py:78
  58.7 3.1 %collective-permute-done.3 = bf16[2,192,256]{2,1,0:T(8,128)(2,1)S(1)} collective-permute-done((bf16[2,192,256]{2,1,0:T(8,128)(2,1)}, bf16[2,192,256]{2,1,0:T(8,128)(2,1)S(1)}, u32[]{:S(2)}, u32[]{:S(2)}) %collective-permute-start.3) | collective-permute-done | bytes 196640 | tf_op jit(solution)/shard_map/ppermute | solution.py:78
  65.2 2.5 %broadcast_select_fusion = bf16[2,16,128,256]{2,3,1,0:T(8,128)(2,1)S(1)} fusion(bf16[2,16,128,256]{2,3,1,0:T(8,128)(2,1)} %copy.165, pred[16,128]{1,0:T(8,128)(4,1)S(1)} %fusion.39, bf16[2,16,256]{2,1,0:T(8,128)(2,1)S(1)} %fusion.16), kind=kLoop, calls=%fused_computation.6 | loop fusion | flops 1048576 | bytes 4212736 | tf_op jit(solution)/shard_map/jit(_where)/select_n | solution.py:219
  70.7 9.1 %all-to-all-start.1 = ((f32[32,2,2,2,129]{4,1,3,2,0:T(2,128)}), f32[32,2,2,2,129]{4,1,3,2,0:T(2,128)S(1)}, u32[]{:S(2)}, u32[]{:S(2)}) async-start(f32[32,2,2,2,129]{4,1,3,2,0:T(2,128)} %copy.171), calls=%async_computation.1 | async-start | bytes 524288 | tf_op jit(solution)/shard_map/all_to_all | solution.py:243
  79.7 3.9 %fusion.1 = (f32[192,2,2]{0,2,1:T(2,128)S(1)}, f32[2,960,192,2]{1,2,3,0:T(8,128)}) fusion(pred[192,960]{1,0:T(8,128)(4,1)} %compare_and_fusion, bf16[192,2,2,128]{3,2,1,0:T(2,128)(2,1)S(1)} %reshape.305, bf16[960,2,128,1]{2,1,0,3:T(2,128)(2,1)} %bitcast.83), kind=kOutput, calls=%fused_computation.4 | convolution fusion | flops 191692032 | bytes 3824640 | tf_op jit(solution)/shard_map/qhgd,khd->qhgk/dot_general | solution.py:83
  83.6 16.5 %all-to-all-done.1 = f32[32,2,2,2,129]{4,1,3,2,0:T(2,128)S(1)} async-done(((f32[32,2,2,2,129]{4,1,3,2,0:T(2,128)}), f32[32,2,2,2,129]{4,1,3,2,0:T(2,128)S(1)}, u32[]{:S(2)}, u32[]{:S(2)}) %all-to-all-start.1) | async-done | bytes 132128 | tf_op jit(solution)/shard_map/all_to_all | solution.py:243
  100.4 35.3 %all-gather.3.cloned.1.call-done = bf16[64,2,384,128]{3,2,1,0:T(8,128)(2,1)} async-done(((bf16[2,2,384,128]{3,2,1,0:T(8,128)(2,1)}), bf16[64,2,384,128]{3,2,1,0:T(8,128)(2,1)}) %all-gather.3.cloned.1.call-update) | async-done | bytes 12582928 | tf_op jit(solution)/shard_map/all_gather | solution.py:167
  135.8 21.7 %shard_map.166 = (f32[2,384,128]{2,1,0:T(8,128)}, f32[2,384,1]{2,1,0:T(8,128)}) custom-call(bf16[2,384,128]{2,1,0:T(8,128)(2,1)} %bitcast.81, bf16[32,2,2,384,128]{4,3,2,1,0:T(8,128)(2,1)} %bitcast.76, bf16[32,2,2,384,128]{4,3,2,1,0:T(8,128)(2,1)} %bitcast.77, s32[32,1,384]{2,1,0:T(1,128)} %broadcast_in_dim.64.own_ref, s32[384,1]{1,0:T(8,128)} %broadcast_in_dim_reshape.4.row_ref), custom_call_target="tpu_custom_call" | custom-call | tf_op jit(solution)/shard_map/pallas_call | solution.py:53
  157.5 1.2 reduce.3
  159.0 3.0 %fusion.20 = bf16[192,2,2,128]{3,0,2,1:T(8,128)(2,1)S(1)} fusion(f32[2,960,192,2]{1,2,3,0:T(8,128)} %get-tuple-element.41, pred[192,960]{1,0:T(8,128)(4,1)S(1)} %copy-done.5, bf16[960,2,128,1]{2,1,0,3:T(2,128)(2,1)S(1)} %bitcast.82, f32[2,192,2,128]{3,2,1,0:T(2,128)} %bitcast.89, f32[192,2,2]{0,2,1:T(2,128)S(1)} %bitcast_add_fusion.1), kind=kOutput, calls=%fused_computation.20 | convolution fusion | flops 191987712 | bytes 4217856 | tf_op jit(solution)/shard_map/qhgk,khd->qhgd/dot_general | solution.py:89
  162.3 4.7 %fusion = bf16[4608,194]{0,1:T(8,128)(2,1)} fusion(bf16[512,4608]{1,0:T(8,128)(2,1)} %param.21, bf16[2,512]{1,0:T(2,128)(2,1)S(1)} %bitcast.87, bf16[192,512]{1,0:T(8,128)(2,1)S(1)} %reshape.310), kind=kOutput, calls=%fused_computation.1 | convolution fusion | flops 916698112 | bytes 6705152 | tf_op jit(solution)/shard_map/ko,rk->or/dot_general | solution.py:252
  167.0 4.3 %reshape.319 = bf16[8,576,194]{1,0,2:T(8,128)(2,1)} reshape(bf16[4608,194]{0,1:T(8,128)(2,1)} %fusion) | data formatting | bytes 3575808 | tf_op jit(solution)/shard_map/reshape | solution.py:256
  171.3 1.8 copy.175
  173.1 31.6 %all_to_all.21 = bf16[8,576,194]{1,2,0:T(8,128)(2,1)S(1)} all-to-all(bf16[8,576,194]{1,2,0:T(8,128)(2,1)S(1)} %copy.175), channel_id=1, replica_groups=mesh['kv'=8,'blk'=32] {'kv'}, dimensions={0} | all-to-all | bytes 3575808 | tf_op jit(solution)/shard_map/all_to_all | solution.py:258
  205.8 3.3 %all-to-all-start.3 = ((f32[8,1,194]{2,1,0:T(1,128)}), f32[8,1,194]{2,1,0:T(1,128)S(1)}, u32[]{:S(2)}, u32[]{:S(2)}) async-start(f32[8,1,194]{2,1,0:T(1,128)} %broadcast_in_dim.59), calls=%async_computation.3 | async-start | bytes 16384 | tf_op jit(solution)/shard_map/all_to_all | solution.py:261
  209.2 2.6 %copy.177 = bf16[2,16,128,256]{3,2,1,0:T(8,128)(2,1)} copy(bf16[2,16,128,256]{2,3,1,0:T(8,128)(2,1)S(1)} %broadcast_select_fusion) | data formatting | bytes 4194304
  211.8 3.5 %all-to-all-done.3 = f32[8,1,194]{2,1,0:T(1,128)S(1)} async-done(((f32[8,1,194]{2,1,0:T(1,128)}), f32[8,1,194]{2,1,0:T(1,128)S(1)}, u32[]{:S(2)}, u32[]{:S(2)}) %all-to-all-start.3) | async-done | bytes 6240 | tf_op jit(solution)/shard_map/all_to_all | solution.py:261
  (96 shorter events, 21.3 us)
Async XLA Ops:
  7.2 39.2 %copy-start.3 = (bf16[192,512]{1,0:T(8,128)(2,1)S(1)}, bf16[192,512]{1,0:T(8,128)(2,1)}, u32[]{:S(2)}) copy-start(bf16[192,512]{1,0:T(8,128)(2,1)} %param.15) | copy-start | bytes 589828
  7.2 40.1 %copy-start = (bf16[2,16,128,256]{3,2,1,0:T(8,128)(2,1)S(1)}, bf16[2,16,128,256]{3,2,1,0:T(8,128)(2,1)}, u32[]{:S(2)}) copy-start(bf16[2,16,128,256]{3,2,1,0:T(8,128)(2,1)} %param.25) | copy-start | bytes 6291460
  7.2 128.6 %all-gather.3.cloned.1.call-start = ((), (), s32[]{:S(2)}) async-start(), calls=%async_computation.4 | async-start | bytes 12976128 | tf_op jit(solution)/shard_map/all_gather | solution.py:167
  9.3 49.4 %collective-permute-start.2 = (bf16[2,192,256]{2,1,0:T(8,128)(2,1)}, bf16[2,192,256]{2,1,0:T(8,128)(2,1)S(1)}, u32[]{:S(2)}, u32[]{:S(2)}) collective-permute-start(bf16[2,192,256]{2,1,0:T(8,128)(2,1)} %param.16), channel_id=1, source_target_pairs={{0,2},{1,3},{2,4},{3,5},{4,6},{5,7},{6,8},{7,9},{8,10},{9,11},{10,... | collective-permute-start | bytes 589832 | tf_op jit(solution)/shard_map/ppermute | solution.py:78
  14.5 44.1 %collective-permute-start.1 = (bf16[2,192,256]{2,1,0:T(8,128)(2,1)}, bf16[2,192,256]{2,1,0:T(8,128)(2,1)S(1)}, u32[]{:S(2)}, u32[]{:S(2)}) collective-permute-start(bf16[2,192,256]{2,1,0:T(8,128)(2,1)} %param.16), channel_id=1, source_target_pairs={{0,3},{1,4},{2,5},{3,6},{4,7},{5,8},{6,9},{7,10},{8,11},{9,12},{10... | collective-permute-start | bytes 589832 | tf_op jit(solution)/shard_map/ppermute | solution.py:78
  20.0 38.6 %collective-permute-start = (bf16[2,192,256]{2,1,0:T(8,128)(2,1)}, bf16[2,192,256]{2,1,0:T(8,128)(2,1)S(1)}, u32[]{:S(2)}, u32[]{:S(2)}) collective-permute-start(bf16[2,192,256]{2,1,0:T(8,128)(2,1)} %param.16), channel_id=1, source_target_pairs={{0,4},{1,5},{2,6},{3,7},{4,8},{5,9},{6,10},{7,11},{8,12},{9,13},{1... | collective-permute-start | bytes 589832 | tf_op jit(solution)/shard_map/ppermute | solution.py:78
  23.7 38.0 %collective-permute-start.3 = (bf16[2,192,256]{2,1,0:T(8,128)(2,1)}, bf16[2,192,256]{2,1,0:T(8,128)(2,1)S(1)}, u32[]{:S(2)}, u32[]{:S(2)}) collective-permute-start(bf16[2,192,256]{2,1,0:T(8,128)(2,1)} %param.16), channel_id=1, source_target_pairs={{0,1},{1,2},{2,3},{3,4},{4,5},{5,6},{6,7},{7,8},{8,9},{9,10},{10,1... | collective-permute-start | bytes 589832 | tf_op jit(solution)/shard_map/ppermute | solution.py:78
  29.0 35.6 %all-to-all-start = ((bf16[32,8,256]{2,1,0:T(8,128)(2,1)}), bf16[32,8,256]{2,1,0:T(8,128)(2,1)S(1)}, u32[]{:S(2)}, u32[]{:S(2)}) async-start(bf16[32,8,256]{2,1,0:T(8,128)(2,1)} %broadcast_in_dim.54), calls=%async_computation | async-start | bytes 262144 | tf_op jit(solution)/shard_map/all_to_all | solution.py:154
  46.4 15.3 %copy-start.4 = (bf16[2,192,256]{2,1,0:T(8,128)(2,1)S(1)}, bf16[2,192,256]{2,1,0:T(8,128)(2,1)}, u32[]{:S(2)}) copy-start(bf16[2,192,256]{2,1,0:T(8,128)(2,1)} %param.16) | copy-start | bytes 589828
  70.7 29.5 %all-to-all-start.1 = ((f32[32,2,2,2,129]{4,1,3,2,0:T(2,128)}), f32[32,2,2,2,129]{4,1,3,2,0:T(2,128)S(1)}, u32[]{:S(2)}, u32[]{:S(2)}) async-start(f32[32,2,2,2,129]{4,1,3,2,0:T(2,128)} %copy.171), calls=%async_computation.1 | async-start | bytes 524288 | tf_op jit(solution)/shard_map/all_to_all | solution.py:243
  135.8 23.2 %copy-start.1 = (bf16[960,2,128]{2,1,0:T(2,128)(2,1)S(1)}, bf16[960,2,128]{2,1,0:T(2,128)(2,1)}, u32[]{:S(2)}) copy-start(bf16[960,2,128]{2,1,0:T(2,128)(2,1)} %reshape_squeeze.12) | copy-start | bytes 1474564
  135.8 23.2 %copy-start.5 = (pred[192,960]{1,0:T(8,128)(4,1)S(1)}, pred[192,960]{1,0:T(8,128)(4,1)}, u32[]{:S(2)}) copy-start(pred[192,960]{1,0:T(8,128)(4,1)} %compare_and_fusion) | copy-start | bytes 552964
  204.7 10.6 %copy-start.2 = (bf16[192,576]{1,0:T(8,128)(2,1)S(1)}, bf16[192,576]{1,0:T(8,128)(2,1)}, u32[]{:S(2)}) copy-start(bf16[192,576]{1,0:T(8,128)(2,1)} %param.17) | copy-start | bytes 663556
  204.8 10.6 %copy-start.6 = (f32[576]{0:T(1024)S(1)}, f32[576]{0:T(1024)}, u32[]{:S(2)}) copy-start(f32[576]{0:T(1024)} %param.22) | copy-start | bytes 6916
  204.8 10.6 %copy-start.7 = (bf16[2,576]{1,0:T(2,128)(2,1)S(1)}, bf16[2,576]{1,0:T(2,128)(2,1)}, u32[]{:S(2)}) copy-start(bf16[2,576]{1,0:T(2,128)(2,1)} %param.20) | copy-start | bytes 6916
  205.8 9.5 %all-to-all-start.3 = ((f32[8,1,194]{2,1,0:T(1,128)}), f32[8,1,194]{2,1,0:T(1,128)S(1)}, u32[]{:S(2)}, u32[]{:S(2)}) async-start(f32[8,1,194]{2,1,0:T(1,128)} %broadcast_in_dim.59), calls=%async_computation.3 | async-start | bytes 16384 | tf_op jit(solution)/shard_map/all_to_all | solution.py:261
Sparse Core Ops, SparseCore 0:
  10.5 125.1 all-gather.2

commit v8 on v7

--- a/solution.py
+++ b/solution.py
@@ -166,6 +166,11 @@
     piece = prefix_page_store.reshape(2, held_rows, kv_heads, head_dim).transpose(0, 2, 1, 3)
     gathered = lax.all_gather(piece, "blk", axis=0, tiled=False)
 
+    kv_size = lax.axis_size("kv")
+    out_cols = out_weight.shape[1] // kv_size
+    weight_blocks = out_weight.reshape(out_weight.shape[0], kv_size, out_cols).transpose(1, 0, 2)
+    my_weight = lax.all_to_all(weight_blocks, "kv", 0, 0, tiled=False)
+
     look_back = 4
     pieces_back = [from_behind(suffix_key_value, "blk", d) for d in range(look_back, 0, -1)]
     window = jnp.concatenate(pieces_back + [suffix_key_value], axis=1)
@@ -249,14 +254,11 @@
 
     attention = jnp.concatenate([suffix_attn, decode_attn], axis=0)
     kv_size = lax.axis_size("kv")
-    projected_t = jnp.einsum(
-        "ko,rk->or", out_weight, attention, preferred_element_type=jnp.float32
-    )
     residual = jnp.concatenate([suffix_resid, decode_resid], axis=0).astype(jnp.float32)
-    shares = projected_t.astype(jnp.bfloat16).reshape(kv_size, -1, projected_t.shape[1])
-    mine = jnp.sum(
-        lax.all_to_all(shares, "kv", 0, 0, tiled=False).astype(jnp.float32), axis=0
-    ).T
+    heard = lax.all_to_all(
+        jnp.broadcast_to(attention[None], (kv_size,) + attention.shape), "kv", 0, 0, tiled=False
+    )
+    mine = jnp.einsum("srk,sko->ro", heard, my_weight, preferred_element_type=jnp.float32)
     squares = jnp.sum(mine * mine, axis=1)
     square_parts = lax.all_to_all(
         jnp.broadcast_to(squares[None], (kv_size,) + squares.shape), "kv", 0, 0, tiled=False

time: 224 us -> 274 us (1.22)
  waiting for transfers between devices: 68.3 us -> 123 us
  blocking collectives: 31.6 us -> 26.3 us
    ppermute x4, waiting for transfers between devices: 12.1 us -> 111 us  [from_behind(): return lax.ppermute(block, axis, route)]
    all_gather x1, waiting for transfers between devices: 35.3 us -> 0.01 us  [body(): gathered = lax.all_gather(piece, 'blk', axis=0, tiled=False)]
    all_to_all x1, waiting for transfers between devices: 16.5 us -> 4.21 us  [body(): lax.all_to_all(slot_sums, 'blk', 0, 0, tiled=False)]
    unnamed x23 -> x30, local copies, waits for them, and re-layouts: 5.06 us -> 13.6 us
    reshape x2 -> x0, local copies, waits for them, and re-layouts: 6.1 us -> none  [body(): projected_t.astype(jnp.bfloat16).reshape(kv_size, -1, projected_t.shape[1])]
    all_to_all x1, blocking collectives: 31.6 us -> 26.3 us  [body(): lax.all_to_all(jnp.broadcast_to(attention[None], (kv_size,) + attention.s...]
    all_to_all x0 -> x1, starting transfers between devices: none -> 5.14 us  [body(): my_weight = lax.all_to_all(weight_blocks, 'kv', 0, 0, tiled=False)]
    all_to_all x1, waiting for transfers between devices: 0.87 us -> 4.96 us  [body(): lax.all_to_all(jnp.broadcast_to(dec_local[None], (blk_size,) + dec_local....]
  transfers between devices with their start and end apart: 8 -> 9, of which waited for: 6 -> 4; matrix products, arithmetic and copies ran while one was open for 12% -> 14% of each run, Pallas kernels for 0% -> 8%
where the time goes in v8:
time: 274 us; the launch traced here: 273 us
  waiting for transfers between devices  123 us (45%)
  starting transfers between devices  40.8 us (15%)
  blocking collectives  26.3 us (10%)
  local copies, waits for them, and re-layouts  25.9 us (9%)
  Pallas kernels  21.7 us (8%)
  between operations  14.5 us (5%)
  matrix products  12.8 us (5%)
  other arithmetic  7.34 us (3%)
    ppermute x4, waiting for transfers between devices, from_behind(): return lax.ppermute(block, axis, route)  111 us
    all_to_all x1, blocking collectives, body(): lax.all_to_all(jnp.broadcast_to(attention[None], (kv_size,) + attention.s...  26.3 us
    pallas_call x1, Pallas kernels, prefix_attention(): pl.pallas_call(kern, grid=(heads, steps), in_specs=[pl.BlockSpec((1, rows...  21.7 us
    ppermute x4, starting transfers between devices, from_behind(): return lax.ppermute(block, axis, route)  15.5 us
    unnamed x30, local copies, waits for them, and re-layouts  13.6 us
    all_to_all x1, starting transfers between devices, body(): lax.all_to_all(jnp.broadcast_to(dec_local[None], (blk_size,) + dec_local....  11.6 us
  transfers between devices with their start and end apart: 9, of which 4 were waited for; matrix products, arithmetic and copies ran while one was open for 14% of the time, Pallas kernels for 8%

profile of v8, /device:TPU:2, one launch (start us, length us, event | category | flops | bytes accessed | tf_op | source)
XLA Modules:
  0.0 272.9 jit_solution(1904649617351662147)
XLA Ops:
  7.2 1.2 reshape.308
  11.4 11.6 %all-to-all-start = ((bf16[32,8,256]{2,1,0:T(8,128)(2,1)}), bf16[32,8,256]{2,1,0:T(8,128)(2,1)S(1)}, u32[]{:S(2)}, u32[]{:S(2)}) async-start(bf16[32,8,256]{2,1,0:T(8,128)(2,1)} %broadcast_in_dim.56), calls=%async_computation | async-start | bytes 262144 | tf_op jit(solution)/shard_map/all_to_all | solution.py:154
  24.9 2.4 copy.169
  27.3 5.0 %all-to-all-done = bf16[32,8,256]{2,1,0:T(8,128)(2,1)S(1)} async-done(((bf16[32,8,256]{2,1,0:T(8,128)(2,1)}), bf16[32,8,256]{2,1,0:T(8,128)(2,1)S(1)}, u32[]{:S(2)}, u32[]{:S(2)}) %all-to-all-start) | async-done | bytes 131104 | tf_op jit(solution)/shard_map/all_to_all | solution.py:154
  32.9 2.5 broadcast_select_fusion
  38.4 5.2 %all-to-all-start.1 = ((f32[32,2,2,2,129]{4,1,3,2,0:T(2,128)}), f32[32,2,2,2,129]{4,1,3,2,0:T(2,128)S(1)}, u32[]{:S(2)}, u32[]{:S(2)}) async-start(f32[32,2,2,2,129]{4,1,3,2,0:T(2,128)} %copy.175), calls=%async_computation.1 | async-start | bytes 524288 | tf_op jit(solution)/shard_map/all_to_all | solution.py:248
  43.6 6.7 %copy.179 = bf16[512,4608]{0,1:T(8,128)(2,1)} copy(bf16[512,4608]{1,0:T(8,128)(2,1)} %param.21) | data formatting | bytes 9437184 | tf_op args[6]
  50.3 4.2 %all-to-all-done.1 = f32[32,2,2,2,129]{4,1,3,2,0:T(2,128)S(1)} async-done(((f32[32,2,2,2,129]{4,1,3,2,0:T(2,128)}), f32[32,2,2,2,129]{4,1,3,2,0:T(2,128)S(1)}, u32[]{:S(2)}, u32[]{:S(2)}) %all-to-all-start.1) | async-done | bytes 132128 | tf_op jit(solution)/shard_map/all_to_all | solution.py:248
  54.5 5.1 %all-to-all-start.3 = ((bf16[8,512,576]{1,2,0:T(8,128)(2,1)}), bf16[8,512,576]{1,2,0:T(8,128)(2,1)}, u32[]{:S(2)}, u32[]{:S(2)}) async-start(bf16[8,512,576]{1,2,0:T(8,128)(2,1)} %bitcast.76), calls=%async_computation.3 | async-start | bytes 9437184 | tf_op jit(solution)/shard_map/all_to_all | solution.py:172
  59.7 3.5 %collective-permute-start.2 = (bf16[2,192,256]{2,1,0:T(8,128)(2,1)S(1)}, bf16[2,192,256]{2,1,0:T(8,128)(2,1)S(1)}, u32[]{:S(2)}, u32[]{:S(2)}) collective-permute-start(bf16[2,192,256]{2,1,0:T(8,128)(2,1)S(1)} %copy-done.4), channel_id=1, source_target_pairs={{0,2},{1,3},{2,4},{3,5},{4,6},{5,7},{6,8},{7,9},{8,10},{9,11},{10,... | collective-permute-start | bytes 589832 | tf_op jit(solution)/shard_map/ppermute | solution.py:78
  63.1 2.9 %collective-permute-start.1 = (bf16[2,192,256]{2,1,0:T(8,128)(2,1)S(1)}, bf16[2,192,256]{2,1,0:T(8,128)(2,1)}, u32[]{:S(2)}, u32[]{:S(2)}) collective-permute-start(bf16[2,192,256]{2,1,0:T(8,128)(2,1)S(1)} %copy-done.4), channel_id=1, source_target_pairs={{0,3},{1,4},{2,5},{3,6},{4,7},{5,8},{6,9},{7,10},{8,11},{9,12},{10... | collective-permute-start | bytes 589832 | tf_op jit(solution)/shard_map/ppermute | solution.py:78
  66.1 7.0 %collective-permute-start = (bf16[2,192,256]{2,1,0:T(8,128)(2,1)S(1)}, bf16[2,192,256]{2,1,0:T(8,128)(2,1)}, u32[]{:S(2)}, u32[]{:S(2)}) collective-permute-start(bf16[2,192,256]{2,1,0:T(8,128)(2,1)S(1)} %copy-done.4), channel_id=1, source_target_pairs={{0,4},{1,5},{2,6},{3,7},{4,8},{5,9},{6,10},{7,11},{8,12},{9,13},{1... | collective-permute-start | bytes 589832 | tf_op jit(solution)/shard_map/ppermute | solution.py:78
  73.1 2.1 collective-permute-start.3
  79.4 110.7 %collective-permute-done = bf16[2,192,256]{2,1,0:T(8,128)(2,1)} collective-permute-done((bf16[2,192,256]{2,1,0:T(8,128)(2,1)S(1)}, bf16[2,192,256]{2,1,0:T(8,128)(2,1)}, u32[]{:S(2)}, u32[]{:S(2)}) %collective-permute-start) | collective-permute-done | bytes 196640 | tf_op jit(solution)/shard_map/ppermute | solution.py:78
  191.0 0.9 constant_dynamic-update-slice_fusion.3
  193.1 3.7 %fusion = (f32[192,2,2]{0,2,1:T(2,128)S(1)}, f32[2,960,192,2]{1,2,3,0:T(8,128)}) fusion(pred[192,960]{1,0:T(8,128)(4,1)} %compare_and_fusion, bf16[192,2,2,128]{3,2,1,0:T(2,128)(2,1)S(1)} %reshape.306, bf16[960,2,128,1]{2,1,0,3:T(2,128)(2,1)S(1)} %bitcast.82), kind=kOutput, calls=%fused_computation.1 | convolution fusion | flops 191692032 | bytes 3824640 | tf_op jit(solution)/shard_map/qhgd,khd->qhgk/dot_general | solution.py:83
  197.2 21.7 %shard_map.166 = (f32[2,384,128]{2,1,0:T(8,128)}, f32[2,384,1]{2,1,0:T(8,128)}) custom-call(bf16[2,384,128]{2,1,0:T(8,128)(2,1)} %bitcast.80, bf16[32,2,2,384,128]{4,3,2,1,0:T(8,128)(2,1)} %bitcast.74, bf16[32,2,2,384,128]{4,3,2,1,0:T(8,128)(2,1)} %bitcast.75, s32[32,1,384]{2,1,0:T(1,128)} %broadcast_in_dim.67.own_ref, s32[384,1]{1,0:T(8,128)} %broadcast_in_dim_reshape.4.row_ref), custom_call_target="tpu_custom_call" | custom-call | tf_op jit(solution)/shard_map/pallas_call | solution.py:53
  219.0 1.2 reduce.2
  220.5 3.0 %fusion.19 = bf16[192,2,2,128]{3,0,2,1:T(8,128)(2,1)S(1)} fusion(f32[2,960,192,2]{1,2,3,0:T(8,128)} %get-tuple-element.41, pred[192,960]{1,0:T(8,128)(4,1)S(1)} %copy-done.5, bf16[960,2,128,1]{2,1,0,3:T(2,128)(2,1)S(1)} %bitcast.81, f32[2,192,2,128]{3,2,1,0:T(2,128)} %bitcast.88, f32[192,2,2]{0,2,1:T(2,128)S(1)} %bitcast_add_fusion), kind=kOutput, calls=%fused_computation.18 | convolution fusion | flops 191987712 | bytes 4217856 | tf_op jit(solution)/shard_map/qhgk,khd->qhgd/dot_general | solution.py:89
  223.9 26.3 %all_to_all.26 = bf16[8,194,512]{2,1,0:T(8,128)(2,1)S(1)} all-to-all(bf16[8,194,512]{2,1,0:T(8,128)(2,1)S(1)} %broadcast_in_dim.65), channel_id=1, replica_groups=mesh['kv'=8,'blk'=32] {'kv'}, dimensions={0} | all-to-all | bytes 3178496 | tf_op jit(solution)/shard_map/all_to_all | solution.py:258
  250.2 4.2 %multiply_reduce_fusion = (f32[194]{0:T(256)S(1)}, f32[194,576]{1,0:T(8,128)S(1)}) fusion(bf16[8,194,512]{2,1,0:T(8,128)(2,1)S(1)} %all_to_all.26, bf16[8,512,576]{1,2,0:T(8,128)(2,1)} %all-to-all-done.3), kind=kOutput, calls=%fused_computation.21 | convolution fusion | flops 915630144 | bytes 6755592 | tf_op jit(solution)/shard_map/srk,sko->ro/dot_general | solution.py:261
  255.1 3.3 %all-to-all-start.4 = ((f32[8,1,194]{2,1,0:T(1,128)}), f32[8,1,194]{2,1,0:T(1,128)S(1)}, u32[]{:S(2)}, u32[]{:S(2)}) async-start(f32[8,1,194]{2,1,0:T(1,128)} %broadcast_in_dim.66), calls=%async_computation.4 | async-start | bytes 16384 | tf_op jit(solution)/shard_map/all_to_all | solution.py:263
  258.5 2.6 copy.181
  261.1 3.5 %all-to-all-done.4 = f32[8,1,194]{2,1,0:T(1,128)S(1)} async-done(((f32[8,1,194]{2,1,0:T(1,128)}), f32[8,1,194]{2,1,0:T(1,128)S(1)}, u32[]{:S(2)}, u32[]{:S(2)}) %all-to-all-start.4) | async-done | bytes 6240 | tf_op jit(solution)/shard_map/all_to_all | solution.py:263
  (103 shorter events, 17.7 us)
Async XLA Ops:
  7.2 17.7 %copy-start = (bf16[2,16,128,256]{3,2,1,0:T(8,128)(2,1)S(1)}, bf16[2,16,128,256]{3,2,1,0:T(8,128)(2,1)}, u32[]{:S(2)}) copy-start(bf16[2,16,128,256]{3,2,1,0:T(8,128)(2,1)} %param.25) | copy-start | bytes 6291460
  7.2 190.0 %all-gather.3.cloned.1.call-start = ((), (), s32[]{:S(2)}) async-start(), calls=%async_computation.5 | async-start | bytes 12976128 | tf_op jit(solution)/shard_map/all_gather | solution.py:167
  11.4 20.9 %all-to-all-start = ((bf16[32,8,256]{2,1,0:T(8,128)(2,1)}), bf16[32,8,256]{2,1,0:T(8,128)(2,1)S(1)}, u32[]{:S(2)}, u32[]{:S(2)}) async-start(bf16[32,8,256]{2,1,0:T(8,128)(2,1)} %broadcast_in_dim.56), calls=%async_computation | async-start | bytes 262144 | tf_op jit(solution)/shard_map/all_to_all | solution.py:154
  38.4 16.1 %all-to-all-start.1 = ((f32[32,2,2,2,129]{4,1,3,2,0:T(2,128)}), f32[32,2,2,2,129]{4,1,3,2,0:T(2,128)S(1)}, u32[]{:S(2)}, u32[]{:S(2)}) async-start(f32[32,2,2,2,129]{4,1,3,2,0:T(2,128)} %copy.175), calls=%async_computation.1 | async-start | bytes 524288 | tf_op jit(solution)/shard_map/all_to_all | solution.py:248
  54.5 5.2 %copy-start.4 = (bf16[2,192,256]{2,1,0:T(8,128)(2,1)S(1)}, bf16[2,192,256]{2,1,0:T(8,128)(2,1)}, u32[]{:S(2)}) copy-start(bf16[2,192,256]{2,1,0:T(8,128)(2,1)} %param.16) | copy-start | bytes 589828
  54.5 20.7 %copy-start.10 = (s32[96]{0:T(128)S(1)}, s32[96]{0:T(128)}, u32[]{:S(2)}) copy-start(s32[96]{0:T(128)} %param.24) | copy-start | bytes 1156
  54.5 20.9 %copy-start.8 = (s32[16]{0:T(128)S(1)}, s32[16]{0:T(128)}, u32[]{:S(2)}) copy-start(s32[16]{0:T(128)} %param.27) | copy-start | bytes 196
  54.5 21.3 %copy-start.9 = (s32[16]{0:T(128)S(1)}, s32[16]{0:T(128)}, u32[]{:S(2)}) copy-start(s32[16]{0:T(128)} %param.28) | copy-start | bytes 196
  54.5 24.0 %copy-start.3 = (bf16[192,512]{1,0:T(8,128)(2,1)S(1)}, bf16[192,512]{1,0:T(8,128)(2,1)}, u32[]{:S(2)}) copy-start(bf16[192,512]{1,0:T(8,128)(2,1)} %param.15) | copy-start | bytes 589828
  54.5 169.2 %all-to-all-start.3 = ((bf16[8,512,576]{1,2,0:T(8,128)(2,1)}), bf16[8,512,576]{1,2,0:T(8,128)(2,1)}, u32[]{:S(2)}, u32[]{:S(2)}) async-start(bf16[8,512,576]{1,2,0:T(8,128)(2,1)} %bitcast.76), calls=%async_computation.3 | async-start | bytes 9437184 | tf_op jit(solution)/shard_map/all_to_all | solution.py:172
  59.7 132.3 %collective-permute-start.2 = (bf16[2,192,256]{2,1,0:T(8,128)(2,1)S(1)}, bf16[2,192,256]{2,1,0:T(8,128)(2,1)S(1)}, u32[]{:S(2)}, u32[]{:S(2)}) collective-permute-start(bf16[2,192,256]{2,1,0:T(8,128)(2,1)S(1)} %copy-done.4), channel_id=1, source_target_pairs={{0,2},{1,3},{2,4},{3,5},{4,6},{5,7},{6,8},{7,9},{8,10},{9,11},{10,... | collective-permute-start | bytes 589832 | tf_op jit(solution)/shard_map/ppermute | solution.py:78
  63.1 127.9 %collective-permute-start.1 = (bf16[2,192,256]{2,1,0:T(8,128)(2,1)S(1)}, bf16[2,192,256]{2,1,0:T(8,128)(2,1)}, u32[]{:S(2)}, u32[]{:S(2)}) collective-permute-start(bf16[2,192,256]{2,1,0:T(8,128)(2,1)S(1)} %copy-done.4), channel_id=1, source_target_pairs={{0,3},{1,4},{2,5},{3,6},{4,7},{5,8},{6,9},{7,10},{8,11},{9,12},{10... | collective-permute-start | bytes 589832 | tf_op jit(solution)/shard_map/ppermute | solution.py:78
  66.1 124.0 %collective-permute-start = (bf16[2,192,256]{2,1,0:T(8,128)(2,1)S(1)}, bf16[2,192,256]{2,1,0:T(8,128)(2,1)}, u32[]{:S(2)}, u32[]{:S(2)}) collective-permute-start(bf16[2,192,256]{2,1,0:T(8,128)(2,1)S(1)} %copy-done.4), channel_id=1, source_target_pairs={{0,4},{1,5},{2,6},{3,7},{4,8},{5,9},{6,10},{7,11},{8,12},{9,13},{1... | collective-permute-start | bytes 589832 | tf_op jit(solution)/shard_map/ppermute | solution.py:78
  73.1 118.9 %collective-permute-start.3 = (bf16[2,192,256]{2,1,0:T(8,128)(2,1)S(1)}, bf16[2,192,256]{2,1,0:T(8,128)(2,1)S(1)}, u32[]{:S(2)}, u32[]{:S(2)}) collective-permute-start(bf16[2,192,256]{2,1,0:T(8,128)(2,1)S(1)} %copy-done.4), channel_id=1, source_target_pairs={{0,1},{1,2},{2,3},{3,4},{4,5},{5,6},{6,7},{7,8},{8,9},{9,10},{10,1... | collective-permute-start | bytes 589832 | tf_op jit(solution)/shard_map/ppermute | solution.py:78
  197.2 23.2 %copy-start.1 = (bf16[960,2,128]{2,1,0:T(2,128)(2,1)S(1)}, bf16[960,2,128]{2,1,0:T(2,128)(2,1)}, u32[]{:S(2)}) copy-start(bf16[960,2,128]{2,1,0:T(2,128)(2,1)} %reshape_squeeze.12) | copy-start | bytes 1474564
  197.2 23.2 %copy-start.5 = (pred[192,960]{1,0:T(8,128)(4,1)S(1)}, pred[192,960]{1,0:T(8,128)(4,1)}, u32[]{:S(2)}) copy-start(pred[192,960]{1,0:T(8,128)(4,1)} %compare_and_fusion) | copy-start | bytes 552964
  254.5 10.1 %copy-start.2 = (bf16[192,576]{1,0:T(8,128)(2,1)S(1)}, bf16[192,576]{1,0:T(8,128)(2,1)}, u32[]{:S(2)}) copy-start(bf16[192,576]{1,0:T(8,128)(2,1)} %param.17) | copy-start | bytes 663556
  254.5 10.1 %copy-start.6 = (f32[576]{0:T(1024)S(1)}, f32[576]{0:T(1024)}, u32[]{:S(2)}) copy-start(f32[576]{0:T(1024)} %param.22) | copy-start | bytes 6916
  254.5 10.1 %copy-start.7 = (bf16[2,576]{1,0:T(2,128)(2,1)S(1)}, bf16[2,576]{1,0:T(2,128)(2,1)}, u32[]{:S(2)}) copy-start(bf16[2,576]{1,0:T(2,128)(2,1)} %param.20) | copy-start | bytes 6916
  255.1 9.5 %all-to-all-start.4 = ((f32[8,1,194]{2,1,0:T(1,128)}), f32[8,1,194]{2,1,0:T(1,128)S(1)}, u32[]{:S(2)}, u32[]{:S(2)}) async-start(f32[8,1,194]{2,1,0:T(1,128)} %broadcast_in_dim.66), calls=%async_computation.4 | async-start | bytes 16384 | tf_op jit(solution)/shard_map/all_to_all | solution.py:263
Sparse Core Ops, SparseCore 0:
  10.5 133.1 all-gather.2

commit v9 on v8

--- a/solution.py
+++ b/solution.py
@@ -166,14 +166,15 @@
     piece = prefix_page_store.reshape(2, held_rows, kv_heads, head_dim).transpose(0, 2, 1, 3)
     gathered = lax.all_gather(piece, "blk", axis=0, tiled=False)
 
+    look_back = 4
+    pieces_back = [from_behind(suffix_key_value, "blk", d) for d in range(look_back, 0, -1)]
+    window = jnp.concatenate(pieces_back + [suffix_key_value], axis=1)
+
     kv_size = lax.axis_size("kv")
     out_cols = out_weight.shape[1] // kv_size
     weight_blocks = out_weight.reshape(out_weight.shape[0], kv_size, out_cols).transpose(1, 0, 2)
+    weight_blocks, window = lax.optimization_barrier((weight_blocks, window))
     my_weight = lax.all_to_all(weight_blocks, "kv", 0, 0, tiled=False)
-
-    look_back = 4
-    pieces_back = [from_behind(suffix_key_value, "blk", d) for d in range(look_back, 0, -1)]
-    window = jnp.concatenate(pieces_back + [suffix_key_value], axis=1)
 
     own_queries = suffix_query.reshape(tok_rows, kv_heads, query_group_width, head_dim)
     token_ids = my_index * tok_rows + jnp.arange(tok_rows, dtype=jnp.int32)

time: 274 us -> 233 us (0.85)
  waiting for transfers between devices: 123 us -> 77.5 us
  local copies, waits for them, and re-layouts: 25.9 us -> 29.1 us
  starting transfers between devices: 40.8 us -> 44 us
    ppermute x4, waiting for transfers between devices: 111 us -> 9.12 us  [from_behind(): return lax.ppermute(block, axis, route)]
    all_gather x1, waiting for transfers between devices: 0.01 us -> 37.1 us  [body(): gathered = lax.all_gather(piece, 'blk', axis=0, tiled=False)]
    all_to_all x1, waiting for transfers between devices: 4.21 us -> 15.1 us  [body(): lax.all_to_all(slot_sums, 'blk', 0, 0, tiled=False)]
    all_to_all x1, waiting for transfers between devices: 0.01 us -> 6.81 us  [body(): my_weight = lax.all_to_all(weight_blocks, 'kv', 0, 0, tiled=False)]
    all_to_all x1, starting transfers between devices: 5.21 us -> 8.25 us  [body(): lax.all_to_all(slot_sums, 'blk', 0, 0, tiled=False)]
    unnamed x30 -> x32, local copies, waits for them, and re-layouts: 13.6 us -> 14.9 us
  transfers between devices with their start and end apart: 9 -> 9, of which waited for: 4 -> 6; matrix products, arithmetic and copies ran while one was open for 14% -> 17% of each run, Pallas kernels for 8% -> 9%
where the time goes in v9:
time: 233 us; the launch traced here: 232 us
  waiting for transfers between devices  77.5 us (33%)
  starting transfers between devices  44 us (19%)
  local copies, waits for them, and re-layouts  29.1 us (12%)
  blocking collectives  25.4 us (11%)
  Pallas kernels  21.7 us (9%)
  between operations  14.5 us (6%)
  matrix products  12.8 us (5%)
  other arithmetic  7.31 us (3%)
    all_gather x1, waiting for transfers between devices, body(): gathered = lax.all_gather(piece, 'blk', axis=0, tiled=False)  37.1 us
    all_to_all x1, blocking collectives, body(): lax.all_to_all(jnp.broadcast_to(attention[None], (kv_size,) + attention.s...  25.4 us
    pallas_call x1, Pallas kernels, prefix_attention(): pl.pallas_call(kern, grid=(heads, steps), in_specs=[pl.BlockSpec((1, rows...  21.7 us
    ppermute x4, starting transfers between devices, from_behind(): return lax.ppermute(block, axis, route)  17.6 us
    all_to_all x1, waiting for transfers between devices, body(): lax.all_to_all(slot_sums, 'blk', 0, 0, tiled=False)  15.1 us
    unnamed x32, local copies, waits for them, and re-layouts  14.9 us
    all_to_all x1, starting transfers between devices, body(): lax.all_to_all(jnp.broadcast_to(dec_local[None], (blk_size,) + dec_local....  9.53 us
    ppermute x4, waiting for transfers between devices, from_behind(): return lax.ppermute(block, axis, route)  9.12 us
  transfers between devices with their start and end apart: 9, of which 6 were waited for; matrix products, arithmetic and copies ran while one was open for 17% of the time, Pallas kernels for 9%

profile of v9, /device:TPU:2, one launch (start us, length us, event | category | flops | bytes accessed | tf_op | source)
XLA Modules:
  0.0 232.3 jit_solution(17809920285975215857)
XLA Ops:
  9.3 5.2 %collective-permute-start.2 = (bf16[2,192,256]{2,1,0:T(8,128)(2,1)}, bf16[2,192,256]{2,1,0:T(8,128)(2,1)}, u32[]{:S(2)}, u32[]{:S(2)}) collective-permute-start(bf16[2,192,256]{2,1,0:T(8,128)(2,1)} %param.16), channel_id=1, source_target_pairs={{0,2},{1,3},{2,4},{3,5},{4,6},{5,7},{6,8},{7,9},{8,10},{9,11},{10,... | collective-permute-start | bytes 589832 | tf_op jit(solution)/shard_map/ppermute | solution.py:78
  14.5 5.6 %collective-permute-start.1 = (bf16[2,192,256]{2,1,0:T(8,128)(2,1)}, bf16[2,192,256]{2,1,0:T(8,128)(2,1)S(1)}, u32[]{:S(2)}, u32[]{:S(2)}) collective-permute-start(bf16[2,192,256]{2,1,0:T(8,128)(2,1)} %param.16), channel_id=1, source_target_pairs={{0,3},{1,4},{2,5},{3,6},{4,7},{5,8},{6,9},{7,10},{8,11},{9,12},{10... | collective-permute-start | bytes 589832 | tf_op jit(solution)/shard_map/ppermute | solution.py:78
  20.1 3.7 %collective-permute-start = (bf16[2,192,256]{2,1,0:T(8,128)(2,1)}, bf16[2,192,256]{2,1,0:T(8,128)(2,1)S(1)}, u32[]{:S(2)}, u32[]{:S(2)}) collective-permute-start(bf16[2,192,256]{2,1,0:T(8,128)(2,1)} %param.16), channel_id=1, source_target_pairs={{0,4},{1,5},{2,6},{3,7},{4,8},{5,9},{6,10},{7,11},{8,12},{9,13},{1... | collective-permute-start | bytes 589832 | tf_op jit(solution)/shard_map/ppermute | solution.py:78
  23.8 3.2 %collective-permute-start.3 = (bf16[2,192,256]{2,1,0:T(8,128)(2,1)}, bf16[2,192,256]{2,1,0:T(8,128)(2,1)}, u32[]{:S(2)}, u32[]{:S(2)}) collective-permute-start(bf16[2,192,256]{2,1,0:T(8,128)(2,1)} %param.16), channel_id=1, source_target_pairs={{0,1},{1,2},{2,3},{3,4},{4,5},{5,6},{6,7},{7,8},{8,9},{9,10},{10,1... | collective-permute-start | bytes 589832 | tf_op jit(solution)/shard_map/ppermute | solution.py:78
  29.0 9.5 %all-to-all-start = ((bf16[32,8,256]{2,1,0:T(8,128)(2,1)}), bf16[32,8,256]{2,1,0:T(8,128)(2,1)S(1)}, u32[]{:S(2)}, u32[]{:S(2)}) async-start(bf16[32,8,256]{2,1,0:T(8,128)(2,1)} %broadcast_in_dim.56), calls=%async_computation | async-start | bytes 262144 | tf_op jit(solution)/shard_map/all_to_all | solution.py:154
  40.5 2.4 %copy.170 = bf16[2,16,128,256]{2,3,1,0:T(8,128)(2,1)} copy(bf16[2,16,128,256]{3,2,1,0:T(8,128)(2,1)S(1)} %copy-done) | data formatting | bytes 4194304 | tf_op args[10]
  42.9 6.6 %copy.156 = bf16[512,4608]{0,1:T(8,128)(2,1)} copy(bf16[512,4608]{1,0:T(8,128)(2,1)} %param.21) | data formatting | bytes 9437184 | tf_op args[6]
  49.5 9.1 %collective-permute-done = bf16[2,192,256]{2,1,0:T(8,128)(2,1)S(1)} collective-permute-done((bf16[2,192,256]{2,1,0:T(8,128)(2,1)}, bf16[2,192,256]{2,1,0:T(8,128)(2,1)S(1)}, u32[]{:S(2)}, u32[]{:S(2)}) %collective-permute-start) | collective-permute-done | bytes 196640 | tf_op jit(solution)/shard_map/ppermute | solution.py:78
  58.7 5.9 %all-to-all-done = bf16[32,8,256]{2,1,0:T(8,128)(2,1)S(1)} async-done(((bf16[32,8,256]{2,1,0:T(8,128)(2,1)}), bf16[32,8,256]{2,1,0:T(8,128)(2,1)S(1)}, u32[]{:S(2)}, u32[]{:S(2)}) %all-to-all-start) | async-done | bytes 131104 | tf_op jit(solution)/shard_map/all_to_all | solution.py:154
  65.2 2.5 %broadcast_select_fusion = bf16[2,16,128,256]{2,3,1,0:T(8,128)(2,1)S(1)} fusion(bf16[2,16,128,256]{2,3,1,0:T(8,128)(2,1)} %copy.170, pred[16,128]{1,0:T(8,128)(4,1)S(1)} %fusion.34, bf16[2,16,256]{2,1,0:T(8,128)(2,1)S(1)} %fusion.15), kind=kLoop, calls=%fused_computation.3 | loop fusion | flops 1048576 | bytes 4212736 | tf_op jit(solution)/shard_map/jit(_where)/select_n | solution.py:225
  70.7 8.2 %all-to-all-start.1 = ((f32[32,2,2,2,129]{4,1,3,2,0:T(2,128)}), f32[32,2,2,2,129]{4,1,3,2,0:T(2,128)S(1)}, u32[]{:S(2)}, u32[]{:S(2)}) async-start(f32[32,2,2,2,129]{4,1,3,2,0:T(2,128)} %copy.176), calls=%async_computation.1 | async-start | bytes 524288 | tf_op jit(solution)/shard_map/all_to_all | solution.py:249
  78.9 1.6 constant_dynamic-update-slice_fusion.2
  82.9 15.1 %all-to-all-done.1 = f32[32,2,2,2,129]{4,1,3,2,0:T(2,128)S(1)} async-done(((f32[32,2,2,2,129]{4,1,3,2,0:T(2,128)}), f32[32,2,2,2,129]{4,1,3,2,0:T(2,128)S(1)}, u32[]{:S(2)}, u32[]{:S(2)}) %all-to-all-start.1) | async-done | bytes 132128 | tf_op jit(solution)/shard_map/all_to_all | solution.py:249
  97.9 5.2 %all-to-all-start.3 = ((bf16[8,512,576]{1,2,0:T(8,128)(2,1)}), bf16[8,512,576]{1,2,0:T(8,128)(2,1)}, u32[]{:S(2)}, u32[]{:S(2)}) async-start(bf16[8,512,576]{1,2,0:T(8,128)(2,1)} %bitcast.76), calls=%async_computation.3 | async-start | bytes 9437184 | tf_op jit(solution)/shard_map/all_to_all | solution.py:177
  109.6 3.7 %fusion = (f32[192,2,2]{0,2,1:T(2,128)S(1)}, f32[2,960,192,2]{1,2,3,0:T(8,128)}) fusion(pred[192,960]{1,0:T(8,128)(4,1)} %compare_and_fusion, bf16[192,2,2,128]{3,2,1,0:T(2,128)(2,1)S(1)} %reshape.307, bf16[960,2,128,1]{2,1,0,3:T(2,128)(2,1)S(1)} %bitcast.82), kind=kOutput, calls=%fused_computation.1 | convolution fusion | flops 191692032 | bytes 3824640 | tf_op jit(solution)/shard_map/qhgd,khd->qhgk/dot_general | solution.py:83
  113.6 37.1 %all-gather.3.cloned.1.call-done = bf16[64,2,384,128]{3,2,1,0:T(8,128)(2,1)} async-done(((bf16[2,2,384,128]{3,2,1,0:T(8,128)(2,1)}), bf16[64,2,384,128]{3,2,1,0:T(8,128)(2,1)}) %all-gather.3.cloned.1.call-update) | async-done | bytes 12582928 | tf_op jit(solution)/shard_map/all_gather | solution.py:167
  150.7 21.7 %shard_map.166 = (f32[2,384,128]{2,1,0:T(8,128)}, f32[2,384,1]{2,1,0:T(8,128)}) custom-call(bf16[2,384,128]{2,1,0:T(8,128)(2,1)} %bitcast.80, bf16[32,2,2,384,128]{4,3,2,1,0:T(8,128)(2,1)} %bitcast.74, bf16[32,2,2,384,128]{4,3,2,1,0:T(8,128)(2,1)} %bitcast.75, s32[32,1,384]{2,1,0:T(1,128)} %broadcast_in_dim.67.own_ref, s32[384,1]{1,0:T(8,128)} %broadcast_in_dim_reshape.4.row_ref), custom_call_target="tpu_custom_call" | custom-call | tf_op jit(solution)/shard_map/pallas_call | solution.py:53
  174.0 3.0 %fusion.19 = bf16[192,2,2,128]{3,0,2,1:T(8,128)(2,1)S(1)} fusion(f32[2,960,192,2]{1,2,3,0:T(8,128)} %get-tuple-element.45, pred[192,960]{1,0:T(8,128)(4,1)S(1)} %copy-done.6, bf16[960,2,128,1]{2,1,0,3:T(2,128)(2,1)S(1)} %bitcast.81, f32[2,192,2,128]{3,2,1,0:T(2,128)} %bitcast.88, f32[192,2,2]{0,2,1:T(2,128)S(1)} %bitcast_add_fusion), kind=kOutput, calls=%fused_computation.18 | convolution fusion | flops 191987712 | bytes 4217856 | tf_op jit(solution)/shard_map/qhgk,khd->qhgd/dot_general | solution.py:89
  177.3 6.8 %all-to-all-done.3 = bf16[8,512,576]{1,2,0:T(8,128)(2,1)} async-done(((bf16[8,512,576]{1,2,0:T(8,128)(2,1)}), bf16[8,512,576]{1,2,0:T(8,128)(2,1)}, u32[]{:S(2)}, u32[]{:S(2)}) %all-to-all-start.3) | async-done | bytes 4718624 | tf_op jit(solution)/shard_map/all_to_all | solution.py:177
  184.2 25.4 %all_to_all.26 = bf16[8,194,512]{2,1,0:T(8,128)(2,1)S(1)} all-to-all(bf16[8,194,512]{2,1,0:T(8,128)(2,1)S(1)} %broadcast_in_dim.65), channel_id=1, replica_groups=mesh['kv'=8,'blk'=32] {'kv'}, dimensions={0} | all-to-all | bytes 3178496 | tf_op jit(solution)/shard_map/all_to_all | solution.py:259
  209.6 4.3 %multiply_reduce_fusion = (f32[194]{0:T(256)S(1)}, f32[194,576]{1,0:T(8,128)S(1)}) fusion(bf16[8,194,512]{2,1,0:T(8,128)(2,1)S(1)} %all_to_all.26, bf16[8,512,576]{1,2,0:T(8,128)(2,1)} %all-to-all-done.3), kind=kOutput, calls=%fused_computation.21 | convolution fusion | flops 915630144 | bytes 6755592 | tf_op jit(solution)/shard_map/srk,sko->ro/dot_general | solution.py:262
  214.5 3.3 %all-to-all-start.4 = ((f32[8,1,194]{2,1,0:T(1,128)}), f32[8,1,194]{2,1,0:T(1,128)S(1)}, u32[]{:S(2)}, u32[]{:S(2)}) async-start(f32[8,1,194]{2,1,0:T(1,128)} %broadcast_in_dim.66), calls=%async_computation.4 | async-start | bytes 16384 | tf_op jit(solution)/shard_map/all_to_all | solution.py:264
  217.9 2.6 %copy.181 = bf16[2,16,128,256]{3,2,1,0:T(8,128)(2,1)} copy(bf16[2,16,128,256]{2,3,1,0:T(8,128)(2,1)S(1)} %broadcast_select_fusion) | data formatting | bytes 4194304
  220.5 3.5 %all-to-all-done.4 = f32[8,1,194]{2,1,0:T(1,128)S(1)} async-done(((f32[8,1,194]{2,1,0:T(1,128)}), f32[8,1,194]{2,1,0:T(1,128)S(1)}, u32[]{:S(2)}, u32[]{:S(2)}) %all-to-all-start.4) | async-done | bytes 6240 | tf_op jit(solution)/shard_map/all_to_all | solution.py:264
  (105 shorter events, 22.6 us)
Async XLA Ops:
  7.2 33.3 %copy-start = (bf16[2,16,128,256]{3,2,1,0:T(8,128)(2,1)S(1)}, bf16[2,16,128,256]{3,2,1,0:T(8,128)(2,1)}, u32[]{:S(2)}) copy-start(bf16[2,16,128,256]{3,2,1,0:T(8,128)(2,1)} %param.25) | copy-start | bytes 6291460
  7.2 143.5 %all-gather.3.cloned.1.call-start = ((), (), s32[]{:S(2)}) async-start(), calls=%async_computation.5 | async-start | bytes 12976128 | tf_op jit(solution)/shard_map/all_gather | solution.py:167
  9.3 69.6 %collective-permute-start.2 = (bf16[2,192,256]{2,1,0:T(8,128)(2,1)}, bf16[2,192,256]{2,1,0:T(8,128)(2,1)}, u32[]{:S(2)}, u32[]{:S(2)}) collective-permute-start(bf16[2,192,256]{2,1,0:T(8,128)(2,1)} %param.16), channel_id=1, source_target_pairs={{0,2},{1,3},{2,4},{3,5},{4,6},{5,7},{6,8},{7,9},{8,10},{9,11},{10,... | collective-permute-start | bytes 589832 | tf_op jit(solution)/shard_map/ppermute | solution.py:78
  14.5 44.1 %collective-permute-start.1 = (bf16[2,192,256]{2,1,0:T(8,128)(2,1)}, bf16[2,192,256]{2,1,0:T(8,128)(2,1)S(1)}, u32[]{:S(2)}, u32[]{:S(2)}) collective-permute-start(bf16[2,192,256]{2,1,0:T(8,128)(2,1)} %param.16), channel_id=1, source_target_pairs={{0,3},{1,4},{2,5},{3,6},{4,7},{5,8},{6,9},{7,10},{8,11},{9,12},{10... | collective-permute-start | bytes 589832 | tf_op jit(solution)/shard_map/ppermute | solution.py:78
  20.1 38.6 %collective-permute-start = (bf16[2,192,256]{2,1,0:T(8,128)(2,1)}, bf16[2,192,256]{2,1,0:T(8,128)(2,1)S(1)}, u32[]{:S(2)}, u32[]{:S(2)}) collective-permute-start(bf16[2,192,256]{2,1,0:T(8,128)(2,1)} %param.16), channel_id=1, source_target_pairs={{0,4},{1,5},{2,6},{3,7},{4,8},{5,9},{6,10},{7,11},{8,12},{9,13},{1... | collective-permute-start | bytes 589832 | tf_op jit(solution)/shard_map/ppermute | solution.py:78
  23.8 56.8 %collective-permute-start.3 = (bf16[2,192,256]{2,1,0:T(8,128)(2,1)}, bf16[2,192,256]{2,1,0:T(8,128)(2,1)}, u32[]{:S(2)}, u32[]{:S(2)}) collective-permute-start(bf16[2,192,256]{2,1,0:T(8,128)(2,1)} %param.16), channel_id=1, source_target_pairs={{0,1},{1,2},{2,3},{3,4},{4,5},{5,6},{6,7},{7,8},{8,9},{9,10},{10,1... | collective-permute-start | bytes 589832 | tf_op jit(solution)/shard_map/ppermute | solution.py:78
  29.0 35.6 %all-to-all-start = ((bf16[32,8,256]{2,1,0:T(8,128)(2,1)}), bf16[32,8,256]{2,1,0:T(8,128)(2,1)S(1)}, u32[]{:S(2)}, u32[]{:S(2)}) async-start(bf16[32,8,256]{2,1,0:T(8,128)(2,1)} %broadcast_in_dim.56), calls=%async_computation | async-start | bytes 262144 | tf_op jit(solution)/shard_map/all_to_all | solution.py:154
  58.7 6.4 %copy-start.1 = (bf16[2,960,256]{2,1,0:T(8,128)(2,1)}, bf16[2,960,256]{2,1,0:T(8,128)(2,1)S(1)}, u32[]{:S(2)}) copy-start(bf16[2,960,256]{2,1,0:T(8,128)(2,1)S(1)} %constant_dynamic-update-slice_fusion.3) | copy-start | bytes 2949124
  67.9 14.3 %copy-start.4 = (bf16[2,192,256]{2,1,0:T(8,128)(2,1)S(1)}, bf16[2,192,256]{2,1,0:T(8,128)(2,1)}, u32[]{:S(2)}) copy-start(bf16[2,192,256]{2,1,0:T(8,128)(2,1)} %param.16) | copy-start | bytes 589828
  70.7 27.3 %all-to-all-start.1 = ((f32[32,2,2,2,129]{4,1,3,2,0:T(2,128)}), f32[32,2,2,2,129]{4,1,3,2,0:T(2,128)S(1)}, u32[]{:S(2)}, u32[]{:S(2)}) async-start(f32[32,2,2,2,129]{4,1,3,2,0:T(2,128)} %copy.176), calls=%async_computation.1 | async-start | bytes 524288 | tf_op jit(solution)/shard_map/all_to_all | solution.py:249
  82.9 20.3 %copy-start.11 = (s32[96]{0:T(128)S(1)}, s32[96]{0:T(128)}, u32[]{:S(2)}) copy-start(s32[96]{0:T(128)} %param.24) | copy-start | bytes 1156
  82.9 20.6 %copy-start.9 = (s32[16]{0:T(128)S(1)}, s32[16]{0:T(128)}, u32[]{:S(2)}) copy-start(s32[16]{0:T(128)} %param.27) | copy-start | bytes 196
  82.9 21.7 %copy-start.10 = (s32[16]{0:T(128)S(1)}, s32[16]{0:T(128)}, u32[]{:S(2)}) copy-start(s32[16]{0:T(128)} %param.28) | copy-start | bytes 196
  82.9 22.7 %copy-start.5 = (bf16[192,512]{1,0:T(8,128)(2,1)S(1)}, bf16[192,512]{1,0:T(8,128)(2,1)}, u32[]{:S(2)}) copy-start(bf16[192,512]{1,0:T(8,128)(2,1)} %param.15) | copy-start | bytes 589828
  97.9 86.1 %all-to-all-start.3 = ((bf16[8,512,576]{1,2,0:T(8,128)(2,1)}), bf16[8,512,576]{1,2,0:T(8,128)(2,1)}, u32[]{:S(2)}, u32[]{:S(2)}) async-start(bf16[8,512,576]{1,2,0:T(8,128)(2,1)} %bitcast.76), calls=%async_computation.3 | async-start | bytes 9437184 | tf_op jit(solution)/shard_map/all_to_all | solution.py:177
  150.7 23.2 %copy-start.2 = (bf16[960,2,128]{2,1,0:T(2,128)(2,1)S(1)}, bf16[960,2,128]{2,1,0:T(2,128)(2,1)}, u32[]{:S(2)}) copy-start(bf16[960,2,128]{2,1,0:T(2,128)(2,1)} %reshape_squeeze.12) | copy-start | bytes 1474564
  150.7 23.2 %copy-start.6 = (pred[192,960]{1,0:T(8,128)(4,1)S(1)}, pred[192,960]{1,0:T(8,128)(4,1)}, u32[]{:S(2)}) copy-start(pred[192,960]{1,0:T(8,128)(4,1)} %compare_and_fusion) | copy-start | bytes 552964
  213.9 10.1 %copy-start.3 = (bf16[192,576]{1,0:T(8,128)(2,1)S(1)}, bf16[192,576]{1,0:T(8,128)(2,1)}, u32[]{:S(2)}) copy-start(bf16[192,576]{1,0:T(8,128)(2,1)} %param.17) | copy-start | bytes 663556
  213.9 10.1 %copy-start.7 = (f32[576]{0:T(1024)S(1)}, f32[576]{0:T(1024)}, u32[]{:S(2)}) copy-start(f32[576]{0:T(1024)} %param.22) | copy-start | bytes 6916
  213.9 10.1 %copy-start.8 = (bf16[2,576]{1,0:T(2,128)(2,1)S(1)}, bf16[2,576]{1,0:T(2,128)(2,1)}, u32[]{:S(2)}) copy-start(bf16[2,576]{1,0:T(2,128)(2,1)} %param.20) | copy-start | bytes 6916
  214.5 9.5 %all-to-all-start.4 = ((f32[8,1,194]{2,1,0:T(1,128)}), f32[8,1,194]{2,1,0:T(1,128)S(1)}, u32[]{:S(2)}, u32[]{:S(2)}) async-start(f32[8,1,194]{2,1,0:T(1,128)} %broadcast_in_dim.66), calls=%async_computation.4 | async-start | bytes 16384 | tf_op jit(solution)/shard_map/all_to_all | solution.py:264
Sparse Core Ops, SparseCore 0:
  10.5 140.1 all-gather.2

commit v10 on v7

--- a/solution.py
+++ b/solution.py
@@ -249,14 +249,12 @@
 
     attention = jnp.concatenate([suffix_attn, decode_attn], axis=0)
     kv_size = lax.axis_size("kv")
-    projected_t = jnp.einsum(
-        "ko,rk->or", out_weight, attention, preferred_element_type=jnp.float32
-    )
+    weight_blocks = out_weight.reshape(out_weight.shape[0], kv_size, -1)
+    shares = jnp.einsum(
+        "rk,kdo->dro", attention, weight_blocks, preferred_element_type=jnp.float32
+    ).astype(jnp.bfloat16)
     residual = jnp.concatenate([suffix_resid, decode_resid], axis=0).astype(jnp.float32)
-    shares = projected_t.astype(jnp.bfloat16).reshape(kv_size, -1, projected_t.shape[1])
-    mine = jnp.sum(
-        lax.all_to_all(shares, "kv", 0, 0, tiled=False).astype(jnp.float32), axis=0
-    ).T
+    mine = jnp.sum(lax.all_to_all(shares, "kv", 0, 0, tiled=False).astype(jnp.float32), axis=0)
     squares = jnp.sum(mine * mine, axis=1)
     square_parts = lax.all_to_all(
         jnp.broadcast_to(squares[None], (kv_size,) + squares.shape), "kv", 0, 0, tiled=False

time: 224 us -> 220 us (0.982)
  waiting for transfers between devices: 68.3 us -> 63.8 us
    ppermute x4, waiting for transfers between devices: 12.1 us -> 5.38 us  [from_behind(): return lax.ppermute(block, axis, route)]
    unnamed x23 -> x24, local copies, waits for them, and re-layouts: 5.06 us -> 11.7 us
    reshape x2 -> x0, local copies, waits for them, and re-layouts: 6.1 us -> none  [body(): projected_t.astype(jnp.bfloat16).reshape(kv_size, -1, projected_t.shape[1])]
    all_gather x1, waiting for transfers between devices: 35.3 us -> 38.5 us  [body(): gathered = lax.all_gather(piece, 'blk', axis=0, tiled=False)]
  transfers between devices with their start and end apart: 8 -> 8, of which waited for: 6 -> 6; matrix products, arithmetic and copies ran while one was open for 12% -> 16% of each run, Pallas kernels for 0% -> 0%
where the time goes in v10:
time: 220 us; the launch traced here: 218 us
  waiting for transfers between devices  63.8 us (29%)
  starting transfers between devices  39.6 us (18%)
  blocking collectives  30.8 us (14%)
  local copies, waits for them, and re-layouts  25.4 us (12%)
  Pallas kernels  21.7 us (10%)
  between operations  14.4 us (7%)
  matrix products  12.6 us (6%)
  other arithmetic  9.7 us (4%)
    all_gather x1, waiting for transfers between devices, body(): gathered = lax.all_gather(piece, 'blk', axis=0, tiled=False)  38.5 us
    all_to_all x1, blocking collectives, body(): lax.all_to_all(shares, 'kv', 0, 0, tiled=False).astype(jnp.float32)  30.8 us
    pallas_call x1, Pallas kernels, prefix_attention(): pl.pallas_call(kern, grid=(heads, steps), in_specs=[pl.BlockSpec((1, rows...  21.7 us
    ppermute x4, starting transfers between devices, from_behind(): return lax.ppermute(block, axis, route)  17.6 us
    all_to_all x1, waiting for transfers between devices, body(): lax.all_to_all(slot_sums, 'blk', 0, 0, tiled=False)  15.5 us
    unnamed x24, local copies, waits for them, and re-layouts  11.7 us
    all_to_all x1, starting transfers between devices, body(): lax.all_to_all(jnp.broadcast_to(dec_local[None], (blk_size,) + dec_local....  9.52 us
    all_to_all x1, starting transfers between devices, body(): lax.all_to_all(slot_sums, 'blk', 0, 0, tiled=False)  9.07 us
  transfers between devices with their start and end apart: 8, of which 6 were waited for; matrix products, arithmetic and copies ran while one was open for 16% of the time, Pallas kernels for 0%

profile of v10, /device:TPU:2, one launch (start us, length us, event | category | flops | bytes accessed | tf_op | source)
XLA Modules:
  0.0 218.0 jit_solution(6034151037705327427)
XLA Ops:
  7.2 1.2 reshape.307
  9.3 5.2 %collective-permute-start.2 = (bf16[2,192,256]{2,1,0:T(8,128)(2,1)}, bf16[2,192,256]{2,1,0:T(8,128)(2,1)S(1)}, u32[]{:S(2)}, u32[]{:S(2)}) collective-permute-start(bf16[2,192,256]{2,1,0:T(8,128)(2,1)} %param.16), channel_id=1, source_target_pairs={{0,2},{1,3},{2,4},{3,5},{4,6},{5,7},{6,8},{7,9},{8,10},{9,11},{10,... | collective-permute-start | bytes 589832 | tf_op jit(solution)/shard_map/ppermute | solution.py:78
  14.5 5.6 %collective-permute-start.1 = (bf16[2,192,256]{2,1,0:T(8,128)(2,1)}, bf16[2,192,256]{2,1,0:T(8,128)(2,1)S(1)}, u32[]{:S(2)}, u32[]{:S(2)}) collective-permute-start(bf16[2,192,256]{2,1,0:T(8,128)(2,1)} %param.16), channel_id=1, source_target_pairs={{0,3},{1,4},{2,5},{3,6},{4,7},{5,8},{6,9},{7,10},{8,11},{9,12},{10... | collective-permute-start | bytes 589832 | tf_op jit(solution)/shard_map/ppermute | solution.py:78
  20.0 3.7 %collective-permute-start = (bf16[2,192,256]{2,1,0:T(8,128)(2,1)}, bf16[2,192,256]{2,1,0:T(8,128)(2,1)S(1)}, u32[]{:S(2)}, u32[]{:S(2)}) collective-permute-start(bf16[2,192,256]{2,1,0:T(8,128)(2,1)} %param.16), channel_id=1, source_target_pairs={{0,4},{1,5},{2,6},{3,7},{4,8},{5,9},{6,10},{7,11},{8,12},{9,13},{1... | collective-permute-start | bytes 589832 | tf_op jit(solution)/shard_map/ppermute | solution.py:78
  23.7 3.2 %collective-permute-start.3 = (bf16[2,192,256]{2,1,0:T(8,128)(2,1)}, bf16[2,192,256]{2,1,0:T(8,128)(2,1)S(1)}, u32[]{:S(2)}, u32[]{:S(2)}) collective-permute-start(bf16[2,192,256]{2,1,0:T(8,128)(2,1)} %param.16), channel_id=1, source_target_pairs={{0,1},{1,2},{2,3},{3,4},{4,5},{5,6},{6,7},{7,8},{8,9},{9,10},{10,1... | collective-permute-start | bytes 589832 | tf_op jit(solution)/shard_map/ppermute | solution.py:78
  29.0 9.5 %all-to-all-start = ((bf16[32,8,256]{2,1,0:T(8,128)(2,1)}), bf16[32,8,256]{2,1,0:T(8,128)(2,1)S(1)}, u32[]{:S(2)}, u32[]{:S(2)}) async-start(bf16[32,8,256]{2,1,0:T(8,128)(2,1)} %broadcast_in_dim.54), calls=%async_computation | async-start | bytes 262144 | tf_op jit(solution)/shard_map/all_to_all | solution.py:154
  47.3 2.4 %copy.173 = bf16[2,16,128,256]{2,3,1,0:T(8,128)(2,1)} copy(bf16[2,16,128,256]{3,2,1,0:T(8,128)(2,1)S(1)} %copy-done) | data formatting | bytes 4194304 | tf_op args[10]
  49.6 6.7 %copy.183 = bf16[512,4608]{0,1:T(8,128)(2,1)} copy(bf16[512,4608]{1,0:T(8,128)(2,1)} %param.21) | data formatting | bytes 9437184 | tf_op args[6]
  56.3 2.3 %collective-permute-done = bf16[2,192,256]{2,1,0:T(8,128)(2,1)S(1)} collective-permute-done((bf16[2,192,256]{2,1,0:T(8,128)(2,1)}, bf16[2,192,256]{2,1,0:T(8,128)(2,1)S(1)}, u32[]{:S(2)}, u32[]{:S(2)}) %collective-permute-start) | collective-permute-done | bytes 196640 | tf_op jit(solution)/shard_map/ppermute | solution.py:78
  58.7 3.1 %collective-permute-done.3 = bf16[2,192,256]{2,1,0:T(8,128)(2,1)S(1)} collective-permute-done((bf16[2,192,256]{2,1,0:T(8,128)(2,1)}, bf16[2,192,256]{2,1,0:T(8,128)(2,1)S(1)}, u32[]{:S(2)}, u32[]{:S(2)}) %collective-permute-start.3) | collective-permute-done | bytes 196640 | tf_op jit(solution)/shard_map/ppermute | solution.py:78
  61.9 0.9 reshape_squeeze.12
  65.2 2.5 %broadcast_select_fusion = bf16[2,16,128,256]{2,3,1,0:T(8,128)(2,1)S(1)} fusion(bf16[2,16,128,256]{2,3,1,0:T(8,128)(2,1)} %copy.173, pred[16,128]{1,0:T(8,128)(4,1)S(1)} %fusion.36, bf16[2,16,256]{2,1,0:T(8,128)(2,1)S(1)} %fusion.15), kind=kLoop, calls=%fused_computation.4 | loop fusion | flops 1048576 | bytes 4212736 | tf_op jit(solution)/shard_map/jit(_where)/select_n | solution.py:219
  70.7 9.1 %all-to-all-start.1 = ((f32[32,2,2,2,129]{4,1,3,2,0:T(2,128)}), f32[32,2,2,2,129]{4,1,3,2,0:T(2,128)S(1)}, u32[]{:S(2)}, u32[]{:S(2)}) async-start(f32[32,2,2,2,129]{4,1,3,2,0:T(2,128)} %copy.179), calls=%async_computation.1 | async-start | bytes 524288 | tf_op jit(solution)/shard_map/all_to_all | solution.py:243
  79.7 3.8 %fusion = (f32[192,2,2]{0,2,1:T(2,128)S(1)}, f32[2,960,192,2]{1,2,3,0:T(8,128)}) fusion(pred[192,960]{1,0:T(8,128)(4,1)} %compare_and_fusion, bf16[192,2,2,128]{3,2,1,0:T(2,128)(2,1)S(1)} %reshape.305, bf16[960,2,128,1]{2,1,0,3:T(2,128)(2,1)} %bitcast.82), kind=kOutput, calls=%fused_computation.2 | convolution fusion | flops 191692032 | bytes 3824640 | tf_op jit(solution)/shard_map/qhgd,khd->qhgk/dot_general | solution.py:83
  83.6 15.5 %all-to-all-done.1 = f32[32,2,2,2,129]{4,1,3,2,0:T(2,128)S(1)} async-done(((f32[32,2,2,2,129]{4,1,3,2,0:T(2,128)}), f32[32,2,2,2,129]{4,1,3,2,0:T(2,128)S(1)}, u32[]{:S(2)}, u32[]{:S(2)}) %all-to-all-start.1) | async-done | bytes 132128 | tf_op jit(solution)/shard_map/all_to_all | solution.py:243
  99.4 38.5 %all-gather.3.cloned.1.call-done = bf16[64,2,384,128]{3,2,1,0:T(8,128)(2,1)} async-done(((bf16[2,2,384,128]{3,2,1,0:T(8,128)(2,1)}), bf16[64,2,384,128]{3,2,1,0:T(8,128)(2,1)}) %all-gather.3.cloned.1.call-update) | async-done | bytes 12582928 | tf_op jit(solution)/shard_map/all_gather | solution.py:167
  137.9 21.7 %shard_map.166 = (f32[2,384,128]{2,1,0:T(8,128)}, f32[2,384,1]{2,1,0:T(8,128)}) custom-call(bf16[2,384,128]{2,1,0:T(8,128)(2,1)} %bitcast.80, bf16[32,2,2,384,128]{4,3,2,1,0:T(8,128)(2,1)} %bitcast.74, bf16[32,2,2,384,128]{4,3,2,1,0:T(8,128)(2,1)} %bitcast.75, s32[32,1,384]{2,1,0:T(1,128)} %broadcast_in_dim.64.own_ref, s32[384,1]{1,0:T(8,128)} %broadcast_in_dim_reshape.4.row_ref), custom_call_target="tpu_custom_call" | custom-call | tf_op jit(solution)/shard_map/pallas_call | solution.py:53
  159.6 1.2 reduce.2
  161.1 3.0 %fusion.19 = bf16[192,2,2,128]{3,0,2,1:T(8,128)(2,1)S(1)} fusion(f32[2,960,192,2]{1,2,3,0:T(8,128)} %get-tuple-element.41, pred[192,960]{1,0:T(8,128)(4,1)S(1)} %copy-done.5, bf16[960,2,128,1]{2,1,0,3:T(2,128)(2,1)S(1)} %bitcast.81, f32[2,192,2,128]{3,2,1,0:T(2,128)} %bitcast.88, f32[192,2,2]{0,2,1:T(2,128)S(1)} %bitcast_add_fusion), kind=kOutput, calls=%fused_computation.19 | convolution fusion | flops 191987712 | bytes 4217856 | tf_op jit(solution)/shard_map/qhgk,khd->qhgd/dot_general | solution.py:89
  164.4 3.9 %convert_bitcast_fusion = bf16[8,194,576]{2,1,0:T(8,128)(2,1)S(1)} fusion(bf16[512,8,576]{0,2,1:T(8,128)(2,1)} %bitcast.76, bf16[2,512]{1,0:T(2,128)(2,1)S(1)} %bitcast.85, bf16[192,512]{1,0:T(8,128)(2,1)S(1)} %reshape.310), kind=kOutput, calls=%fused_computation.5 | convolution fusion | flops 916698112 | bytes 6705152 | tf_op jit(solution)/shard_map/rk,kdo->dro/dot_general | solution.py:253
  168.3 30.8 %all_to_all.21 = bf16[8,194,576]{2,1,0:T(8,128)(2,1)S(1)} all-to-all(bf16[8,194,576]{2,1,0:T(8,128)(2,1)S(1)} %convert_bitcast_fusion), channel_id=1, replica_groups=mesh['kv'=8,'blk'=32] {'kv'}, dimensions={0} | all-to-all | bytes 3575808 | tf_op jit(solution)/shard_map/all_to_all | solution.py:257
  200.1 3.3 %all-to-all-start.3 = ((f32[8,1,194]{2,1,0:T(1,128)}), f32[8,1,194]{2,1,0:T(1,128)S(1)}, u32[]{:S(2)}, u32[]{:S(2)}) async-start(f32[8,1,194]{2,1,0:T(1,128)} %broadcast_in_dim.59), calls=%async_computation.3 | async-start | bytes 16384 | tf_op jit(solution)/shard_map/all_to_all | solution.py:259
  203.5 2.6 %copy.185 = bf16[2,16,128,256]{3,2,1,0:T(8,128)(2,1)} copy(bf16[2,16,128,256]{2,3,1,0:T(8,128)(2,1)S(1)} %broadcast_select_fusion) | data formatting | bytes 4194304
  206.1 3.5 %all-to-all-done.3 = f32[8,1,194]{2,1,0:T(1,128)S(1)} async-done(((f32[8,1,194]{2,1,0:T(1,128)}), f32[8,1,194]{2,1,0:T(1,128)S(1)}, u32[]{:S(2)}, u32[]{:S(2)}) %all-to-all-start.3) | async-done | bytes 6240 | tf_op jit(solution)/shard_map/all_to_all | solution.py:259
  (95 shorter events, 20.4 us)
Async XLA Ops:
  7.2 39.2 %copy-start.3 = (bf16[192,512]{1,0:T(8,128)(2,1)S(1)}, bf16[192,512]{1,0:T(8,128)(2,1)}, u32[]{:S(2)}) copy-start(bf16[192,512]{1,0:T(8,128)(2,1)} %param.15) | copy-start | bytes 589828
  7.2 40.1 %copy-start = (bf16[2,16,128,256]{3,2,1,0:T(8,128)(2,1)S(1)}, bf16[2,16,128,256]{3,2,1,0:T(8,128)(2,1)}, u32[]{:S(2)}) copy-start(bf16[2,16,128,256]{3,2,1,0:T(8,128)(2,1)} %param.25) | copy-start | bytes 6291460
  7.2 130.7 %all-gather.3.cloned.1.call-start = ((), (), s32[]{:S(2)}) async-start(), calls=%async_computation.4 | async-start | bytes 12976128 | tf_op jit(solution)/shard_map/all_gather | solution.py:167
  9.3 49.4 %collective-permute-start.2 = (bf16[2,192,256]{2,1,0:T(8,128)(2,1)}, bf16[2,192,256]{2,1,0:T(8,128)(2,1)S(1)}, u32[]{:S(2)}, u32[]{:S(2)}) collective-permute-start(bf16[2,192,256]{2,1,0:T(8,128)(2,1)} %param.16), channel_id=1, source_target_pairs={{0,2},{1,3},{2,4},{3,5},{4,6},{5,7},{6,8},{7,9},{8,10},{9,11},{10,... | collective-permute-start | bytes 589832 | tf_op jit(solution)/shard_map/ppermute | solution.py:78
  14.5 44.1 %collective-permute-start.1 = (bf16[2,192,256]{2,1,0:T(8,128)(2,1)}, bf16[2,192,256]{2,1,0:T(8,128)(2,1)S(1)}, u32[]{:S(2)}, u32[]{:S(2)}) collective-permute-start(bf16[2,192,256]{2,1,0:T(8,128)(2,1)} %param.16), channel_id=1, source_target_pairs={{0,3},{1,4},{2,5},{3,6},{4,7},{5,8},{6,9},{7,10},{8,11},{9,12},{10... | collective-permute-start | bytes 589832 | tf_op jit(solution)/shard_map/ppermute | solution.py:78
  20.0 38.6 %collective-permute-start = (bf16[2,192,256]{2,1,0:T(8,128)(2,1)}, bf16[2,192,256]{2,1,0:T(8,128)(2,1)S(1)}, u32[]{:S(2)}, u32[]{:S(2)}) collective-permute-start(bf16[2,192,256]{2,1,0:T(8,128)(2,1)} %param.16), channel_id=1, source_target_pairs={{0,4},{1,5},{2,6},{3,7},{4,8},{5,9},{6,10},{7,11},{8,12},{9,13},{1... | collective-permute-start | bytes 589832 | tf_op jit(solution)/shard_map/ppermute | solution.py:78
  23.7 38.0 %collective-permute-start.3 = (bf16[2,192,256]{2,1,0:T(8,128)(2,1)}, bf16[2,192,256]{2,1,0:T(8,128)(2,1)S(1)}, u32[]{:S(2)}, u32[]{:S(2)}) collective-permute-start(bf16[2,192,256]{2,1,0:T(8,128)(2,1)} %param.16), channel_id=1, source_target_pairs={{0,1},{1,2},{2,3},{3,4},{4,5},{5,6},{6,7},{7,8},{8,9},{9,10},{10,1... | collective-permute-start | bytes 589832 | tf_op jit(solution)/shard_map/ppermute | solution.py:78
  29.0 35.6 %all-to-all-start = ((bf16[32,8,256]{2,1,0:T(8,128)(2,1)}), bf16[32,8,256]{2,1,0:T(8,128)(2,1)S(1)}, u32[]{:S(2)}, u32[]{:S(2)}) async-start(bf16[32,8,256]{2,1,0:T(8,128)(2,1)} %broadcast_in_dim.54), calls=%async_computation | async-start | bytes 262144 | tf_op jit(solution)/shard_map/all_to_all | solution.py:154
  49.6 12.2 %copy-start.4 = (bf16[2,192,256]{2,1,0:T(8,128)(2,1)S(1)}, bf16[2,192,256]{2,1,0:T(8,128)(2,1)}, u32[]{:S(2)}) copy-start(bf16[2,192,256]{2,1,0:T(8,128)(2,1)} %param.16) | copy-start | bytes 589828
  70.7 28.5 %all-to-all-start.1 = ((f32[32,2,2,2,129]{4,1,3,2,0:T(2,128)}), f32[32,2,2,2,129]{4,1,3,2,0:T(2,128)S(1)}, u32[]{:S(2)}, u32[]{:S(2)}) async-start(f32[32,2,2,2,129]{4,1,3,2,0:T(2,128)} %copy.179), calls=%async_computation.1 | async-start | bytes 524288 | tf_op jit(solution)/shard_map/all_to_all | solution.py:243
  137.9 23.2 %copy-start.1 = (bf16[960,2,128]{2,1,0:T(2,128)(2,1)S(1)}, bf16[960,2,128]{2,1,0:T(2,128)(2,1)}, u32[]{:S(2)}) copy-start(bf16[960,2,128]{2,1,0:T(2,128)(2,1)} %reshape_squeeze.12) | copy-start | bytes 1474564
  137.9 23.2 %copy-start.5 = (pred[192,960]{1,0:T(8,128)(4,1)S(1)}, pred[192,960]{1,0:T(8,128)(4,1)}, u32[]{:S(2)}) copy-start(pred[192,960]{1,0:T(8,128)(4,1)} %compare_and_fusion) | copy-start | bytes 552964
  199.1 10.6 %copy-start.2 = (bf16[192,576]{1,0:T(8,128)(2,1)S(1)}, bf16[192,576]{1,0:T(8,128)(2,1)}, u32[]{:S(2)}) copy-start(bf16[192,576]{1,0:T(8,128)(2,1)} %param.17) | copy-start | bytes 663556
  199.1 10.6 %copy-start.6 = (f32[576]{0:T(1024)S(1)}, f32[576]{0:T(1024)}, u32[]{:S(2)}) copy-start(f32[576]{0:T(1024)} %param.22) | copy-start | bytes 6916
  199.1 10.6 %copy-start.7 = (bf16[2,576]{1,0:T(2,128)(2,1)S(1)}, bf16[2,576]{1,0:T(2,128)(2,1)}, u32[]{:S(2)}) copy-start(bf16[2,576]{1,0:T(2,128)(2,1)} %param.20) | copy-start | bytes 6916
  200.1 9.5 %all-to-all-start.3 = ((f32[8,1,194]{2,1,0:T(1,128)}), f32[8,1,194]{2,1,0:T(1,128)S(1)}, u32[]{:S(2)}, u32[]{:S(2)}) async-start(f32[8,1,194]{2,1,0:T(1,128)} %broadcast_in_dim.59), calls=%async_computation.3 | async-start | bytes 16384 | tf_op jit(solution)/shard_map/all_to_all | solution.py:259
Sparse Core Ops, SparseCore 0:
  10.5 127.3 all-gather.2

commit v11 on v10

--- a/solution.py
+++ b/solution.py
@@ -45,7 +45,7 @@
     den_ref[0] = denom
 
 
-def prefix_attention(q_heads, gathered, key_owner, row_prefix, q_scale, group=8):
+def prefix_attention(q_heads, gathered, key_owner, row_prefix, q_scale, group=16):
     heads, rows_q, head_dim = q_heads.shape
     sources, _, _, held_rows, _ = gathered.shape
     steps = sources // group

time: 220 us -> 219 us (level)
  no operation moved by 1% of the time
where the time goes in v11:
time: 219 us; the launch traced here: 217 us
  waiting for transfers between devices  63.8 us (29%)
  starting transfers between devices  39.6 us (18%)
  blocking collectives  30.7 us (14%)
  local copies, waits for them, and re-layouts  25.4 us (12%)
  Pallas kernels  21.3 us (10%)
  between operations  14.4 us (7%)
  matrix products  12.6 us (6%)
  other arithmetic  9.7 us (4%)
    all_gather x1, waiting for transfers between devices, body(): gathered = lax.all_gather(piece, 'blk', axis=0, tiled=False)  38.5 us
    all_to_all x1, blocking collectives, body(): lax.all_to_all(shares, 'kv', 0, 0, tiled=False).astype(jnp.float32)  30.7 us
    pallas_call x1, Pallas kernels, prefix_attention(): pl.pallas_call(kern, grid=(heads, steps), in_specs=[pl.BlockSpec((1, rows...  21.3 us
    ppermute x4, starting transfers between devices, from_behind(): return lax.ppermute(block, axis, route)  17.6 us
    all_to_all x1, waiting for transfers between devices, body(): lax.all_to_all(slot_sums, 'blk', 0, 0, tiled=False)  15.5 us
    unnamed x24, local copies, waits for them, and re-layouts  11.7 us
    all_to_all x1, starting transfers between devices, body(): lax.all_to_all(jnp.broadcast_to(dec_local[None], (blk_size,) + dec_local....  9.52 us
    all_to_all x1, starting transfers between devices, body(): lax.all_to_all(slot_sums, 'blk', 0, 0, tiled=False)  9.07 us
  transfers between devices with their start and end apart: 8, of which 6 were waited for; matrix products, arithmetic and copies ran while one was open for 16% of the time, Pallas kernels for 0%

profile of v11, /device:TPU:2, one launch (start us, length us, event | category | flops | bytes accessed | tf_op | source)
XLA Modules:
  0.0 217.5 jit_solution(7932076840401460189)
XLA Ops:
  7.2 1.2 reshape.307
  9.3 5.2 %collective-permute-start.2 = (bf16[2,192,256]{2,1,0:T(8,128)(2,1)}, bf16[2,192,256]{2,1,0:T(8,128)(2,1)S(1)}, u32[]{:S(2)}, u32[]{:S(2)}) collective-permute-start(bf16[2,192,256]{2,1,0:T(8,128)(2,1)} %param.16), channel_id=1, source_target_pairs={{0,2},{1,3},{2,4},{3,5},{4,6},{5,7},{6,8},{7,9},{8,10},{9,11},{10,... | collective-permute-start | bytes 589832 | tf_op jit(solution)/shard_map/ppermute | solution.py:78
  14.5 5.6 %collective-permute-start.1 = (bf16[2,192,256]{2,1,0:T(8,128)(2,1)}, bf16[2,192,256]{2,1,0:T(8,128)(2,1)S(1)}, u32[]{:S(2)}, u32[]{:S(2)}) collective-permute-start(bf16[2,192,256]{2,1,0:T(8,128)(2,1)} %param.16), channel_id=1, source_target_pairs={{0,3},{1,4},{2,5},{3,6},{4,7},{5,8},{6,9},{7,10},{8,11},{9,12},{10... | collective-permute-start | bytes 589832 | tf_op jit(solution)/shard_map/ppermute | solution.py:78
  20.0 3.7 %collective-permute-start = (bf16[2,192,256]{2,1,0:T(8,128)(2,1)}, bf16[2,192,256]{2,1,0:T(8,128)(2,1)S(1)}, u32[]{:S(2)}, u32[]{:S(2)}) collective-permute-start(bf16[2,192,256]{2,1,0:T(8,128)(2,1)} %param.16), channel_id=1, source_target_pairs={{0,4},{1,5},{2,6},{3,7},{4,8},{5,9},{6,10},{7,11},{8,12},{9,13},{1... | collective-permute-start | bytes 589832 | tf_op jit(solution)/shard_map/ppermute | solution.py:78
  23.7 3.2 %collective-permute-start.3 = (bf16[2,192,256]{2,1,0:T(8,128)(2,1)}, bf16[2,192,256]{2,1,0:T(8,128)(2,1)S(1)}, u32[]{:S(2)}, u32[]{:S(2)}) collective-permute-start(bf16[2,192,256]{2,1,0:T(8,128)(2,1)} %param.16), channel_id=1, source_target_pairs={{0,1},{1,2},{2,3},{3,4},{4,5},{5,6},{6,7},{7,8},{8,9},{9,10},{10,1... | collective-permute-start | bytes 589832 | tf_op jit(solution)/shard_map/ppermute | solution.py:78
  29.0 9.5 %all-to-all-start = ((bf16[32,8,256]{2,1,0:T(8,128)(2,1)}), bf16[32,8,256]{2,1,0:T(8,128)(2,1)S(1)}, u32[]{:S(2)}, u32[]{:S(2)}) async-start(bf16[32,8,256]{2,1,0:T(8,128)(2,1)} %broadcast_in_dim.54), calls=%async_computation | async-start | bytes 262144 | tf_op jit(solution)/shard_map/all_to_all | solution.py:154
  47.3 2.4 %copy.173 = bf16[2,16,128,256]{2,3,1,0:T(8,128)(2,1)} copy(bf16[2,16,128,256]{3,2,1,0:T(8,128)(2,1)S(1)} %copy-done) | data formatting | bytes 4194304 | tf_op args[10]
  49.6 6.7 %copy.183 = bf16[512,4608]{0,1:T(8,128)(2,1)} copy(bf16[512,4608]{1,0:T(8,128)(2,1)} %param.21) | data formatting | bytes 9437184 | tf_op args[6]
  56.3 2.3 %collective-permute-done = bf16[2,192,256]{2,1,0:T(8,128)(2,1)S(1)} collective-permute-done((bf16[2,192,256]{2,1,0:T(8,128)(2,1)}, bf16[2,192,256]{2,1,0:T(8,128)(2,1)S(1)}, u32[]{:S(2)}, u32[]{:S(2)}) %collective-permute-start) | collective-permute-done | bytes 196640 | tf_op jit(solution)/shard_map/ppermute | solution.py:78
  58.7 3.1 %collective-permute-done.3 = bf16[2,192,256]{2,1,0:T(8,128)(2,1)S(1)} collective-permute-done((bf16[2,192,256]{2,1,0:T(8,128)(2,1)}, bf16[2,192,256]{2,1,0:T(8,128)(2,1)S(1)}, u32[]{:S(2)}, u32[]{:S(2)}) %collective-permute-start.3) | collective-permute-done | bytes 196640 | tf_op jit(solution)/shard_map/ppermute | solution.py:78
  61.9 0.9 reshape_squeeze.12
  65.2 2.5 %broadcast_select_fusion = bf16[2,16,128,256]{2,3,1,0:T(8,128)(2,1)S(1)} fusion(bf16[2,16,128,256]{2,3,1,0:T(8,128)(2,1)} %copy.173, pred[16,128]{1,0:T(8,128)(4,1)S(1)} %fusion.36, bf16[2,16,256]{2,1,0:T(8,128)(2,1)S(1)} %fusion.15), kind=kLoop, calls=%fused_computation.4 | loop fusion | flops 1048576 | bytes 4212736 | tf_op jit(solution)/shard_map/jit(_where)/select_n | solution.py:219
  70.7 9.1 %all-to-all-start.1 = ((f32[32,2,2,2,129]{4,1,3,2,0:T(2,128)}), f32[32,2,2,2,129]{4,1,3,2,0:T(2,128)S(1)}, u32[]{:S(2)}, u32[]{:S(2)}) async-start(f32[32,2,2,2,129]{4,1,3,2,0:T(2,128)} %copy.179), calls=%async_computation.1 | async-start | bytes 524288 | tf_op jit(solution)/shard_map/all_to_all | solution.py:243
  79.7 3.8 %fusion = (f32[192,2,2]{0,2,1:T(2,128)S(1)}, f32[2,960,192,2]{1,2,3,0:T(8,128)}) fusion(pred[192,960]{1,0:T(8,128)(4,1)} %compare_and_fusion, bf16[192,2,2,128]{3,2,1,0:T(2,128)(2,1)S(1)} %reshape.305, bf16[960,2,128,1]{2,1,0,3:T(2,128)(2,1)} %bitcast.82), kind=kOutput, calls=%fused_computation.2 | convolution fusion | flops 191692032 | bytes 3824640 | tf_op jit(solution)/shard_map/qhgd,khd->qhgk/dot_general | solution.py:83
  83.6 15.5 %all-to-all-done.1 = f32[32,2,2,2,129]{4,1,3,2,0:T(2,128)S(1)} async-done(((f32[32,2,2,2,129]{4,1,3,2,0:T(2,128)}), f32[32,2,2,2,129]{4,1,3,2,0:T(2,128)S(1)}, u32[]{:S(2)}, u32[]{:S(2)}) %all-to-all-start.1) | async-done | bytes 132128 | tf_op jit(solution)/shard_map/all_to_all | solution.py:243
  99.4 38.5 %all-gather.3.cloned.1.call-done = bf16[64,2,384,128]{3,2,1,0:T(8,128)(2,1)} async-done(((bf16[2,2,384,128]{3,2,1,0:T(8,128)(2,1)}), bf16[64,2,384,128]{3,2,1,0:T(8,128)(2,1)}) %all-gather.3.cloned.1.call-update) | async-done | bytes 12582928 | tf_op jit(solution)/shard_map/all_gather | solution.py:167
  137.9 21.3 %shard_map.166 = (f32[2,384,128]{2,1,0:T(8,128)}, f32[2,384,1]{2,1,0:T(8,128)}) custom-call(bf16[2,384,128]{2,1,0:T(8,128)(2,1)} %bitcast.80, bf16[32,2,2,384,128]{4,3,2,1,0:T(8,128)(2,1)} %bitcast.74, bf16[32,2,2,384,128]{4,3,2,1,0:T(8,128)(2,1)} %bitcast.75, s32[32,1,384]{2,1,0:T(1,128)} %broadcast_in_dim.64.own_ref, s32[384,1]{1,0:T(8,128)} %broadcast_in_dim_reshape.4.row_ref), custom_call_target="tpu_custom_call" | custom-call | tf_op jit(solution)/shard_map/pallas_call | solution.py:53
  159.2 1.2 reduce.2
  160.7 3.0 %fusion.19 = bf16[192,2,2,128]{3,0,2,1:T(8,128)(2,1)S(1)} fusion(f32[2,960,192,2]{1,2,3,0:T(8,128)} %get-tuple-element.41, pred[192,960]{1,0:T(8,128)(4,1)S(1)} %copy-done.5, bf16[960,2,128,1]{2,1,0,3:T(2,128)(2,1)S(1)} %bitcast.81, f32[2,192,2,128]{3,2,1,0:T(2,128)} %bitcast.88, f32[192,2,2]{0,2,1:T(2,128)S(1)} %bitcast_add_fusion), kind=kOutput, calls=%fused_computation.19 | convolution fusion | flops 191987712 | bytes 4217856 | tf_op jit(solution)/shard_map/qhgk,khd->qhgd/dot_general | solution.py:89
  163.9 3.9 %convert_bitcast_fusion = bf16[8,194,576]{2,1,0:T(8,128)(2,1)S(1)} fusion(bf16[512,8,576]{0,2,1:T(8,128)(2,1)} %bitcast.76, bf16[2,512]{1,0:T(2,128)(2,1)S(1)} %bitcast.85, bf16[192,512]{1,0:T(8,128)(2,1)S(1)} %reshape.310), kind=kOutput, calls=%fused_computation.5 | convolution fusion | flops 916698112 | bytes 6705152 | tf_op jit(solution)/shard_map/rk,kdo->dro/dot_general | solution.py:253
  167.9 30.7 %all_to_all.21 = bf16[8,194,576]{2,1,0:T(8,128)(2,1)S(1)} all-to-all(bf16[8,194,576]{2,1,0:T(8,128)(2,1)S(1)} %convert_bitcast_fusion), channel_id=1, replica_groups=mesh['kv'=8,'blk'=32] {'kv'}, dimensions={0} | all-to-all | bytes 3575808 | tf_op jit(solution)/shard_map/all_to_all | solution.py:257
  199.7 3.3 %all-to-all-start.3 = ((f32[8,1,194]{2,1,0:T(1,128)}), f32[8,1,194]{2,1,0:T(1,128)S(1)}, u32[]{:S(2)}, u32[]{:S(2)}) async-start(f32[8,1,194]{2,1,0:T(1,128)} %broadcast_in_dim.59), calls=%async_computation.3 | async-start | bytes 16384 | tf_op jit(solution)/shard_map/all_to_all | solution.py:259
  203.0 2.6 %copy.185 = bf16[2,16,128,256]{3,2,1,0:T(8,128)(2,1)} copy(bf16[2,16,128,256]{2,3,1,0:T(8,128)(2,1)S(1)} %broadcast_select_fusion) | data formatting | bytes 4194304
  205.6 3.5 %all-to-all-done.3 = f32[8,1,194]{2,1,0:T(1,128)S(1)} async-done(((f32[8,1,194]{2,1,0:T(1,128)}), f32[8,1,194]{2,1,0:T(1,128)S(1)}, u32[]{:S(2)}, u32[]{:S(2)}) %all-to-all-start.3) | async-done | bytes 6240 | tf_op jit(solution)/shard_map/all_to_all | solution.py:259
  (95 shorter events, 20.4 us)
Async XLA Ops:
  7.2 39.2 %copy-start.3 = (bf16[192,512]{1,0:T(8,128)(2,1)S(1)}, bf16[192,512]{1,0:T(8,128)(2,1)}, u32[]{:S(2)}) copy-start(bf16[192,512]{1,0:T(8,128)(2,1)} %param.15) | copy-start | bytes 589828
  7.2 40.1 %copy-start = (bf16[2,16,128,256]{3,2,1,0:T(8,128)(2,1)S(1)}, bf16[2,16,128,256]{3,2,1,0:T(8,128)(2,1)}, u32[]{:S(2)}) copy-start(bf16[2,16,128,256]{3,2,1,0:T(8,128)(2,1)} %param.25) | copy-start | bytes 6291460
  7.2 130.7 %all-gather.3.cloned.1.call-start = ((), (), s32[]{:S(2)}) async-start(), calls=%async_computation.4 | async-start | bytes 12976128 | tf_op jit(solution)/shard_map/all_gather | solution.py:167
  9.3 49.4 %collective-permute-start.2 = (bf16[2,192,256]{2,1,0:T(8,128)(2,1)}, bf16[2,192,256]{2,1,0:T(8,128)(2,1)S(1)}, u32[]{:S(2)}, u32[]{:S(2)}) collective-permute-start(bf16[2,192,256]{2,1,0:T(8,128)(2,1)} %param.16), channel_id=1, source_target_pairs={{0,2},{1,3},{2,4},{3,5},{4,6},{5,7},{6,8},{7,9},{8,10},{9,11},{10,... | collective-permute-start | bytes 589832 | tf_op jit(solution)/shard_map/ppermute | solution.py:78
  14.5 44.1 %collective-permute-start.1 = (bf16[2,192,256]{2,1,0:T(8,128)(2,1)}, bf16[2,192,256]{2,1,0:T(8,128)(2,1)S(1)}, u32[]{:S(2)}, u32[]{:S(2)}) collective-permute-start(bf16[2,192,256]{2,1,0:T(8,128)(2,1)} %param.16), channel_id=1, source_target_pairs={{0,3},{1,4},{2,5},{3,6},{4,7},{5,8},{6,9},{7,10},{8,11},{9,12},{10... | collective-permute-start | bytes 589832 | tf_op jit(solution)/shard_map/ppermute | solution.py:78
  20.0 38.6 %collective-permute-start = (bf16[2,192,256]{2,1,0:T(8,128)(2,1)}, bf16[2,192,256]{2,1,0:T(8,128)(2,1)S(1)}, u32[]{:S(2)}, u32[]{:S(2)}) collective-permute-start(bf16[2,192,256]{2,1,0:T(8,128)(2,1)} %param.16), channel_id=1, source_target_pairs={{0,4},{1,5},{2,6},{3,7},{4,8},{5,9},{6,10},{7,11},{8,12},{9,13},{1... | collective-permute-start | bytes 589832 | tf_op jit(solution)/shard_map/ppermute | solution.py:78
  23.7 38.0 %collective-permute-start.3 = (bf16[2,192,256]{2,1,0:T(8,128)(2,1)}, bf16[2,192,256]{2,1,0:T(8,128)(2,1)S(1)}, u32[]{:S(2)}, u32[]{:S(2)}) collective-permute-start(bf16[2,192,256]{2,1,0:T(8,128)(2,1)} %param.16), channel_id=1, source_target_pairs={{0,1},{1,2},{2,3},{3,4},{4,5},{5,6},{6,7},{7,8},{8,9},{9,10},{10,1... | collective-permute-start | bytes 589832 | tf_op jit(solution)/shard_map/ppermute | solution.py:78
  29.0 35.6 %all-to-all-start = ((bf16[32,8,256]{2,1,0:T(8,128)(2,1)}), bf16[32,8,256]{2,1,0:T(8,128)(2,1)S(1)}, u32[]{:S(2)}, u32[]{:S(2)}) async-start(bf16[32,8,256]{2,1,0:T(8,128)(2,1)} %broadcast_in_dim.54), calls=%async_computation | async-start | bytes 262144 | tf_op jit(solution)/shard_map/all_to_all | solution.py:154
  49.6 12.2 %copy-start.4 = (bf16[2,192,256]{2,1,0:T(8,128)(2,1)S(1)}, bf16[2,192,256]{2,1,0:T(8,128)(2,1)}, u32[]{:S(2)}) copy-start(bf16[2,192,256]{2,1,0:T(8,128)(2,1)} %param.16) | copy-start | bytes 589828
  70.7 28.5 %all-to-all-start.1 = ((f32[32,2,2,2,129]{4,1,3,2,0:T(2,128)}), f32[32,2,2,2,129]{4,1,3,2,0:T(2,128)S(1)}, u32[]{:S(2)}, u32[]{:S(2)}) async-start(f32[32,2,2,2,129]{4,1,3,2,0:T(2,128)} %copy.179), calls=%async_computation.1 | async-start | bytes 524288 | tf_op jit(solution)/shard_map/all_to_all | solution.py:243
  137.9 22.7 %copy-start.1 = (bf16[960,2,128]{2,1,0:T(2,128)(2,1)S(1)}, bf16[960,2,128]{2,1,0:T(2,128)(2,1)}, u32[]{:S(2)}) copy-start(bf16[960,2,128]{2,1,0:T(2,128)(2,1)} %reshape_squeeze.12) | copy-start | bytes 1474564
  137.9 22.7 %copy-start.5 = (pred[192,960]{1,0:T(8,128)(4,1)S(1)}, pred[192,960]{1,0:T(8,128)(4,1)}, u32[]{:S(2)}) copy-start(pred[192,960]{1,0:T(8,128)(4,1)} %compare_and_fusion) | copy-start | bytes 552964
  198.6 10.6 %copy-start.2 = (bf16[192,576]{1,0:T(8,128)(2,1)S(1)}, bf16[192,576]{1,0:T(8,128)(2,1)}, u32[]{:S(2)}) copy-start(bf16[192,576]{1,0:T(8,128)(2,1)} %param.17) | copy-start | bytes 663556
  198.6 10.6 %copy-start.6 = (f32[576]{0:T(1024)S(1)}, f32[576]{0:T(1024)}, u32[]{:S(2)}) copy-start(f32[576]{0:T(1024)} %param.22) | copy-start | bytes 6916
  198.6 10.6 %copy-start.7 = (bf16[2,576]{1,0:T(2,128)(2,1)S(1)}, bf16[2,576]{1,0:T(2,128)(2,1)}, u32[]{:S(2)}) copy-start(bf16[2,576]{1,0:T(2,128)(2,1)} %param.20) | copy-start | bytes 6916
  199.7 9.5 %all-to-all-start.3 = ((f32[8,1,194]{2,1,0:T(1,128)}), f32[8,1,194]{2,1,0:T(1,128)S(1)}, u32[]{:S(2)}, u32[]{:S(2)}) async-start(f32[8,1,194]{2,1,0:T(1,128)} %broadcast_in_dim.59), calls=%async_computation.3 | async-start | bytes 16384 | tf_op jit(solution)/shard_map/all_to_all | solution.py:259
Sparse Core Ops, SparseCore 0:
  10.5 127.3 all-gather.2

commit v12 on v11

--- a/solution.py
+++ b/solution.py
@@ -253,7 +253,6 @@
     shares = jnp.einsum(
         "rk,kdo->dro", attention, weight_blocks, preferred_element_type=jnp.float32
     ).astype(jnp.bfloat16)
-    residual = jnp.concatenate([suffix_resid, decode_resid], axis=0).astype(jnp.float32)
     mine = jnp.sum(lax.all_to_all(shares, "kv", 0, 0, tiled=False).astype(jnp.float32), axis=0)
     squares = jnp.sum(mine * mine, axis=1)
     square_parts = lax.all_to_all(
@@ -261,8 +260,9 @@
     )
     mean_square = jnp.sum(square_parts, axis=0) / D
     normed = mine * lax.rsqrt(mean_square + norm_eps)[:, None] * post_gain[None, :]
-    hidden = (residual + normed).astype(jnp.bfloat16)
-    return (hidden[:tok_rows], hidden[tok_rows:], new_cache)
+    suffix_hidden = (suffix_resid.astype(jnp.float32) + normed[:tok_rows]).astype(jnp.bfloat16)
+    decode_hidden = (decode_resid.astype(jnp.float32) + normed[tok_rows:]).astype(jnp.bfloat16)
+    return (suffix_hidden, decode_hidden, new_cache)
 
 
 def solution(mesh):

time: 219 us -> 219 us (level)
  no operation moved by 1% of the time
where the time goes in v12:
time: 219 us; the launch traced here: 218 us
  waiting for transfers between devices  63.8 us (29%)
  starting transfers between devices  39.6 us (18%)
  blocking collectives  30.7 us (14%)
  local copies, waits for them, and re-layouts  24.1 us (11%)
  Pallas kernels  21.3 us (10%)
  between operations  14.5 us (7%)
  matrix products  12.6 us (6%)
  other arithmetic  11 us (5%)
    all_gather x1, waiting for transfers between devices, body(): gathered = lax.all_gather(piece, 'blk', axis=0, tiled=False)  38.5 us
    all_to_all x1, blocking collectives, body(): lax.all_to_all(shares, 'kv', 0, 0, tiled=False).astype(jnp.float32)  30.7 us
    pallas_call x1, Pallas kernels, prefix_attention(): pl.pallas_call(kern, grid=(heads, steps), in_specs=[pl.BlockSpec((1, rows...  21.3 us
    ppermute x4, starting transfers between devices, from_behind(): return lax.ppermute(block, axis, route)  17.6 us
    all_to_all x1, waiting for transfers between devices, body(): lax.all_to_all(slot_sums, 'blk', 0, 0, tiled=False)  15.5 us
    unnamed x24, local copies, waits for them, and re-layouts  11.7 us
    all_to_all x1, starting transfers between devices, body(): lax.all_to_all(jnp.broadcast_to(dec_local[None], (blk_size,) + dec_local....  9.52 us
    all_to_all x1, starting transfers between devices, body(): lax.all_to_all(slot_sums, 'blk', 0, 0, tiled=False)  9.07 us
  transfers between devices with their start and end apart: 8, of which 6 were waited for; matrix products, arithmetic and copies ran while one was open for 16% of the time, Pallas kernels for 0%

profile of v12, /device:TPU:2, one launch (start us, length us, event | category | flops | bytes accessed | tf_op | source)
XLA Modules:
  0.0 217.5 jit_solution(8952971837496592126)
XLA Ops:
  7.2 1.2 reshape.307
  9.3 5.2 %collective-permute-start.2 = (bf16[2,192,256]{2,1,0:T(8,128)(2,1)}, bf16[2,192,256]{2,1,0:T(8,128)(2,1)S(1)}, u32[]{:S(2)}, u32[]{:S(2)}) collective-permute-start(bf16[2,192,256]{2,1,0:T(8,128)(2,1)} %param.16), channel_id=1, source_target_pairs={{0,2},{1,3},{2,4},{3,5},{4,6},{5,7},{6,8},{7,9},{8,10},{9,11},{10,... | collective-permute-start | bytes 589832 | tf_op jit(solution)/shard_map/ppermute | solution.py:78
  14.5 5.6 %collective-permute-start.1 = (bf16[2,192,256]{2,1,0:T(8,128)(2,1)}, bf16[2,192,256]{2,1,0:T(8,128)(2,1)S(1)}, u32[]{:S(2)}, u32[]{:S(2)}) collective-permute-start(bf16[2,192,256]{2,1,0:T(8,128)(2,1)} %param.16), channel_id=1, source_target_pairs={{0,3},{1,4},{2,5},{3,6},{4,7},{5,8},{6,9},{7,10},{8,11},{9,12},{10... | collective-permute-start | bytes 589832 | tf_op jit(solution)/shard_map/ppermute | solution.py:78
  20.0 3.7 %collective-permute-start = (bf16[2,192,256]{2,1,0:T(8,128)(2,1)}, bf16[2,192,256]{2,1,0:T(8,128)(2,1)S(1)}, u32[]{:S(2)}, u32[]{:S(2)}) collective-permute-start(bf16[2,192,256]{2,1,0:T(8,128)(2,1)} %param.16), channel_id=1, source_target_pairs={{0,4},{1,5},{2,6},{3,7},{4,8},{5,9},{6,10},{7,11},{8,12},{9,13},{1... | collective-permute-start | bytes 589832 | tf_op jit(solution)/shard_map/ppermute | solution.py:78
  23.7 3.2 %collective-permute-start.3 = (bf16[2,192,256]{2,1,0:T(8,128)(2,1)}, bf16[2,192,256]{2,1,0:T(8,128)(2,1)S(1)}, u32[]{:S(2)}, u32[]{:S(2)}) collective-permute-start(bf16[2,192,256]{2,1,0:T(8,128)(2,1)} %param.16), channel_id=1, source_target_pairs={{0,1},{1,2},{2,3},{3,4},{4,5},{5,6},{6,7},{7,8},{8,9},{9,10},{10,1... | collective-permute-start | bytes 589832 | tf_op jit(solution)/shard_map/ppermute | solution.py:78
  29.0 9.5 %all-to-all-start = ((bf16[32,8,256]{2,1,0:T(8,128)(2,1)}), bf16[32,8,256]{2,1,0:T(8,128)(2,1)S(1)}, u32[]{:S(2)}, u32[]{:S(2)}) async-start(bf16[32,8,256]{2,1,0:T(8,128)(2,1)} %broadcast_in_dim.54), calls=%async_computation | async-start | bytes 262144 | tf_op jit(solution)/shard_map/all_to_all | solution.py:154
  47.3 2.4 %copy.173 = bf16[2,16,128,256]{2,3,1,0:T(8,128)(2,1)} copy(bf16[2,16,128,256]{3,2,1,0:T(8,128)(2,1)S(1)} %copy-done) | data formatting | bytes 4194304 | tf_op args[10]
  49.6 6.7 %copy.183 = bf16[512,4608]{0,1:T(8,128)(2,1)} copy(bf16[512,4608]{1,0:T(8,128)(2,1)} %param.21) | data formatting | bytes 9437184 | tf_op args[6]
  56.3 2.3 %collective-permute-done = bf16[2,192,256]{2,1,0:T(8,128)(2,1)S(1)} collective-permute-done((bf16[2,192,256]{2,1,0:T(8,128)(2,1)}, bf16[2,192,256]{2,1,0:T(8,128)(2,1)S(1)}, u32[]{:S(2)}, u32[]{:S(2)}) %collective-permute-start) | collective-permute-done | bytes 196640 | tf_op jit(solution)/shard_map/ppermute | solution.py:78
  58.7 3.1 %collective-permute-done.3 = bf16[2,192,256]{2,1,0:T(8,128)(2,1)S(1)} collective-permute-done((bf16[2,192,256]{2,1,0:T(8,128)(2,1)}, bf16[2,192,256]{2,1,0:T(8,128)(2,1)S(1)}, u32[]{:S(2)}, u32[]{:S(2)}) %collective-permute-start.3) | collective-permute-done | bytes 196640 | tf_op jit(solution)/shard_map/ppermute | solution.py:78
  61.9 0.9 reshape_squeeze.12
  65.2 2.5 %broadcast_select_fusion = bf16[2,16,128,256]{2,3,1,0:T(8,128)(2,1)S(1)} fusion(bf16[2,16,128,256]{2,3,1,0:T(8,128)(2,1)} %copy.173, pred[16,128]{1,0:T(8,128)(4,1)S(1)} %fusion.37, bf16[2,16,256]{2,1,0:T(8,128)(2,1)S(1)} %fusion.15), kind=kLoop, calls=%fused_computation.4 | loop fusion | flops 1048576 | bytes 4212736 | tf_op jit(solution)/shard_map/jit(_where)/select_n | solution.py:219
  70.7 9.1 %all-to-all-start.1 = ((f32[32,2,2,2,129]{4,1,3,2,0:T(2,128)}), f32[32,2,2,2,129]{4,1,3,2,0:T(2,128)S(1)}, u32[]{:S(2)}, u32[]{:S(2)}) async-start(f32[32,2,2,2,129]{4,1,3,2,0:T(2,128)} %copy.179), calls=%async_computation.1 | async-start | bytes 524288 | tf_op jit(solution)/shard_map/all_to_all | solution.py:243
  79.7 3.8 %fusion = (f32[192,2,2]{0,2,1:T(2,128)S(1)}, f32[2,960,192,2]{1,2,3,0:T(8,128)}) fusion(pred[192,960]{1,0:T(8,128)(4,1)} %compare_and_fusion, bf16[192,2,2,128]{3,2,1,0:T(2,128)(2,1)S(1)} %reshape.305, bf16[960,2,128,1]{2,1,0,3:T(2,128)(2,1)} %bitcast.82), kind=kOutput, calls=%fused_computation.2 | convolution fusion | flops 191692032 | bytes 3824640 | tf_op jit(solution)/shard_map/qhgd,khd->qhgk/dot_general | solution.py:83
  83.6 15.5 %all-to-all-done.1 = f32[32,2,2,2,129]{4,1,3,2,0:T(2,128)S(1)} async-done(((f32[32,2,2,2,129]{4,1,3,2,0:T(2,128)}), f32[32,2,2,2,129]{4,1,3,2,0:T(2,128)S(1)}, u32[]{:S(2)}, u32[]{:S(2)}) %all-to-all-start.1) | async-done | bytes 132128 | tf_op jit(solution)/shard_map/all_to_all | solution.py:243
  99.4 38.5 %all-gather.3.cloned.1.call-done = bf16[64,2,384,128]{3,2,1,0:T(8,128)(2,1)} async-done(((bf16[2,2,384,128]{3,2,1,0:T(8,128)(2,1)}), bf16[64,2,384,128]{3,2,1,0:T(8,128)(2,1)}) %all-gather.3.cloned.1.call-update) | async-done | bytes 12582928 | tf_op jit(solution)/shard_map/all_gather | solution.py:167
  137.9 21.3 %shard_map.166 = (f32[2,384,128]{2,1,0:T(8,128)}, f32[2,384,1]{2,1,0:T(8,128)}) custom-call(bf16[2,384,128]{2,1,0:T(8,128)(2,1)} %bitcast.80, bf16[32,2,2,384,128]{4,3,2,1,0:T(8,128)(2,1)} %bitcast.74, bf16[32,2,2,384,128]{4,3,2,1,0:T(8,128)(2,1)} %bitcast.75, s32[32,1,384]{2,1,0:T(1,128)} %broadcast_in_dim.64.own_ref, s32[384,1]{1,0:T(8,128)} %broadcast_in_dim_reshape.4.row_ref), custom_call_target="tpu_custom_call" | custom-call | tf_op jit(solution)/shard_map/pallas_call | solution.py:53
  159.2 1.2 reduce.2
  160.7 3.0 %fusion.19 = bf16[192,2,2,128]{3,0,2,1:T(8,128)(2,1)S(1)} fusion(f32[2,960,192,2]{1,2,3,0:T(8,128)} %get-tuple-element.41, pred[192,960]{1,0:T(8,128)(4,1)S(1)} %copy-done.5, bf16[960,2,128,1]{2,1,0,3:T(2,128)(2,1)S(1)} %bitcast.81, f32[2,192,2,128]{3,2,1,0:T(2,128)} %bitcast.88, f32[192,2,2]{0,2,1:T(2,128)S(1)} %bitcast_add_fusion), kind=kOutput, calls=%fused_computation.19 | convolution fusion | flops 191987712 | bytes 4217856 | tf_op jit(solution)/shard_map/qhgk,khd->qhgd/dot_general | solution.py:89
  163.9 3.9 %convert_bitcast_fusion = bf16[8,194,576]{2,1,0:T(8,128)(2,1)S(1)} fusion(bf16[512,8,576]{0,2,1:T(8,128)(2,1)} %bitcast.76, bf16[2,512]{1,0:T(2,128)(2,1)S(1)} %bitcast.85, bf16[192,512]{1,0:T(8,128)(2,1)S(1)} %reshape.310), kind=kOutput, calls=%fused_computation.5 | convolution fusion | flops 916698112 | bytes 6705152 | tf_op jit(solution)/shard_map/rk,kdo->dro/dot_general | solution.py:253
  167.9 30.7 %all_to_all.21 = bf16[8,194,576]{2,1,0:T(8,128)(2,1)S(1)} all-to-all(bf16[8,194,576]{2,1,0:T(8,128)(2,1)S(1)} %convert_bitcast_fusion), channel_id=1, replica_groups=mesh['kv'=8,'blk'=32] {'kv'}, dimensions={0} | all-to-all | bytes 3575808 | tf_op jit(solution)/shard_map/all_to_all | solution.py:256
  199.7 3.3 %all-to-all-start.3 = ((f32[8,1,194]{2,1,0:T(1,128)}), f32[8,1,194]{2,1,0:T(1,128)S(1)}, u32[]{:S(2)}, u32[]{:S(2)}) async-start(f32[8,1,194]{2,1,0:T(1,128)} %broadcast_in_dim.59), calls=%async_computation.3 | async-start | bytes 16384 | tf_op jit(solution)/shard_map/all_to_all | solution.py:258
  203.0 2.6 %copy.185 = bf16[2,16,128,256]{3,2,1,0:T(8,128)(2,1)} copy(bf16[2,16,128,256]{2,3,1,0:T(8,128)(2,1)S(1)} %broadcast_select_fusion) | data formatting | bytes 4194304
  205.6 3.5 %all-to-all-done.3 = f32[8,1,194]{2,1,0:T(1,128)S(1)} async-done(((f32[8,1,194]{2,1,0:T(1,128)}), f32[8,1,194]{2,1,0:T(1,128)S(1)}, u32[]{:S(2)}, u32[]{:S(2)}) %all-to-all-start.3) | async-done | bytes 6240 | tf_op jit(solution)/shard_map/all_to_all | solution.py:258
  (95 shorter events, 20.4 us)
Async XLA Ops:
  7.2 39.2 %copy-start.3 = (bf16[192,512]{1,0:T(8,128)(2,1)S(1)}, bf16[192,512]{1,0:T(8,128)(2,1)}, u32[]{:S(2)}) copy-start(bf16[192,512]{1,0:T(8,128)(2,1)} %param.15) | copy-start | bytes 589828
  7.2 40.1 %copy-start = (bf16[2,16,128,256]{3,2,1,0:T(8,128)(2,1)S(1)}, bf16[2,16,128,256]{3,2,1,0:T(8,128)(2,1)}, u32[]{:S(2)}) copy-start(bf16[2,16,128,256]{3,2,1,0:T(8,128)(2,1)} %param.25) | copy-start | bytes 6291460
  7.2 130.7 %all-gather.3.cloned.1.call-start = ((), (), s32[]{:S(2)}) async-start(), calls=%async_computation.4 | async-start | bytes 12976128 | tf_op jit(solution)/shard_map/all_gather | solution.py:167
  9.3 49.4 %collective-permute-start.2 = (bf16[2,192,256]{2,1,0:T(8,128)(2,1)}, bf16[2,192,256]{2,1,0:T(8,128)(2,1)S(1)}, u32[]{:S(2)}, u32[]{:S(2)}) collective-permute-start(bf16[2,192,256]{2,1,0:T(8,128)(2,1)} %param.16), channel_id=1, source_target_pairs={{0,2},{1,3},{2,4},{3,5},{4,6},{5,7},{6,8},{7,9},{8,10},{9,11},{10,... | collective-permute-start | bytes 589832 | tf_op jit(solution)/shard_map/ppermute | solution.py:78
  14.5 44.1 %collective-permute-start.1 = (bf16[2,192,256]{2,1,0:T(8,128)(2,1)}, bf16[2,192,256]{2,1,0:T(8,128)(2,1)S(1)}, u32[]{:S(2)}, u32[]{:S(2)}) collective-permute-start(bf16[2,192,256]{2,1,0:T(8,128)(2,1)} %param.16), channel_id=1, source_target_pairs={{0,3},{1,4},{2,5},{3,6},{4,7},{5,8},{6,9},{7,10},{8,11},{9,12},{10... | collective-permute-start | bytes 589832 | tf_op jit(solution)/shard_map/ppermute | solution.py:78
  20.0 38.6 %collective-permute-start = (bf16[2,192,256]{2,1,0:T(8,128)(2,1)}, bf16[2,192,256]{2,1,0:T(8,128)(2,1)S(1)}, u32[]{:S(2)}, u32[]{:S(2)}) collective-permute-start(bf16[2,192,256]{2,1,0:T(8,128)(2,1)} %param.16), channel_id=1, source_target_pairs={{0,4},{1,5},{2,6},{3,7},{4,8},{5,9},{6,10},{7,11},{8,12},{9,13},{1... | collective-permute-start | bytes 589832 | tf_op jit(solution)/shard_map/ppermute | solution.py:78
  23.7 38.0 %collective-permute-start.3 = (bf16[2,192,256]{2,1,0:T(8,128)(2,1)}, bf16[2,192,256]{2,1,0:T(8,128)(2,1)S(1)}, u32[]{:S(2)}, u32[]{:S(2)}) collective-permute-start(bf16[2,192,256]{2,1,0:T(8,128)(2,1)} %param.16), channel_id=1, source_target_pairs={{0,1},{1,2},{2,3},{3,4},{4,5},{5,6},{6,7},{7,8},{8,9},{9,10},{10,1... | collective-permute-start | bytes 589832 | tf_op jit(solution)/shard_map/ppermute | solution.py:78
  29.0 35.6 %all-to-all-start = ((bf16[32,8,256]{2,1,0:T(8,128)(2,1)}), bf16[32,8,256]{2,1,0:T(8,128)(2,1)S(1)}, u32[]{:S(2)}, u32[]{:S(2)}) async-start(bf16[32,8,256]{2,1,0:T(8,128)(2,1)} %broadcast_in_dim.54), calls=%async_computation | async-start | bytes 262144 | tf_op jit(solution)/shard_map/all_to_all | solution.py:154
  49.6 12.2 %copy-start.4 = (bf16[2,192,256]{2,1,0:T(8,128)(2,1)S(1)}, bf16[2,192,256]{2,1,0:T(8,128)(2,1)}, u32[]{:S(2)}) copy-start(bf16[2,192,256]{2,1,0:T(8,128)(2,1)} %param.16) | copy-start | bytes 589828
  70.7 28.4 %all-to-all-start.1 = ((f32[32,2,2,2,129]{4,1,3,2,0:T(2,128)}), f32[32,2,2,2,129]{4,1,3,2,0:T(2,128)S(1)}, u32[]{:S(2)}, u32[]{:S(2)}) async-start(f32[32,2,2,2,129]{4,1,3,2,0:T(2,128)} %copy.179), calls=%async_computation.1 | async-start | bytes 524288 | tf_op jit(solution)/shard_map/all_to_all | solution.py:243
  137.9 22.7 %copy-start.1 = (bf16[960,2,128]{2,1,0:T(2,128)(2,1)S(1)}, bf16[960,2,128]{2,1,0:T(2,128)(2,1)}, u32[]{:S(2)}) copy-start(bf16[960,2,128]{2,1,0:T(2,128)(2,1)} %reshape_squeeze.12) | copy-start | bytes 1474564
  137.9 22.7 %copy-start.5 = (pred[192,960]{1,0:T(8,128)(4,1)S(1)}, pred[192,960]{1,0:T(8,128)(4,1)}, u32[]{:S(2)}) copy-start(pred[192,960]{1,0:T(8,128)(4,1)} %compare_and_fusion) | copy-start | bytes 552964
  198.6 10.6 %copy-start.6 = (f32[576]{0:T(1024)S(1)}, f32[576]{0:T(1024)}, u32[]{:S(2)}) copy-start(f32[576]{0:T(1024)} %param.22) | copy-start | bytes 6916
  198.9 10.4 %copy-start.7 = (bf16[2,576]{1,0:T(2,128)(2,1)S(1)}, bf16[2,576]{1,0:T(2,128)(2,1)}, u32[]{:S(2)}) copy-start(bf16[2,576]{1,0:T(2,128)(2,1)} %param.20) | copy-start | bytes 6916
  198.9 11.0 %copy-start.2 = (bf16[192,576]{1,0:T(8,128)(2,1)S(1)}, bf16[192,576]{1,0:T(8,128)(2,1)}, u32[]{:S(2)}) copy-start(bf16[192,576]{1,0:T(8,128)(2,1)} %param.17) | copy-start | bytes 663556
  199.7 9.5 %all-to-all-start.3 = ((f32[8,1,194]{2,1,0:T(1,128)}), f32[8,1,194]{2,1,0:T(1,128)S(1)}, u32[]{:S(2)}, u32[]{:S(2)}) async-start(f32[8,1,194]{2,1,0:T(1,128)} %broadcast_in_dim.59), calls=%async_computation.3 | async-start | bytes 16384 | tf_op jit(solution)/shard_map/all_to_all | solution.py:258
Sparse Core Ops, SparseCore 0:
  10.5 127.3 all-gather.2

commit v13 on v12

--- a/solution.py
+++ b/solution.py
@@ -39,7 +39,8 @@
         capped = soft_cap * jnp.tanh(s * (q_scale / soft_cap))
         seen = rows == own_ref[part]
         w = jnp.where(seen, jnp.exp(capped), 0.0)
-        denom = denom + jnp.sum(w, axis=1, keepdims=True)
+        for lane in range(0, w.shape[1], 128):
+            denom = denom + w[:, lane : lane + 128]
         numer = numer + jnp.dot(w.astype(jnp.bfloat16), v, preferred_element_type=jnp.float32)
     num_ref[0] = numer
     den_ref[0] = denom
@@ -62,11 +63,11 @@
         ],
         out_specs=[
             pl.BlockSpec((1, rows_q, head_dim), lambda h, j: (h, 0, 0)),
-            pl.BlockSpec((1, rows_q, 1), lambda h, j: (h, 0, 0)),
+            pl.BlockSpec((1, rows_q, 128), lambda h, j: (h, 0, 0)),
         ],
         out_shape=[
             jax.ShapeDtypeStruct((heads, rows_q, head_dim), jnp.float32),
-            jax.ShapeDtypeStruct((heads, rows_q, 1), jnp.float32),
+            jax.ShapeDtypeStruct((heads, rows_q, 128), jnp.float32),
         ],
         compiler_params=pltpu.CompilerParams(dimension_semantics=("parallel", "arbitrary")),
     )(q_heads, gathered, gathered, key_owner, row_prefix)
@@ -190,7 +191,8 @@
     row_prefix = jnp.repeat(tok_prefix, query_group_width)[:, None]
     rows_q = tok_rows * query_group_width
     q_by_head = own_queries.transpose(1, 0, 2, 3).reshape(kv_heads, rows_q, head_dim)
-    numer_p, denom_p = prefix_attention(q_by_head, gathered, key_owner, row_prefix, q_scale)
+    numer_p, denom_lanes = prefix_attention(q_by_head, gathered, key_owner, row_prefix, q_scale)
+    denom_p = jnp.sum(denom_lanes, axis=2)
     pre_numer = numer_p.reshape(kv_heads, tok_rows, query_group_width, head_dim).transpose(
         1, 0, 2, 3
     )

time: 219 us -> 219 us (level)
  no operation moved by 1% of the time
where the time goes in v13:
time: 219 us; the launch traced here: 218 us
  waiting for transfers between devices  63.8 us (29%)
  starting transfers between devices  39.6 us (18%)
  blocking collectives  30.7 us (14%)
  local copies, waits for them, and re-layouts  24.1 us (11%)
  Pallas kernels  21.5 us (10%)
  between operations  14.5 us (7%)
  matrix products  12.6 us (6%)
  other arithmetic  11 us (5%)
    all_gather x1, waiting for transfers between devices, body(): gathered = lax.all_gather(piece, 'blk', axis=0, tiled=False)  38.5 us
    all_to_all x1, blocking collectives, body(): lax.all_to_all(shares, 'kv', 0, 0, tiled=False).astype(jnp.float32)  30.7 us
    pallas_call x1, Pallas kernels, prefix_attention(): pl.pallas_call(kern, grid=(heads, steps), in_specs=[pl.BlockSpec((1, rows...  21.5 us
    ppermute x4, starting transfers between devices, from_behind(): return lax.ppermute(block, axis, route)  17.6 us
    all_to_all x1, waiting for transfers between devices, body(): lax.all_to_all(slot_sums, 'blk', 0, 0, tiled=False)  15.5 us
    unnamed x24, local copies, waits for them, and re-layouts  11.7 us
    all_to_all x1, starting transfers between devices, body(): lax.all_to_all(jnp.broadcast_to(dec_local[None], (blk_size,) + dec_local....  9.52 us
    all_to_all x1, starting transfers between devices, body(): lax.all_to_all(slot_sums, 'blk', 0, 0, tiled=False)  9.07 us
  transfers between devices with their start and end apart: 8, of which 6 were waited for; matrix products, arithmetic and copies ran while one was open for 16% of the time, Pallas kernels for 0%

profile of v13, /device:TPU:2, one launch (start us, length us, event | category | flops | bytes accessed | tf_op | source)
XLA Modules:
  0.0 217.7 jit_solution(2803510707501037302)
XLA Ops:
  7.2 1.2 reshape.307
  9.3 5.2 %collective-permute-start.2 = (bf16[2,192,256]{2,1,0:T(8,128)(2,1)}, bf16[2,192,256]{2,1,0:T(8,128)(2,1)S(1)}, u32[]{:S(2)}, u32[]{:S(2)}) collective-permute-start(bf16[2,192,256]{2,1,0:T(8,128)(2,1)} %param.16), channel_id=1, source_target_pairs={{0,2},{1,3},{2,4},{3,5},{4,6},{5,7},{6,8},{7,9},{8,10},{9,11},{10,... | collective-permute-start | bytes 589832 | tf_op jit(solution)/shard_map/ppermute | solution.py:79
  14.5 5.6 %collective-permute-start.1 = (bf16[2,192,256]{2,1,0:T(8,128)(2,1)}, bf16[2,192,256]{2,1,0:T(8,128)(2,1)S(1)}, u32[]{:S(2)}, u32[]{:S(2)}) collective-permute-start(bf16[2,192,256]{2,1,0:T(8,128)(2,1)} %param.16), channel_id=1, source_target_pairs={{0,3},{1,4},{2,5},{3,6},{4,7},{5,8},{6,9},{7,10},{8,11},{9,12},{10... | collective-permute-start | bytes 589832 | tf_op jit(solution)/shard_map/ppermute | solution.py:79
  20.0 3.7 %collective-permute-start = (bf16[2,192,256]{2,1,0:T(8,128)(2,1)}, bf16[2,192,256]{2,1,0:T(8,128)(2,1)S(1)}, u32[]{:S(2)}, u32[]{:S(2)}) collective-permute-start(bf16[2,192,256]{2,1,0:T(8,128)(2,1)} %param.16), channel_id=1, source_target_pairs={{0,4},{1,5},{2,6},{3,7},{4,8},{5,9},{6,10},{7,11},{8,12},{9,13},{1... | collective-permute-start | bytes 589832 | tf_op jit(solution)/shard_map/ppermute | solution.py:79
  23.7 3.2 %collective-permute-start.3 = (bf16[2,192,256]{2,1,0:T(8,128)(2,1)}, bf16[2,192,256]{2,1,0:T(8,128)(2,1)S(1)}, u32[]{:S(2)}, u32[]{:S(2)}) collective-permute-start(bf16[2,192,256]{2,1,0:T(8,128)(2,1)} %param.16), channel_id=1, source_target_pairs={{0,1},{1,2},{2,3},{3,4},{4,5},{5,6},{6,7},{7,8},{8,9},{9,10},{10,1... | collective-permute-start | bytes 589832 | tf_op jit(solution)/shard_map/ppermute | solution.py:79
  29.0 9.5 %all-to-all-start = ((bf16[32,8,256]{2,1,0:T(8,128)(2,1)}), bf16[32,8,256]{2,1,0:T(8,128)(2,1)S(1)}, u32[]{:S(2)}, u32[]{:S(2)}) async-start(bf16[32,8,256]{2,1,0:T(8,128)(2,1)} %broadcast_in_dim.54), calls=%async_computation | async-start | bytes 262144 | tf_op jit(solution)/shard_map/all_to_all | solution.py:155
  47.3 2.4 %copy.172 = bf16[2,16,128,256]{2,3,1,0:T(8,128)(2,1)} copy(bf16[2,16,128,256]{3,2,1,0:T(8,128)(2,1)S(1)} %copy-done) | data formatting | bytes 4194304 | tf_op args[10]
  49.6 6.7 %copy.182 = bf16[512,4608]{0,1:T(8,128)(2,1)} copy(bf16[512,4608]{1,0:T(8,128)(2,1)} %param.21) | data formatting | bytes 9437184 | tf_op args[6]
  56.3 2.3 %collective-permute-done = bf16[2,192,256]{2,1,0:T(8,128)(2,1)S(1)} collective-permute-done((bf16[2,192,256]{2,1,0:T(8,128)(2,1)}, bf16[2,192,256]{2,1,0:T(8,128)(2,1)S(1)}, u32[]{:S(2)}, u32[]{:S(2)}) %collective-permute-start) | collective-permute-done | bytes 196640 | tf_op jit(solution)/shard_map/ppermute | solution.py:79
  58.7 3.1 %collective-permute-done.3 = bf16[2,192,256]{2,1,0:T(8,128)(2,1)S(1)} collective-permute-done((bf16[2,192,256]{2,1,0:T(8,128)(2,1)}, bf16[2,192,256]{2,1,0:T(8,128)(2,1)S(1)}, u32[]{:S(2)}, u32[]{:S(2)}) %collective-permute-start.3) | collective-permute-done | bytes 196640 | tf_op jit(solution)/shard_map/ppermute | solution.py:79
  61.9 0.9 reshape_squeeze.12
  65.2 2.5 %broadcast_select_fusion = bf16[2,16,128,256]{2,3,1,0:T(8,128)(2,1)S(1)} fusion(bf16[2,16,128,256]{2,3,1,0:T(8,128)(2,1)} %copy.172, pred[16,128]{1,0:T(8,128)(4,1)S(1)} %fusion.37, bf16[2,16,256]{2,1,0:T(8,128)(2,1)S(1)} %fusion.15), kind=kLoop, calls=%fused_computation.4 | loop fusion | flops 1048576 | bytes 4212736 | tf_op jit(solution)/shard_map/jit(_where)/select_n | solution.py:221
  70.7 9.1 %all-to-all-start.1 = ((f32[32,2,2,2,129]{4,1,3,2,0:T(2,128)}), f32[32,2,2,2,129]{4,1,3,2,0:T(2,128)S(1)}, u32[]{:S(2)}, u32[]{:S(2)}) async-start(f32[32,2,2,2,129]{4,1,3,2,0:T(2,128)} %copy.178), calls=%async_computation.1 | async-start | bytes 524288 | tf_op jit(solution)/shard_map/all_to_all | solution.py:245
  79.7 3.8 %fusion = (f32[192,2,2]{0,2,1:T(2,128)S(1)}, f32[2,960,192,2]{1,2,3,0:T(8,128)}) fusion(pred[192,960]{1,0:T(8,128)(4,1)} %compare_and_fusion, bf16[192,2,2,128]{3,2,1,0:T(2,128)(2,1)S(1)} %reshape.305, bf16[960,2,128,1]{2,1,0,3:T(2,128)(2,1)} %bitcast.82), kind=kOutput, calls=%fused_computation.2 | convolution fusion | flops 191692032 | bytes 3824640 | tf_op jit(solution)/shard_map/qhgd,khd->qhgk/dot_general | solution.py:84
  83.6 15.5 %all-to-all-done.1 = f32[32,2,2,2,129]{4,1,3,2,0:T(2,128)S(1)} async-done(((f32[32,2,2,2,129]{4,1,3,2,0:T(2,128)}), f32[32,2,2,2,129]{4,1,3,2,0:T(2,128)S(1)}, u32[]{:S(2)}, u32[]{:S(2)}) %all-to-all-start.1) | async-done | bytes 132128 | tf_op jit(solution)/shard_map/all_to_all | solution.py:245
  99.4 38.5 %all-gather.3.cloned.1.call-done = bf16[64,2,384,128]{3,2,1,0:T(8,128)(2,1)} async-done(((bf16[2,2,384,128]{3,2,1,0:T(8,128)(2,1)}), bf16[64,2,384,128]{3,2,1,0:T(8,128)(2,1)}) %all-gather.3.cloned.1.call-update) | async-done | bytes 12582928 | tf_op jit(solution)/shard_map/all_gather | solution.py:168
  137.9 21.5 %shard_map.166 = (f32[2,384,128]{2,1,0:T(8,128)}, f32[2,384,128]{2,1,0:T(8,128)}) custom-call(bf16[2,384,128]{2,1,0:T(8,128)(2,1)} %bitcast.80, bf16[32,2,2,384,128]{4,3,2,1,0:T(8,128)(2,1)} %bitcast.74, bf16[32,2,2,384,128]{4,3,2,1,0:T(8,128)(2,1)} %bitcast.75, s32[32,1,384]{2,1,0:T(1,128)} %broadcast_in_dim.64.own_ref, ...), custom_call_target="tpu_custom_call" | custom-call | tf_op jit(solution)/shard_map/pallas_call | solution.py:54
  159.4 1.2 reduce_sum.112
  160.9 3.0 %fusion.19 = bf16[192,2,2,128]{3,0,2,1:T(8,128)(2,1)S(1)} fusion(f32[2,960,192,2]{1,2,3,0:T(8,128)} %get-tuple-element.41, pred[192,960]{1,0:T(8,128)(4,1)S(1)} %copy-done.5, bf16[960,2,128,1]{2,1,0,3:T(2,128)(2,1)S(1)} %bitcast.81, f32[2,192,2,128]{3,2,1,0:T(2,128)} %bitcast.88, f32[192,2,2]{0,2,1:T(2,128)S(1)} %bitcast_add_fusion), kind=kOutput, calls=%fused_computation.19 | convolution fusion | flops 191987712 | bytes 4217856 | tf_op jit(solution)/shard_map/qhgk,khd->qhgd/dot_general | solution.py:90
  164.1 3.9 %convert_bitcast_fusion = bf16[8,194,576]{2,1,0:T(8,128)(2,1)S(1)} fusion(bf16[512,8,576]{0,2,1:T(8,128)(2,1)} %bitcast.76, bf16[2,512]{1,0:T(2,128)(2,1)S(1)} %bitcast.85, bf16[192,512]{1,0:T(8,128)(2,1)S(1)} %reshape.310), kind=kOutput, calls=%fused_computation.5 | convolution fusion | flops 916698112 | bytes 6705152 | tf_op jit(solution)/shard_map/rk,kdo->dro/dot_general | solution.py:255
  168.1 30.7 %all_to_all.21 = bf16[8,194,576]{2,1,0:T(8,128)(2,1)S(1)} all-to-all(bf16[8,194,576]{2,1,0:T(8,128)(2,1)S(1)} %convert_bitcast_fusion), channel_id=1, replica_groups=mesh['kv'=8,'blk'=32] {'kv'}, dimensions={0} | all-to-all | bytes 3575808 | tf_op jit(solution)/shard_map/all_to_all | solution.py:258
  199.9 3.3 %all-to-all-start.3 = ((f32[8,1,194]{2,1,0:T(1,128)}), f32[8,1,194]{2,1,0:T(1,128)S(1)}, u32[]{:S(2)}, u32[]{:S(2)}) async-start(f32[8,1,194]{2,1,0:T(1,128)} %broadcast_in_dim.59), calls=%async_computation.3 | async-start | bytes 16384 | tf_op jit(solution)/shard_map/all_to_all | solution.py:260
  203.2 2.6 %copy.184 = bf16[2,16,128,256]{3,2,1,0:T(8,128)(2,1)} copy(bf16[2,16,128,256]{2,3,1,0:T(8,128)(2,1)S(1)} %broadcast_select_fusion) | data formatting | bytes 4194304
  205.8 3.5 %all-to-all-done.3 = f32[8,1,194]{2,1,0:T(1,128)S(1)} async-done(((f32[8,1,194]{2,1,0:T(1,128)}), f32[8,1,194]{2,1,0:T(1,128)S(1)}, u32[]{:S(2)}, u32[]{:S(2)}) %all-to-all-start.3) | async-done | bytes 6240 | tf_op jit(solution)/shard_map/all_to_all | solution.py:260
  (95 shorter events, 20.4 us)
Async XLA Ops:
  7.2 39.2 %copy-start.3 = (bf16[192,512]{1,0:T(8,128)(2,1)S(1)}, bf16[192,512]{1,0:T(8,128)(2,1)}, u32[]{:S(2)}) copy-start(bf16[192,512]{1,0:T(8,128)(2,1)} %param.15) | copy-start | bytes 589828
  7.2 40.1 %copy-start = (bf16[2,16,128,256]{3,2,1,0:T(8,128)(2,1)S(1)}, bf16[2,16,128,256]{3,2,1,0:T(8,128)(2,1)}, u32[]{:S(2)}) copy-start(bf16[2,16,128,256]{3,2,1,0:T(8,128)(2,1)} %param.25) | copy-start | bytes 6291460
  7.2 130.7 %all-gather.3.cloned.1.call-start = ((), (), s32[]{:S(2)}) async-start(), calls=%async_computation.4 | async-start | bytes 12976128 | tf_op jit(solution)/shard_map/all_gather | solution.py:168
  9.3 49.4 %collective-permute-start.2 = (bf16[2,192,256]{2,1,0:T(8,128)(2,1)}, bf16[2,192,256]{2,1,0:T(8,128)(2,1)S(1)}, u32[]{:S(2)}, u32[]{:S(2)}) collective-permute-start(bf16[2,192,256]{2,1,0:T(8,128)(2,1)} %param.16), channel_id=1, source_target_pairs={{0,2},{1,3},{2,4},{3,5},{4,6},{5,7},{6,8},{7,9},{8,10},{9,11},{10,... | collective-permute-start | bytes 589832 | tf_op jit(solution)/shard_map/ppermute | solution.py:79
  14.5 44.1 %collective-permute-start.1 = (bf16[2,192,256]{2,1,0:T(8,128)(2,1)}, bf16[2,192,256]{2,1,0:T(8,128)(2,1)S(1)}, u32[]{:S(2)}, u32[]{:S(2)}) collective-permute-start(bf16[2,192,256]{2,1,0:T(8,128)(2,1)} %param.16), channel_id=1, source_target_pairs={{0,3},{1,4},{2,5},{3,6},{4,7},{5,8},{6,9},{7,10},{8,11},{9,12},{10... | collective-permute-start | bytes 589832 | tf_op jit(solution)/shard_map/ppermute | solution.py:79
  20.0 38.6 %collective-permute-start = (bf16[2,192,256]{2,1,0:T(8,128)(2,1)}, bf16[2,192,256]{2,1,0:T(8,128)(2,1)S(1)}, u32[]{:S(2)}, u32[]{:S(2)}) collective-permute-start(bf16[2,192,256]{2,1,0:T(8,128)(2,1)} %param.16), channel_id=1, source_target_pairs={{0,4},{1,5},{2,6},{3,7},{4,8},{5,9},{6,10},{7,11},{8,12},{9,13},{1... | collective-permute-start | bytes 589832 | tf_op jit(solution)/shard_map/ppermute | solution.py:79
  23.7 38.0 %collective-permute-start.3 = (bf16[2,192,256]{2,1,0:T(8,128)(2,1)}, bf16[2,192,256]{2,1,0:T(8,128)(2,1)S(1)}, u32[]{:S(2)}, u32[]{:S(2)}) collective-permute-start(bf16[2,192,256]{2,1,0:T(8,128)(2,1)} %param.16), channel_id=1, source_target_pairs={{0,1},{1,2},{2,3},{3,4},{4,5},{5,6},{6,7},{7,8},{8,9},{9,10},{10,1... | collective-permute-start | bytes 589832 | tf_op jit(solution)/shard_map/ppermute | solution.py:79
  29.0 35.6 %all-to-all-start = ((bf16[32,8,256]{2,1,0:T(8,128)(2,1)}), bf16[32,8,256]{2,1,0:T(8,128)(2,1)S(1)}, u32[]{:S(2)}, u32[]{:S(2)}) async-start(bf16[32,8,256]{2,1,0:T(8,128)(2,1)} %broadcast_in_dim.54), calls=%async_computation | async-start | bytes 262144 | tf_op jit(solution)/shard_map/all_to_all | solution.py:155
  49.6 12.2 %copy-start.4 = (bf16[2,192,256]{2,1,0:T(8,128)(2,1)S(1)}, bf16[2,192,256]{2,1,0:T(8,128)(2,1)}, u32[]{:S(2)}) copy-start(bf16[2,192,256]{2,1,0:T(8,128)(2,1)} %param.16) | copy-start | bytes 589828
  70.7 28.4 %all-to-all-start.1 = ((f32[32,2,2,2,129]{4,1,3,2,0:T(2,128)}), f32[32,2,2,2,129]{4,1,3,2,0:T(2,128)S(1)}, u32[]{:S(2)}, u32[]{:S(2)}) async-start(f32[32,2,2,2,129]{4,1,3,2,0:T(2,128)} %copy.178), calls=%async_computation.1 | async-start | bytes 524288 | tf_op jit(solution)/shard_map/all_to_all | solution.py:245
  137.9 22.9 %copy-start.1 = (bf16[960,2,128]{2,1,0:T(2,128)(2,1)S(1)}, bf16[960,2,128]{2,1,0:T(2,128)(2,1)}, u32[]{:S(2)}) copy-start(bf16[960,2,128]{2,1,0:T(2,128)(2,1)} %reshape_squeeze.12) | copy-start | bytes 1474564
  137.9 23.0 %copy-start.5 = (pred[192,960]{1,0:T(8,128)(4,1)S(1)}, pred[192,960]{1,0:T(8,128)(4,1)}, u32[]{:S(2)}) copy-start(pred[192,960]{1,0:T(8,128)(4,1)} %compare_and_fusion) | copy-start | bytes 552964
  198.8 10.6 %copy-start.6 = (f32[576]{0:T(1024)S(1)}, f32[576]{0:T(1024)}, u32[]{:S(2)}) copy-start(f32[576]{0:T(1024)} %param.22) | copy-start | bytes 6916
  199.1 10.4 %copy-start.7 = (bf16[2,576]{1,0:T(2,128)(2,1)S(1)}, bf16[2,576]{1,0:T(2,128)(2,1)}, u32[]{:S(2)}) copy-start(bf16[2,576]{1,0:T(2,128)(2,1)} %param.20) | copy-start | bytes 6916
  199.2 11.0 %copy-start.2 = (bf16[192,576]{1,0:T(8,128)(2,1)S(1)}, bf16[192,576]{1,0:T(8,128)(2,1)}, u32[]{:S(2)}) copy-start(bf16[192,576]{1,0:T(8,128)(2,1)} %param.17) | copy-start | bytes 663556
  199.9 9.5 %all-to-all-start.3 = ((f32[8,1,194]{2,1,0:T(1,128)}), f32[8,1,194]{2,1,0:T(1,128)S(1)}, u32[]{:S(2)}, u32[]{:S(2)}) async-start(f32[8,1,194]{2,1,0:T(1,128)} %broadcast_in_dim.59), calls=%async_computation.3 | async-start | bytes 16384 | tf_op jit(solution)/shard_map/all_to_all | solution.py:260
Sparse Core Ops, SparseCore 0:
  10.5 127.3 all-gather.2

commit v14 on v12

--- a/solution.py
+++ b/solution.py
@@ -45,7 +45,7 @@
     den_ref[0] = denom
 
 
-def prefix_attention(q_heads, gathered, key_owner, row_prefix, q_scale, group=16):
+def prefix_attention(q_heads, gathered, key_owner, row_prefix, q_scale, group=32):
     heads, rows_q, head_dim = q_heads.shape
     sources, _, _, held_rows, _ = gathered.shape
     steps = sources // group

time: 219 us -> 220 us (level)
  no operation moved by 1% of the time
where the time goes in v14:
time: 220 us; the launch traced here: 218 us
  waiting for transfers between devices  63.8 us (29%)
  starting transfers between devices  39.6 us (18%)
  blocking collectives  30.8 us (14%)
  local copies, waits for them, and re-layouts  24.1 us (11%)
  Pallas kernels  21.9 us (10%)
  between operations  14.5 us (7%)
  matrix products  12.6 us (6%)
  other arithmetic  11 us (5%)
    all_gather x1, waiting for transfers between devices, body(): gathered = lax.all_gather(piece, 'blk', axis=0, tiled=False)  38.5 us
    all_to_all x1, blocking collectives, body(): lax.all_to_all(shares, 'kv', 0, 0, tiled=False).astype(jnp.float32)  30.8 us
    pallas_call x1, Pallas kernels, prefix_attention(): pl.pallas_call(kern, grid=(heads, steps), in_specs=[pl.BlockSpec((1, rows...  21.9 us
    ppermute x4, starting transfers between devices, from_behind(): return lax.ppermute(block, axis, route)  17.6 us
    all_to_all x1, waiting for transfers between devices, body(): lax.all_to_all(slot_sums, 'blk', 0, 0, tiled=False)  15.5 us
    unnamed x24, local copies, waits for them, and re-layouts  11.7 us
    all_to_all x1, starting transfers between devices, body(): lax.all_to_all(jnp.broadcast_to(dec_local[None], (blk_size,) + dec_local....  9.52 us
    all_to_all x1, starting transfers between devices, body(): lax.all_to_all(slot_sums, 'blk', 0, 0, tiled=False)  9.07 us
  transfers between devices with their start and end apart: 8, of which 6 were waited for; matrix products, arithmetic and copies ran while one was open for 16% of the time, Pallas kernels for 0%

profile of v14, /device:TPU:2, one launch (start us, length us, event | category | flops | bytes accessed | tf_op | source)
XLA Modules:
  0.0 218.1 jit_solution(6872373311253434495)
XLA Ops:
  7.2 1.2 reshape.307
  9.3 5.2 %collective-permute-start.2 = (bf16[2,192,256]{2,1,0:T(8,128)(2,1)}, bf16[2,192,256]{2,1,0:T(8,128)(2,1)S(1)}, u32[]{:S(2)}, u32[]{:S(2)}) collective-permute-start(bf16[2,192,256]{2,1,0:T(8,128)(2,1)} %param.16), channel_id=1, source_target_pairs={{0,2},{1,3},{2,4},{3,5},{4,6},{5,7},{6,8},{7,9},{8,10},{9,11},{10,... | collective-permute-start | bytes 589832 | tf_op jit(solution)/shard_map/ppermute | solution.py:78
  14.5 5.6 %collective-permute-start.1 = (bf16[2,192,256]{2,1,0:T(8,128)(2,1)}, bf16[2,192,256]{2,1,0:T(8,128)(2,1)S(1)}, u32[]{:S(2)}, u32[]{:S(2)}) collective-permute-start(bf16[2,192,256]{2,1,0:T(8,128)(2,1)} %param.16), channel_id=1, source_target_pairs={{0,3},{1,4},{2,5},{3,6},{4,7},{5,8},{6,9},{7,10},{8,11},{9,12},{10... | collective-permute-start | bytes 589832 | tf_op jit(solution)/shard_map/ppermute | solution.py:78
  20.0 3.7 %collective-permute-start = (bf16[2,192,256]{2,1,0:T(8,128)(2,1)}, bf16[2,192,256]{2,1,0:T(8,128)(2,1)S(1)}, u32[]{:S(2)}, u32[]{:S(2)}) collective-permute-start(bf16[2,192,256]{2,1,0:T(8,128)(2,1)} %param.16), channel_id=1, source_target_pairs={{0,4},{1,5},{2,6},{3,7},{4,8},{5,9},{6,10},{7,11},{8,12},{9,13},{1... | collective-permute-start | bytes 589832 | tf_op jit(solution)/shard_map/ppermute | solution.py:78
  23.7 3.2 %collective-permute-start.3 = (bf16[2,192,256]{2,1,0:T(8,128)(2,1)}, bf16[2,192,256]{2,1,0:T(8,128)(2,1)S(1)}, u32[]{:S(2)}, u32[]{:S(2)}) collective-permute-start(bf16[2,192,256]{2,1,0:T(8,128)(2,1)} %param.16), channel_id=1, source_target_pairs={{0,1},{1,2},{2,3},{3,4},{4,5},{5,6},{6,7},{7,8},{8,9},{9,10},{10,1... | collective-permute-start | bytes 589832 | tf_op jit(solution)/shard_map/ppermute | solution.py:78
  29.0 9.5 %all-to-all-start = ((bf16[32,8,256]{2,1,0:T(8,128)(2,1)}), bf16[32,8,256]{2,1,0:T(8,128)(2,1)S(1)}, u32[]{:S(2)}, u32[]{:S(2)}) async-start(bf16[32,8,256]{2,1,0:T(8,128)(2,1)} %broadcast_in_dim.54), calls=%async_computation | async-start | bytes 262144 | tf_op jit(solution)/shard_map/all_to_all | solution.py:154
  47.3 2.4 %copy.173 = bf16[2,16,128,256]{2,3,1,0:T(8,128)(2,1)} copy(bf16[2,16,128,256]{3,2,1,0:T(8,128)(2,1)S(1)} %copy-done) | data formatting | bytes 4194304 | tf_op args[10]
  49.6 6.7 %copy.183 = bf16[512,4608]{0,1:T(8,128)(2,1)} copy(bf16[512,4608]{1,0:T(8,128)(2,1)} %param.21) | data formatting | bytes 9437184 | tf_op args[6]
  56.3 2.3 %collective-permute-done = bf16[2,192,256]{2,1,0:T(8,128)(2,1)S(1)} collective-permute-done((bf16[2,192,256]{2,1,0:T(8,128)(2,1)}, bf16[2,192,256]{2,1,0:T(8,128)(2,1)S(1)}, u32[]{:S(2)}, u32[]{:S(2)}) %collective-permute-start) | collective-permute-done | bytes 196640 | tf_op jit(solution)/shard_map/ppermute | solution.py:78
  58.7 3.1 %collective-permute-done.3 = bf16[2,192,256]{2,1,0:T(8,128)(2,1)S(1)} collective-permute-done((bf16[2,192,256]{2,1,0:T(8,128)(2,1)}, bf16[2,192,256]{2,1,0:T(8,128)(2,1)S(1)}, u32[]{:S(2)}, u32[]{:S(2)}) %collective-permute-start.3) | collective-permute-done | bytes 196640 | tf_op jit(solution)/shard_map/ppermute | solution.py:78
  61.9 0.9 reshape_squeeze.12
  65.2 2.5 %broadcast_select_fusion = bf16[2,16,128,256]{2,3,1,0:T(8,128)(2,1)S(1)} fusion(bf16[2,16,128,256]{2,3,1,0:T(8,128)(2,1)} %copy.173, pred[16,128]{1,0:T(8,128)(4,1)S(1)} %fusion.37, bf16[2,16,256]{2,1,0:T(8,128)(2,1)S(1)} %fusion.15), kind=kLoop, calls=%fused_computation.4 | loop fusion | flops 1048576 | bytes 4212736 | tf_op jit(solution)/shard_map/jit(_where)/select_n | solution.py:219
  70.7 9.1 %all-to-all-start.1 = ((f32[32,2,2,2,129]{4,1,3,2,0:T(2,128)}), f32[32,2,2,2,129]{4,1,3,2,0:T(2,128)S(1)}, u32[]{:S(2)}, u32[]{:S(2)}) async-start(f32[32,2,2,2,129]{4,1,3,2,0:T(2,128)} %copy.179), calls=%async_computation.1 | async-start | bytes 524288 | tf_op jit(solution)/shard_map/all_to_all | solution.py:243
  79.7 3.8 %fusion = (f32[192,2,2]{0,2,1:T(2,128)S(1)}, f32[2,960,192,2]{1,2,3,0:T(8,128)}) fusion(pred[192,960]{1,0:T(8,128)(4,1)} %compare_and_fusion, bf16[192,2,2,128]{3,2,1,0:T(2,128)(2,1)S(1)} %reshape.305, bf16[960,2,128,1]{2,1,0,3:T(2,128)(2,1)} %bitcast.82), kind=kOutput, calls=%fused_computation.2 | convolution fusion | flops 191692032 | bytes 3824640 | tf_op jit(solution)/shard_map/qhgd,khd->qhgk/dot_general | solution.py:83
  83.6 15.5 %all-to-all-done.1 = f32[32,2,2,2,129]{4,1,3,2,0:T(2,128)S(1)} async-done(((f32[32,2,2,2,129]{4,1,3,2,0:T(2,128)}), f32[32,2,2,2,129]{4,1,3,2,0:T(2,128)S(1)}, u32[]{:S(2)}, u32[]{:S(2)}) %all-to-all-start.1) | async-done | bytes 132128 | tf_op jit(solution)/shard_map/all_to_all | solution.py:243
  99.4 38.5 %all-gather.3.cloned.1.call-done = bf16[64,2,384,128]{3,2,1,0:T(8,128)(2,1)} async-done(((bf16[2,2,384,128]{3,2,1,0:T(8,128)(2,1)}), bf16[64,2,384,128]{3,2,1,0:T(8,128)(2,1)}) %all-gather.3.cloned.1.call-update) | async-done | bytes 12582928 | tf_op jit(solution)/shard_map/all_gather | solution.py:167
  137.9 21.9 %shard_map.166 = (f32[2,384,128]{2,1,0:T(8,128)}, f32[2,384,1]{2,1,0:T(8,128)}) custom-call(bf16[2,384,128]{2,1,0:T(8,128)(2,1)} %bitcast.80, bf16[32,2,2,384,128]{4,3,2,1,0:T(8,128)(2,1)} %bitcast.74, bf16[32,2,2,384,128]{4,3,2,1,0:T(8,128)(2,1)} %bitcast.75, s32[32,1,384]{2,1,0:T(1,128)} %broadcast_in_dim.64.own_ref, s32[384,1]{1,0:T(8,128)} %broadcast_in_dim_reshape.4.row_ref), custom_call_target="tpu_custom_call" | custom-call | tf_op jit(solution)/shard_map/pallas_call | solution.py:53
  159.8 1.2 reduce.2
  161.3 3.0 %fusion.19 = bf16[192,2,2,128]{3,0,2,1:T(8,128)(2,1)S(1)} fusion(f32[2,960,192,2]{1,2,3,0:T(8,128)} %get-tuple-element.41, pred[192,960]{1,0:T(8,128)(4,1)S(1)} %copy-done.5, bf16[960,2,128,1]{2,1,0,3:T(2,128)(2,1)S(1)} %bitcast.81, f32[2,192,2,128]{3,2,1,0:T(2,128)} %bitcast.88, f32[192,2,2]{0,2,1:T(2,128)S(1)} %bitcast_add_fusion), kind=kOutput, calls=%fused_computation.19 | convolution fusion | flops 191987712 | bytes 4217856 | tf_op jit(solution)/shard_map/qhgk,khd->qhgd/dot_general | solution.py:89
  164.6 3.9 %convert_bitcast_fusion = bf16[8,194,576]{2,1,0:T(8,128)(2,1)S(1)} fusion(bf16[512,8,576]{0,2,1:T(8,128)(2,1)} %bitcast.76, bf16[2,512]{1,0:T(2,128)(2,1)S(1)} %bitcast.85, bf16[192,512]{1,0:T(8,128)(2,1)S(1)} %reshape.310), kind=kOutput, calls=%fused_computation.5 | convolution fusion | flops 916698112 | bytes 6705152 | tf_op jit(solution)/shard_map/rk,kdo->dro/dot_general | solution.py:253
  168.5 30.8 %all_to_all.21 = bf16[8,194,576]{2,1,0:T(8,128)(2,1)S(1)} all-to-all(bf16[8,194,576]{2,1,0:T(8,128)(2,1)S(1)} %convert_bitcast_fusion), channel_id=1, replica_groups=mesh['kv'=8,'blk'=32] {'kv'}, dimensions={0} | all-to-all | bytes 3575808 | tf_op jit(solution)/shard_map/all_to_all | solution.py:256
  200.3 3.3 %all-to-all-start.3 = ((f32[8,1,194]{2,1,0:T(1,128)}), f32[8,1,194]{2,1,0:T(1,128)S(1)}, u32[]{:S(2)}, u32[]{:S(2)}) async-start(f32[8,1,194]{2,1,0:T(1,128)} %broadcast_in_dim.59), calls=%async_computation.3 | async-start | bytes 16384 | tf_op jit(solution)/shard_map/all_to_all | solution.py:258
  203.7 2.6 %copy.185 = bf16[2,16,128,256]{3,2,1,0:T(8,128)(2,1)} copy(bf16[2,16,128,256]{2,3,1,0:T(8,128)(2,1)S(1)} %broadcast_select_fusion) | data formatting | bytes 4194304
  206.3 3.5 %all-to-all-done.3 = f32[8,1,194]{2,1,0:T(1,128)S(1)} async-done(((f32[8,1,194]{2,1,0:T(1,128)}), f32[8,1,194]{2,1,0:T(1,128)S(1)}, u32[]{:S(2)}, u32[]{:S(2)}) %all-to-all-start.3) | async-done | bytes 6240 | tf_op jit(solution)/shard_map/all_to_all | solution.py:258
  (95 shorter events, 20.4 us)
Async XLA Ops:
  7.2 39.2 %copy-start.3 = (bf16[192,512]{1,0:T(8,128)(2,1)S(1)}, bf16[192,512]{1,0:T(8,128)(2,1)}, u32[]{:S(2)}) copy-start(bf16[192,512]{1,0:T(8,128)(2,1)} %param.15) | copy-start | bytes 589828
  7.2 40.1 %copy-start = (bf16[2,16,128,256]{3,2,1,0:T(8,128)(2,1)S(1)}, bf16[2,16,128,256]{3,2,1,0:T(8,128)(2,1)}, u32[]{:S(2)}) copy-start(bf16[2,16,128,256]{3,2,1,0:T(8,128)(2,1)} %param.25) | copy-start | bytes 6291460
  7.2 130.7 %all-gather.3.cloned.1.call-start = ((), (), s32[]{:S(2)}) async-start(), calls=%async_computation.4 | async-start | bytes 12976128 | tf_op jit(solution)/shard_map/all_gather | solution.py:167
  9.3 49.4 %collective-permute-start.2 = (bf16[2,192,256]{2,1,0:T(8,128)(2,1)}, bf16[2,192,256]{2,1,0:T(8,128)(2,1)S(1)}, u32[]{:S(2)}, u32[]{:S(2)}) collective-permute-start(bf16[2,192,256]{2,1,0:T(8,128)(2,1)} %param.16), channel_id=1, source_target_pairs={{0,2},{1,3},{2,4},{3,5},{4,6},{5,7},{6,8},{7,9},{8,10},{9,11},{10,... | collective-permute-start | bytes 589832 | tf_op jit(solution)/shard_map/ppermute | solution.py:78
  14.5 44.1 %collective-permute-start.1 = (bf16[2,192,256]{2,1,0:T(8,128)(2,1)}, bf16[2,192,256]{2,1,0:T(8,128)(2,1)S(1)}, u32[]{:S(2)}, u32[]{:S(2)}) collective-permute-start(bf16[2,192,256]{2,1,0:T(8,128)(2,1)} %param.16), channel_id=1, source_target_pairs={{0,3},{1,4},{2,5},{3,6},{4,7},{5,8},{6,9},{7,10},{8,11},{9,12},{10... | collective-permute-start | bytes 589832 | tf_op jit(solution)/shard_map/ppermute | solution.py:78
  20.0 38.6 %collective-permute-start = (bf16[2,192,256]{2,1,0:T(8,128)(2,1)}, bf16[2,192,256]{2,1,0:T(8,128)(2,1)S(1)}, u32[]{:S(2)}, u32[]{:S(2)}) collective-permute-start(bf16[2,192,256]{2,1,0:T(8,128)(2,1)} %param.16), channel_id=1, source_target_pairs={{0,4},{1,5},{2,6},{3,7},{4,8},{5,9},{6,10},{7,11},{8,12},{9,13},{1... | collective-permute-start | bytes 589832 | tf_op jit(solution)/shard_map/ppermute | solution.py:78
  23.7 38.0 %collective-permute-start.3 = (bf16[2,192,256]{2,1,0:T(8,128)(2,1)}, bf16[2,192,256]{2,1,0:T(8,128)(2,1)S(1)}, u32[]{:S(2)}, u32[]{:S(2)}) collective-permute-start(bf16[2,192,256]{2,1,0:T(8,128)(2,1)} %param.16), channel_id=1, source_target_pairs={{0,1},{1,2},{2,3},{3,4},{4,5},{5,6},{6,7},{7,8},{8,9},{9,10},{10,1... | collective-permute-start | bytes 589832 | tf_op jit(solution)/shard_map/ppermute | solution.py:78
  29.0 35.6 %all-to-all-start = ((bf16[32,8,256]{2,1,0:T(8,128)(2,1)}), bf16[32,8,256]{2,1,0:T(8,128)(2,1)S(1)}, u32[]{:S(2)}, u32[]{:S(2)}) async-start(bf16[32,8,256]{2,1,0:T(8,128)(2,1)} %broadcast_in_dim.54), calls=%async_computation | async-start | bytes 262144 | tf_op jit(solution)/shard_map/all_to_all | solution.py:154
  49.6 12.2 %copy-start.4 = (bf16[2,192,256]{2,1,0:T(8,128)(2,1)S(1)}, bf16[2,192,256]{2,1,0:T(8,128)(2,1)}, u32[]{:S(2)}) copy-start(bf16[2,192,256]{2,1,0:T(8,128)(2,1)} %param.16) | copy-start | bytes 589828
  70.7 28.4 %all-to-all-start.1 = ((f32[32,2,2,2,129]{4,1,3,2,0:T(2,128)}), f32[32,2,2,2,129]{4,1,3,2,0:T(2,128)S(1)}, u32[]{:S(2)}, u32[]{:S(2)}) async-start(f32[32,2,2,2,129]{4,1,3,2,0:T(2,128)} %copy.179), calls=%async_computation.1 | async-start | bytes 524288 | tf_op jit(solution)/shard_map/all_to_all | solution.py:243
  137.9 23.4 %copy-start.1 = (bf16[960,2,128]{2,1,0:T(2,128)(2,1)S(1)}, bf16[960,2,128]{2,1,0:T(2,128)(2,1)}, u32[]{:S(2)}) copy-start(bf16[960,2,128]{2,1,0:T(2,128)(2,1)} %reshape_squeeze.12) | copy-start | bytes 1474564
  137.9 23.4 %copy-start.5 = (pred[192,960]{1,0:T(8,128)(4,1)S(1)}, pred[192,960]{1,0:T(8,128)(4,1)}, u32[]{:S(2)}) copy-start(pred[192,960]{1,0:T(8,128)(4,1)} %compare_and_fusion) | copy-start | bytes 552964
  199.2 10.6 %copy-start.6 = (f32[576]{0:T(1024)S(1)}, f32[576]{0:T(1024)}, u32[]{:S(2)}) copy-start(f32[576]{0:T(1024)} %param.22) | copy-start | bytes 6916
  199.6 10.4 %copy-start.7 = (bf16[2,576]{1,0:T(2,128)(2,1)S(1)}, bf16[2,576]{1,0:T(2,128)(2,1)}, u32[]{:S(2)}) copy-start(bf16[2,576]{1,0:T(2,128)(2,1)} %param.20) | copy-start | bytes 6916
  199.6 11.0 %copy-start.2 = (bf16[192,576]{1,0:T(8,128)(2,1)S(1)}, bf16[192,576]{1,0:T(8,128)(2,1)}, u32[]{:S(2)}) copy-start(bf16[192,576]{1,0:T(8,128)(2,1)} %param.17) | copy-start | bytes 663556
  200.3 9.5 %all-to-all-start.3 = ((f32[8,1,194]{2,1,0:T(1,128)}), f32[8,1,194]{2,1,0:T(1,128)S(1)}, u32[]{:S(2)}, u32[]{:S(2)}) async-start(f32[8,1,194]{2,1,0:T(1,128)} %broadcast_in_dim.59), calls=%async_computation.3 | async-start | bytes 16384 | tf_op jit(solution)/shard_map/all_to_all | solution.py:258
Sparse Core Ops, SparseCore 0:
  10.5 127.3 all-gather.2
